TPU v7x, 256 devices: a whole 4x4x8 slice. The times are simulated.
256 devices in a mesh: ctx: 16 (over y_lo, x, core), ch: 16 (over z, y_hi).
Axes of the slice: x: 4, y: 4 (y_hi: 2, y_lo: 2; y = y_hi * 2 + y_lo), z: 8, core: 2. Of those that a mesh axis runs over, the one named last changes fastest.
Arguments:
- tokens: bfloat16 [6144, 4096], P('ctx', 'ch'), may hold values from -2.5 to 2.5
- mr_gain: float32 [4096], replicated, may hold values from 0.1 to 1.9
- mr_inproj: bfloat16 [4096, 3, 4096], P('ctx', None, 'ch'), may hold values from -0.09375 to 0.09375
- mr_outproj: bfloat16 [4096, 4096], P('ch', 'ctx'), may hold values from -0.09375 to 0.09375
- mr_filter: float32 [128, 4096], P(None, 'ch'), may hold values from -0.5 to 0.5
- li_gain: float32 [4096], replicated, may hold values from 0.1 to 1.9
- li_inproj: bfloat16 [4096, 3, 4096], P('ctx', None, 'ch'), may hold values from -0.09375 to 0.09375
- li_outproj: bfloat16 [4096, 4096], P('ch', 'ctx'), may hold values from -0.09375 to 0.09375
- li_decay: float32 [16, 4096], P(None, 'ch'), may hold values from 8.138021e-07 to 0.125
- li_residue: float32 [16, 4096], P(None, 'ch'), may hold values from -1 to 1
- doc_ids: int32 [6144], replicated, may hold values from 0 to 3, never falling along the last dimension, each value on 1 to 3072 neighbouring positions
Outputs:
- layer_out: bfloat16 [6144, 4096], P('ctx', 'ch')
Inputs may be any that keep to these rules, and one draw needn't show every extreme that they name: `doc_ids`: ids never fall along the sequence and every one of the 4 ids occurs.
All inputs are finite; a program needn't handle non-finite values.
Results may differ from a plain program's by a relative error of at most 0.03.
Values may be sent and summed in bfloat16 or wider, within the bound.
No kernel may reach another device: no remote copies, remote signals or barrier semaphores. Data moves between devices by JAX's collectives and lax.ppermute only.
A program may use at most 128 MiB of HBM per device.

v0:
```python
import math

import jax
import jax.numpy as jnp
from jax import lax
from jax.sharding import PartitionSpec as P


def extended(value, sides, width):
    for axis, dim in sides:
        count, length = (lax.axis_size(axis), value.shape[dim])
        up = [(i, (i + 1) % count) for i in range(count - 1)]
        down = [(j, i) for i, j in up]
        last = lax.slice_in_dim(value, length - width, length, axis=dim)
        initial = lax.slice_in_dim(value, 0, width, axis=dim)
        before = lax.ppermute(last, axis, up)
        after = lax.ppermute(initial, axis, down)
        value = jnp.concatenate([before, value, after], axis=dim)
    return value


def features_in(stream, gain, inproj):
    whole = lax.all_gather(stream, "ch", axis=1, tiled=True)
    floats = whole.astype(jnp.float32)
    scaled = lax.rsqrt(jnp.mean(floats * floats, axis=1, keepdims=True) + 1e-06)
    normed = (floats * scaled * gain[None, :]).astype(jnp.bfloat16)
    channels = inproj.shape[2]
    piece = lax.all_gather(inproj, "ctx", axis=0, tiled=True)
    flat = piece.reshape(piece.shape[0], 3 * channels)
    joined = jnp.dot(normed, flat, preferred_element_type=jnp.float32).astype(jnp.bfloat16)
    product = (
        joined[:, channels : 2 * channels].astype(jnp.float32)
        * joined[:, 2 * channels :].astype(jnp.float32)
    ).astype(jnp.bfloat16)
    return (joined[:, :channels], product)


def features_out(stream, query, mixed, outproj):
    gated = (query.astype(jnp.float32) * mixed).astype(jnp.bfloat16)
    terms = jnp.dot(
        gated,
        lax.all_gather(outproj, "ctx", axis=1, tiled=True),
        preferred_element_type=jnp.float32,
    )
    summed = lax.psum_scatter(
        terms.astype(jnp.bfloat16), "ch", scatter_dimension=1, tiled=True
    ).astype(jnp.float32)
    return (stream.astype(jnp.float32) + summed).astype(jnp.bfloat16)


def span_layout(shard_rows):
    ctx_count = lax.axis_size("ctx")
    ctx_index = lax.axis_index("ctx")
    span_rows = shard_rows // 2
    span_starts = jnp.stack([ctx_index * span_rows, (2 * ctx_count - 1 - ctx_index) * span_rows])
    positions = span_starts[:, None] + jnp.arange(span_rows)[None, :]
    return (ctx_count, ctx_index, span_rows, span_starts, positions)


def short_mix(product, mr_filter, doc_ids):
    shard_rows, channels = product.shape
    ctx_count, ctx_index, span_rows, span_starts, positions = span_layout(shard_rows)
    tap_count = mr_filter.shape[0]
    reach_rows = tap_count - 1
    halves = product.reshape(2, span_rows, channels)
    tails = jnp.concatenate(
        [halves[1, span_rows - reach_rows :], halves[0, span_rows - reach_rows :]], 0
    )
    framed = extended(tails, (("ctx", 0),), reach_rows)
    before_upper = jnp.where(
        ctx_index == ctx_count - 1, halves[0, span_rows - reach_rows :], framed[3 * reach_rows :]
    )
    lower_window = jnp.concatenate([framed[:reach_rows], halves[0]], 0)
    upper_window = jnp.concatenate([before_upper, halves[1]], 0)
    windows = jnp.stack([lower_window, upper_window]).astype(jnp.float32)
    window_places = span_starts[:, None] - reach_rows + jnp.arange(reach_rows + span_rows)[None, :]
    window_docs = jnp.where(
        window_places >= 0, jnp.take(doc_ids, jnp.clip(window_places, 0, None)), -1
    )
    target_docs = window_docs[:, reach_rows:]
    tap_block = math.gcd(tap_count, 16)

    def tap_group(group_number, running):
        for offset in range(tap_block):
            tap_lag = group_number * tap_block + offset
            source = lax.dynamic_slice_in_dim(windows, reach_rows - tap_lag, span_rows, 1)
            source_docs = lax.dynamic_slice_in_dim(window_docs, reach_rows - tap_lag, span_rows, 1)
            weight = lax.dynamic_slice_in_dim(mr_filter, tap_lag, 1, 0)
            running = (
                running
                + jnp.where((source_docs == target_docs)[:, :, None], source, 0.0) * weight[None]
            )
        return running

    mixed = lax.fori_loop(
        0, tap_count // tap_block, tap_group, jnp.zeros((2, span_rows, channels), jnp.float32)
    )
    return mixed.reshape(shard_rows, channels)


def combine_pairs(early, late):
    return (early[0] * late[0], late[0] * early[1] + late[1])


def long_mix(product, li_decay, li_residue, doc_ids):
    shard_rows, channels = product.shape
    ctx_count, ctx_index, span_rows, span_starts, positions = span_layout(shard_rows)
    modes = li_decay.shape[0]
    own_docs = jnp.take(doc_ids, positions)
    follows = jnp.concatenate([jnp.zeros((2, 1), bool), own_docs[:, 1:] == own_docs[:, :-1]], 1)
    factor = jnp.exp(-li_decay)
    values = product.reshape(2, span_rows, channels).astype(jnp.float32)
    carried = jnp.where(follows[:, :, None, None], factor[None, None], 0.0)
    inputs = jnp.broadcast_to(values[:, :, None, :], carried.shape)
    _, states = lax.associative_scan(combine_pairs, (carried, inputs), axis=1)
    head_docs = own_docs[:, 0]
    empty = jnp.zeros((2, modes, channels), jnp.float32)
    piece = lax.all_gather(product, "ctx", axis=0, tiled=True)
    step_rows = math.gcd(piece.shape[0], span_rows)

    def one_block(number, inner):
        begin = number * step_rows
        part_rows = lax.dynamic_slice_in_dim(piece, begin, step_rows, 0).astype(jnp.float32)
        stored = begin + jnp.arange(step_rows)
        owner = stored // shard_rows
        local_row = stored % shard_rows
        seq_block = jnp.where(local_row < span_rows, owner, 2 * ctx_count - 1 - owner)
        source_places = seq_block * span_rows + local_row % span_rows
        source_docs = jnp.take(doc_ids, source_places)
        updated = []
        for half in range(2):
            keep = (source_places < span_starts[half]) & (source_docs == head_docs[half])
            distance = jnp.where(keep, span_starts[half] - source_places, 0).astype(jnp.float32)
            weights = (
                jnp.exp(-li_decay[:, :, None] * distance[None, None, :])
                * keep.astype(jnp.float32)[None, None, :]
            )
            updated.append(inner[half] + jnp.einsum("mcs,sc->mc", weights, part_rows))
        return jnp.stack(updated)

    incoming = lax.fori_loop(0, piece.shape[0] // step_rows, one_block, empty)
    entry_mask = (own_docs == head_docs[:, None]).astype(jnp.float32)
    elapsed = jnp.arange(span_rows).astype(jnp.float32)
    arriving = (
        jnp.exp(-li_decay[None, None] * elapsed[None, :, None, None])
        * incoming[:, None]
        * entry_mask[:, :, None, None]
    )
    mixed = jnp.einsum("gtmc,mc->gtc", states + arriving, li_residue)
    return mixed.reshape(shard_rows, channels)


def body(
    tokens,
    mr_gain,
    mr_inproj,
    mr_outproj,
    mr_filter,
    li_gain,
    li_inproj,
    li_outproj,
    li_decay,
    li_residue,
    doc_ids,
):
    query, product = features_in(tokens, mr_gain, mr_inproj)
    stream = features_out(tokens, query, short_mix(product, mr_filter, doc_ids), mr_outproj)
    query, product = features_in(stream, li_gain, li_inproj)
    return features_out(stream, query, long_mix(product, li_decay, li_residue, doc_ids), li_outproj)


def solution(mesh):
    in_specs = (
        P("ctx", "ch"),
        P(),
        P("ctx", None, "ch"),
        P("ch", "ctx"),
        P(None, "ch"),
        P(),
        P("ctx", None, "ch"),
        P("ch", "ctx"),
        P(None, "ch"),
        P(None, "ch"),
        P(),
    )
    out_specs = P("ctx", "ch")
    return jax.shard_map(body, mesh=mesh, in_specs=in_specs, out_specs=out_specs, check_vma=False)
```

profile of v0, /device:TPU:4, one launch (start us, length us, event | category | flops | bytes accessed | tf_op | source)
XLA Modules:
  0.0 1398.8 jit_solution(12417820259638597614)
XLA Ops:
  10.3 3.9 gather_fusion.1
  14.4 93.0 %all-gather.8.cloned.1.call-done = bf16[384,4096]{1,0:T(8,128)(2,1)} async-done(((bf16[384,256]{1,0:T(8,128)(2,1)}), bf16[384,4096]{1,0:T(8,128)(2,1)}) %all-gather.8.cloned.1.call-update) | async-done | bytes 3145744 | tf_op jit(solution)/shard_map/all_gather | solution.py:23
  110.0 50.2 %all-gather.10.cloned.1.call-done = bf16[4096,3,256]{0,2,1:T(8,128)(2,1)} async-done(((bf16[256,3,256]{0,2,1:T(8,128)(2,1)}), bf16[4096,3,256]{0,2,1:T(8,128)(2,1)}) %all-gather.10.cloned.1.call-update) | async-done | bytes 6291472 | tf_op jit(solution)/shard_map/all_gather | solution.py:28
  160.2 6.4 fusion.52
  166.7 3.6 collective-permute-start.1
  172.3 3.6 collective-permute-done
  176.0 29.5 %while.34 = (s32[]{:T(128)}, f32[2,192,256]{2,1,0:T(8,128)S(1)}, s32[2,319]{1,0:T(2,128)S(1)}, s32[2,192]{1,0:T(2,128)S(1)}, f32[2,319,256]{2,1,0:T(8,128)S(1)},...) while((s32[]{:T(128)}, f32[2,192,256]{2,1,0:T(8,128)S(1)}, ...), condition=%wide.region_2.3_spmd.clone, body=%wide.region_1.2_spmd.clone.sunk | while | flops 4823171 | bytes 7167471 | solution.py:95
  205.6 4.2 convolution_convert_fusion.1
  209.9 213.3 %reduce-scatter.3.cloned.1.call-done = bf16[384,256]{1,0:T(8,128)(2,1)} async-done(((bf16[384,4096]{1,0:T(8,128)(2,1)}), bf16[384,256]{1,0:T(8,128)(2,1)}) %reduce-scatter.3.cloned.1.call-update) | async-done | bytes 196624 | tf_op jit(solution)/shard_map/reduce_scatter | solution.py:45
  425.9 92.3 %all-gather.14.cloned.1.call-done = bf16[384,4096]{1,0:T(8,128)(2,1)} async-done(((bf16[384,256]{1,0:T(8,128)(2,1)}), bf16[384,4096]{1,0:T(8,128)(2,1)}) %all-gather.14.cloned.1.call-update) | async-done | bytes 3145744 | tf_op jit(solution)/shard_map/all_gather | solution.py:23
  520.8 50.0 %all-gather.16.cloned.1.call-done = bf16[4096,3,256]{0,2,1:T(8,128)(2,1)} async-done(((bf16[256,3,256]{0,2,1:T(8,128)(2,1)}), bf16[4096,3,256]{0,2,1:T(8,128)(2,1)}) %all-gather.16.cloned.1.call-update) | async-done | bytes 6291472 | tf_op jit(solution)/shard_map/all_gather | solution.py:28
  570.8 6.4 fusion.55
  584.5 2.9 broadcast_select_fusion
  587.6 4.3 slice_multiply_fusion
  602.4 4.0 pad.47
  612.8 4.4 pad.49
  619.8 8.7 pad.51
  629.5 8.1 pad.50
  641.1 23.0 %pad.53 = f32[2,48,16,256]{3,2,1,0:T(8,128)} pad(f32[2,24,16,256]{3,2,1,0:T(8,128)} %add.1536, f32[]{:T(128)} %constant.448.clone.1), padding=0_0_0x1_0_1x0_0_0x0_0_0 | pad | bytes 2359300 | tf_op jit(solution)/shard_map/pad | solution.py:115
  664.1 3.1 add.1538
  667.2 3.2 fusion.51
  670.6 44.6 %pad.55 = f32[2,96,16,256]{3,2,1,0:T(8,128)} pad(f32[2,48,16,256]{3,2,1,0:T(8,128)} %add.1538, f32[]{:T(128)} %constant.448.clone.1), padding=0_0_0x1_0_1x0_0_0x0_0_0 | pad | bytes 4718596 | tf_op jit(solution)/shard_map/pad | solution.py:115
  716.6 30.5 %pad.54 = f32[2,96,16,256]{3,2,1,0:T(8,128)} pad(f32[2,48,16,256]{3,2,1,0:T(8,128)S(1)} %pad_maximum_fusion.2, f32[]{:T(128)} %constant.448.clone.1), padding=0_0_0x0_1_1x0_0_0x0_0_0 | pad | bytes 4718596 | tf_op jit(solution)/shard_map/pad | solution.py:115
  747.2 5.5 add.1540
  757.5 87.6 %pad.56 = f32[2,192,16,256]{3,2,1,0:T(8,128)} pad(f32[2,96,16,256]{3,2,1,0:T(8,128)} %pad_maximum_fusion.1, f32[]{:T(128)} %constant.448.clone.1), padding=0_0_0x0_1_1x0_0_0x0_0_0 | pad | bytes 9437188 | tf_op jit(solution)/shard_map/pad | solution.py:115
  845.1 87.6 %pad.57 = f32[2,192,16,256]{3,2,1,0:T(8,128)} pad(f32[2,96,16,256]{3,2,1,0:T(8,128)} %add.1540, f32[]{:T(128)} %constant.448.clone.1), padding=0_0_0x1_0_1x0_0_0x0_0_0 | pad | bytes 9437188 | tf_op jit(solution)/shard_map/pad | solution.py:115
  932.7 233.4 %while.33 = (s32[]{:T(128)}, f32[2,16,256]{2,1,0:T(8,128)S(1)}, bf16[6144,256]{1,0:T(8,128)(2,1)}, f32[16,256,1]{1,2,0:T(1,128)S(1)}, s32[]{:T(128)}, /*index=5*...) while((s32[]{:T(128)}, f32[2,16,256]{2,1,0:T(8,128)S(1)}, ...), condition=%wide.region_6.7_spmd, body=%wide.region_5.6_spmd.sunk | while | flops 6363654 | bytes 1146327 | solution.py:141
  937.1 2.9 multiply_reduce_fusion.4
  944.4 2.9 multiply_reduce_fusion.4
  959.0 2.9 multiply_reduce_fusion.4
  966.3 2.9 multiply_reduce_fusion.4
  973.5 2.9 multiply_reduce_fusion.4
  980.8 2.9 multiply_reduce_fusion.4
  995.4 2.9 multiply_reduce_fusion.4
  1002.7 2.9 multiply_reduce_fusion.4
  1010.0 2.9 multiply_reduce_fusion.4
  1017.3 2.9 multiply_reduce_fusion.4
  1024.6 2.9 multiply_reduce_fusion.4
  1031.9 2.9 multiply_reduce_fusion.4
  1046.5 2.9 multiply_reduce_fusion.4
  1053.8 2.9 multiply_reduce_fusion.4
  1061.1 2.9 multiply_reduce_fusion.4
  1068.3 2.9 multiply_reduce_fusion.4
  1075.6 2.9 multiply_reduce_fusion.4
  1082.9 2.9 multiply_reduce_fusion.4
  1166.1 6.7 multiply_reduce_fusion.2
  1173.8 4.2 convolution_convert_fusion
  1178.1 212.5 %reduce-scatter.5.cloned.1.call-done = bf16[384,256]{1,0:T(8,128)(2,1)} async-done(((bf16[384,4096]{1,0:T(8,128)(2,1)}), bf16[384,256]{1,0:T(8,128)(2,1)}) %reduce-scatter.5.cloned.1.call-update) | async-done | bytes 196624 | tf_op jit(solution)/shard_map/reduce_scatter | solution.py:45
  (565 shorter events, 260.9 us)
Async XLA Ops:
  6.5 3.8 copy-start
  6.5 100.9 %all-gather.8.cloned.1.call-start = ((), (), s32[]{:S(2)}) async-start(), calls=%async_computation.2 | async-start | bytes 3342336 | tf_op jit(solution)/shard_map/all_gather | solution.py:23
  7.3 152.9 %all-gather.10.cloned.1.call-start = ((), (), s32[]{:S(2)}) async-start(), calls=%async_computation.3 | async-start | bytes 6684672 | tf_op jit(solution)/shard_map/all_gather | solution.py:28
  9.3 196.3 %all-gather.12.cloned.1.call-start = ((), (), s32[]{:S(2)}) async-start(), calls=%async_computation.4 | async-start | bytes 2228224 | tf_op jit(solution)/shard_map/all_gather | solution.py:42
  10.0 413.2 %reduce-scatter.3.cloned.1.call-start = ((), (), s32[]{:S(2)}) async-start(), calls=%async_computation.5 | async-start | bytes 3342336 | tf_op jit(solution)/shard_map/reduce_scatter | solution.py:45
  10.3 149.8 %copy-start.19 = (f32[4096]{0:T(1024)S(1)}, f32[4096]{0:T(1024)}, u32[]{:S(2)}) copy-start(f32[4096]{0:T(1024)} %param.16) | copy-start | bytes 49156
  166.7 5.6 collective-permute-start.1
  170.3 5.6 collective-permute-start
  209.8 213.3 %copy-start.14 = (bf16[384,256]{1,0:T(8,128)(2,1)S(1)}, bf16[384,256]{1,0:T(8,128)(2,1)}, u32[]{:S(2)}) copy-start(bf16[384,256]{1,0:T(8,128)(2,1)} %param.15) | copy-start | bytes 589828
  209.8 215.1 %copy-start.16 = (bf16[256,3,256]{2,0,1:T(8,128)(2,1)S(1)}, bf16[256,3,256]{2,0,1:T(8,128)(2,1)}, u32[]{:S(2)}) copy-start(bf16[256,3,256]{2,0,1:T(8,128)(2,1)} %param.21) | copy-start | bytes 1179652
  209.8 360.9 %copy-start.20 = (f32[4096]{0:T(1024)S(1)}, f32[4096]{0:T(1024)}, u32[]{:S(2)}) copy-start(f32[4096]{0:T(1024)} %param.20) | copy-start | bytes 49156
  209.9 308.3 %all-gather.14.cloned.1.call-start = ((), (), s32[]{:S(2)}) async-start(), calls=%async_computation.6 | async-start | bytes 3342336 | tf_op jit(solution)/shard_map/all_gather | solution.py:23
  424.8 145.9 %all-gather.16.cloned.1.call-start = ((), (), s32[]{:S(2)}) async-start(), calls=%async_computation.7 | async-start | bytes 6684672 | tf_op jit(solution)/shard_map/all_gather | solution.py:28
  425.8 506.9 %all-gather.18.cloned.1.call-start = ((), (), s32[]{:S(2)}) async-start(), calls=%async_computation.8 | async-start | bytes 3342336 | tf_op jit(solution)/shard_map/all_gather | solution.py:118
  570.8 11.3 copy-start.18
  577.2 7.2 copy-start.15
  578.1 595.7 %all-gather.20.cloned.1.call-start = ((), (), s32[]{:S(2)}) async-start(), calls=%async_computation.9 | async-start | bytes 2228224 | tf_op jit(solution)/shard_map/all_gather | solution.py:42
  578.8 811.8 %reduce-scatter.5.cloned.1.call-start = ((), (), s32[]{:S(2)}) async-start(), calls=%async_computation.10 | async-start | bytes 3342336 | tf_op jit(solution)/shard_map/reduce_scatter | solution.py:45
  584.5 3.0 copy-start.9
  591.9 1.7 copy-start.3
  591.9 2.6 copy-start.5
  594.5 1.2 copy-start.7
  594.9 1.1 copy-start.10
  596.0 0.7 copy-start.12
  596.0 0.7 copy-start.13
  637.6 1.8 copy-start.8
  664.1 3.1 copy-start.4
  664.1 3.1 copy-start.6
  747.2 5.5 copy-start.1
  747.2 5.5 copy-start.2
  932.7 233.4 %copy-start.17 = (f32[16,256]{1,0:T(8,128)S(1)}, f32[16,256]{1,0:T(8,128)}, u32[]{:S(2)}) copy-start(f32[16,256]{1,0:T(8,128)} %param.24) | copy-start | bytes 49156
  1178.0 212.6 %copy-start.11 = (bf16[384,256]{1,0:T(8,128)(2,1)S(1)}, bf16[384,256]{1,0:T(8,128)(2,1)}, u32[]{:S(2)}) copy-start(bf16[384,256]{1,0:T(8,128)(2,1)} %add_convert_fusion.1) | copy-start | bytes 589828
Sparse Core Ops, SparseCore 0:
  9.8 97.5 all-gather.7
  109.2 50.9 all-gather.9
  161.9 39.7 all-gather.11
  210.0 213.1 reduce-scatter.2
  425.5 92.6 all-gather.13
  519.8 50.9 all-gather.15
  578.2 38.0 all-gather.17
  618.1 39.6 all-gather.19
  1178.2 212.3 reduce-scatter.4
where the time goes:
time: 1430 us; the launch traced here: 1400 us
  waiting for transfers between devices  717 us (50%)
  local copies, waits for them, and re-layouts  395 us (28%)
  other arithmetic  241 us (17%)
  matrix products  21.3 us (1%)
    reduce_scatter x2, waiting for transfers between devices, features_out(): lax.psum_scatter(terms.astype(jnp.bfloat16), 'ch', scatter_dimension=1, t...  426 us
    pad x13, local copies, waits for them, and re-layouts, long_mix(): _, states = lax.associative_scan(combine_pairs, (carried, inputs), axis=1)  303 us
    all_gather x2, waiting for transfers between devices, features_in(): whole = lax.all_gather(stream, 'ch', axis=1, tiled=True)  185 us
    all_gather x2, waiting for transfers between devices, features_in(): piece = lax.all_gather(inproj, 'ctx', axis=0, tiled=True)  100 us
    dot_general x32, other arithmetic, one_block(): updated.append(inner[half] + jnp.einsum('mcs,sc->mc', weights, part_rows))  92.3 us
    gather x32, local copies, waits for them, and re-layouts, one_block(): source_docs = jnp.take(doc_ids, source_places)  46.1 us
    convert_element_type x32, other arithmetic, one_block(): jnp.where(keep, span_starts[half] - source_places, 0).astype(jnp.float32)  38.9 us
    while x32, other arithmetic  29.2 us
  transfers between devices with their start and end apart: 11, of which 7 were waited for; matrix products, arithmetic and copies ran while one was open for 45% of the time, Pallas kernels for 0%

commit v1 on v0

--- a/solution.py
+++ b/solution.py
@@ -3,6 +3,8 @@
 import jax
 import jax.numpy as jnp
 from jax import lax
+from jax.experimental import pallas as pl
+from jax.experimental.pallas import tpu as pltpu
 from jax.sharding import PartitionSpec as P
 
 
@@ -35,16 +37,26 @@
     return (joined[:, :channels], product)
 
 
-def features_out(stream, query, mixed, outproj):
+def outproj_columns(outproj):
+    ctx_count, ch_count = (lax.axis_size("ctx"), lax.axis_size("ch"))
+    assert ctx_count == ch_count
+    pairs = [(i * ch_count + c, c * ch_count + i) for i in range(ctx_count) for c in range(ch_count)]
+    swapped = lax.ppermute(outproj, ("ctx", "ch"), pairs)
+    return lax.all_gather(swapped, "ctx", axis=0, tiled=True)
+
+
+def features_out(stream, query, mixed, columns):
     gated = (query.astype(jnp.float32) * mixed).astype(jnp.bfloat16)
-    terms = jnp.dot(
-        gated,
-        lax.all_gather(outproj, "ctx", axis=1, tiled=True),
+    whole = lax.all_gather(gated, "ch", axis=1, tiled=True)
+    rows, width = gated.shape
+    groups = whole.shape[1] // width
+    parts = jnp.einsum(
+        "tgk,gkj->gtj",
+        whole.reshape(rows, groups, width),
+        columns.reshape(groups, width, columns.shape[1]),
         preferred_element_type=jnp.float32,
-    )
-    summed = lax.psum_scatter(
-        terms.astype(jnp.bfloat16), "ch", scatter_dimension=1, tiled=True
-    ).astype(jnp.float32)
+    ).astype(jnp.bfloat16)
+    summed = jnp.sum(parts.astype(jnp.float32), axis=0)
     return (stream.astype(jnp.float32) + summed).astype(jnp.bfloat16)
 
 
@@ -98,8 +110,38 @@
     return mixed.reshape(shard_rows, channels)
 
 
-def combine_pairs(early, late):
-    return (early[0] * late[0], late[0] * early[1] + late[1])
+def scan_kernel(flags_ref, x_ref, factor_ref, init_ref, residue_ref, mixed_ref, end_ref):
+    halves, span_rows, _ = x_ref.shape
+    factor = factor_ref[...]
+    residue = residue_ref[...]
+    for half in range(halves):
+
+        def step(t, state):
+            kept = factor * flags_ref[half * span_rows + t]
+            state = kept * state + x_ref[half, pl.ds(t, 1), :]
+            mixed_ref[half, pl.ds(t, 1), :] = jnp.sum(residue * state, axis=0, keepdims=True)
+            return state
+
+        end_ref[half] = lax.fori_loop(0, span_rows, step, init_ref[half], unroll=8)
+
+
+def run_scan(flags, values, factor, init, residue):
+    halves, span_rows, channels = values.shape
+    modes = factor.shape[0]
+    vmem = pl.BlockSpec(memory_space=pltpu.VMEM)
+    steps = halves * span_rows * modes * channels
+    return pl.pallas_call(
+        scan_kernel,
+        out_shape=(
+            jax.ShapeDtypeStruct((halves, span_rows, channels), jnp.float32),
+            jax.ShapeDtypeStruct((halves, modes, channels), jnp.float32),
+        ),
+        in_specs=[pl.BlockSpec(memory_space=pltpu.SMEM), vmem, vmem, vmem, vmem],
+        out_specs=(vmem, vmem),
+        cost_estimate=pl.CostEstimate(
+            flops=5 * steps, transcendentals=0, bytes_accessed=8 * halves * span_rows * channels
+        ),
+    )(flags, values, factor, init, residue)
 
 
 def long_mix(product, li_decay, li_residue, doc_ids):
@@ -107,46 +149,24 @@
     ctx_count, ctx_index, span_rows, span_starts, positions = span_layout(shard_rows)
     modes = li_decay.shape[0]
     own_docs = jnp.take(doc_ids, positions)
-    follows = jnp.concatenate([jnp.zeros((2, 1), bool), own_docs[:, 1:] == own_docs[:, :-1]], 1)
+    prior_docs = jnp.take(doc_ids, jnp.clip(positions - 1, 0, None))
+    flags = ((positions > 0) & (own_docs == prior_docs)).astype(jnp.float32).reshape(-1)
     factor = jnp.exp(-li_decay)
     values = product.reshape(2, span_rows, channels).astype(jnp.float32)
-    carried = jnp.where(follows[:, :, None, None], factor[None, None], 0.0)
-    inputs = jnp.broadcast_to(values[:, :, None, :], carried.shape)
-    _, states = lax.associative_scan(combine_pairs, (carried, inputs), axis=1)
-    head_docs = own_docs[:, 0]
-    empty = jnp.zeros((2, modes, channels), jnp.float32)
-    piece = lax.all_gather(product, "ctx", axis=0, tiled=True)
-    step_rows = math.gcd(piece.shape[0], span_rows)
-
-    def one_block(number, inner):
-        begin = number * step_rows
-        part_rows = lax.dynamic_slice_in_dim(piece, begin, step_rows, 0).astype(jnp.float32)
-        stored = begin + jnp.arange(step_rows)
-        owner = stored // shard_rows
-        local_row = stored % shard_rows
-        seq_block = jnp.where(local_row < span_rows, owner, 2 * ctx_count - 1 - owner)
-        source_places = seq_block * span_rows + local_row % span_rows
-        source_docs = jnp.take(doc_ids, source_places)
-        updated = []
-        for half in range(2):
-            keep = (source_places < span_starts[half]) & (source_docs == head_docs[half])
-            distance = jnp.where(keep, span_starts[half] - source_places, 0).astype(jnp.float32)
-            weights = (
-                jnp.exp(-li_decay[:, :, None] * distance[None, None, :])
-                * keep.astype(jnp.float32)[None, None, :]
-            )
-            updated.append(inner[half] + jnp.einsum("mcs,sc->mc", weights, part_rows))
-        return jnp.stack(updated)
-
-    incoming = lax.fori_loop(0, piece.shape[0] // step_rows, one_block, empty)
-    entry_mask = (own_docs == head_docs[:, None]).astype(jnp.float32)
-    elapsed = jnp.arange(span_rows).astype(jnp.float32)
-    arriving = (
-        jnp.exp(-li_decay[None, None] * elapsed[None, :, None, None])
-        * incoming[:, None]
-        * entry_mask[:, :, None, None]
-    )
-    mixed = jnp.einsum("gtmc,mc->gtc", states + arriving, li_residue)
+    zeros = jnp.zeros((2, modes, channels), jnp.float32)
+    _, ends = run_scan(flags, values, factor, zeros, li_residue)
+    gathered = lax.all_gather(ends, "ctx", axis=0, tiled=False)
+    block_ends = jnp.concatenate([gathered[:, 0], gathered[::-1, 1]], 0)
+    block_count = 2 * ctx_count
+    blocks = jnp.arange(block_count)
+    end_docs = jnp.take(doc_ids, (blocks + 1) * span_rows - 1)
+    targets = span_starts // span_rows
+    entry_docs = jnp.take(doc_ids, jnp.clip(span_starts - 1, 0, None))
+    linked = (blocks[None, :] < targets[:, None]) & (end_docs[None, :] == entry_docs[:, None])
+    distance = jnp.where(linked, (targets[:, None] - blocks[None, :] - 1) * span_rows, 0).astype(jnp.float32)
+    weights = jnp.exp(-li_decay[None, None] * distance[:, :, None, None]) * linked.astype(jnp.float32)[:, :, None, None]
+    entry = jnp.sum(weights * block_ends[None], axis=1)
+    mixed, _ = run_scan(flags, values, factor, entry, li_residue)
     return mixed.reshape(shard_rows, channels)
 
 
@@ -163,10 +183,12 @@
     li_residue,
     doc_ids,
 ):
+    mr_columns = outproj_columns(mr_outproj)
+    li_columns = outproj_columns(li_outproj)
     query, product = features_in(tokens, mr_gain, mr_inproj)
-    stream = features_out(tokens, query, short_mix(product, mr_filter, doc_ids), mr_outproj)
+    stream = features_out(tokens, query, short_mix(product, mr_filter, doc_ids), mr_columns)
     query, product = features_in(stream, li_gain, li_inproj)
-    return features_out(stream, query, long_mix(product, li_decay, li_residue, doc_ids), li_outproj)
+    return features_out(stream, query, long_mix(product, li_decay, li_residue, doc_ids), li_columns)
 
 
 def solution(mesh):

time: 1430 us -> 606 us (0.42); the launches traced: 1400 us -> 605 us
  local copies, waits for them, and re-layouts: 395 us -> 24.9 us
  waiting for transfers between devices: 717 us -> 473 us
  other arithmetic: 241 us -> 31.9 us
  blocking collectives: 0 us -> 17.6 us
    reduce_scatter x2 -> x0, waiting for transfers between devices: 426 us -> none  [features_out(): lax.psum_scatter(terms.astype(jnp.bfloat16), 'ch', scatter_dimension=1, t...]
    pad x13 -> x0, local copies, waits for them, and re-layouts: 303 us -> none  [long_mix(): _, states = lax.associative_scan(combine_pairs, (carried, inputs), axis=1)]
    all_gather x3 -> x4, waiting for transfers between devices: 0.04 us -> 198 us  [the longest x2 195 us: features_out(): whole = lax.all_gather(gated, 'ch', axis=1, tiled=True)]
    dot_general x33 -> x0, other arithmetic: 99 us -> none  [the longest x32 92.3 us: one_block(): updated.append(inner[half] + jnp.einsum('mcs,sc->mc', weights, part_rows))]
    gather x32 -> x4, local copies, waits for them, and re-layouts: 46.1 us -> 3.94 us  [the longest x2 2.61 us: long_mix(): prior_docs = jnp.take(doc_ids, jnp.clip(positions - 1, 0, None))]
    convert_element_type x98 -> x3, other arithmetic: 39.3 us -> 0.92 us  [the longest x1 0.77 us: long_mix(): values = product.reshape(2, span_rows, channels).astype(jnp.float32)]
    while x32 -> x0, other arithmetic: 29.2 us -> none
    all_gather x2, waiting for transfers between devices: 185 us -> 157 us  [features_in(): whole = lax.all_gather(stream, 'ch', axis=1, tiled=True)]
  transfers between devices with their start and end apart: 11 -> 12, of which waited for: 7 -> 10; matrix products, arithmetic and copies ran while one was open for 45% -> 11% of each run, Pallas kernels for 0% -> 1%
where the time goes in v1:
time: 606 us; the launch traced here: 605 us
  waiting for transfers between devices  473 us (78%)
  other arithmetic  31.9 us (5%)
  local copies, waits for them, and re-layouts  24.9 us (4%)
  matrix products  20 us (3%)
  blocking collectives  17.6 us (3%)
  between operations  13.8 us (2%)
  starting transfers between devices  13.6 us (2%)
  Pallas kernels  8.29 us (1%)
    all_gather x2, waiting for transfers between devices, features_out(): whole = lax.all_gather(gated, 'ch', axis=1, tiled=True)  195 us
    all_gather x2, waiting for transfers between devices, features_in(): whole = lax.all_gather(stream, 'ch', axis=1, tiled=True)  157 us
    all_gather x2, waiting for transfers between devices, features_in(): piece = lax.all_gather(inproj, 'ctx', axis=0, tiled=True)  100 us
    add x8, other arithmetic, tap_group(): running + jnp.where((source_docs == target_docs)[:, :, None], source, 0.0...  18.1 us
    all_gather x1, blocking collectives, long_mix(): gathered = lax.all_gather(ends, 'ctx', axis=0, tiled=False)  17.6 us
    ppermute x2, waiting for transfers between devices, outproj_columns(): swapped = lax.ppermute(outproj, ('ctx', 'ch'), pairs)  13.2 us
    dot_general x2, matrix products, features_in(): jnp.dot(normed, flat, preferred_element_type=jnp.float32)  12.8 us
  transfers between devices with their start and end apart: 12, of which 10 were waited for; matrix products, arithmetic and copies ran while one was open for 11% of the time, Pallas kernels for 1%

profile of v1, /device:TPU:4, one launch (start us, length us, event | category | flops | bytes accessed | tf_op | source)
XLA Modules:
  0.0 604.7 jit_solution(2828579262374152721)
XLA Ops:
  7.3 1.9 copy.25
  9.3 5.1 collective-permute-start.2
  15.4 3.9 gather_fusion
  19.5 3.9 collective-permute-done.2
  24.2 85.2 %all-gather.10.cloned.1.call-done = bf16[384,4096]{1,0:T(8,128)(2,1)} async-done(((bf16[384,256]{1,0:T(8,128)(2,1)}), bf16[384,4096]{1,0:T(8,128)(2,1)}) %all-gather.10.cloned.1.call-update) | async-done | bytes 3145744 | tf_op jit(solution)/shard_map/all_gather | solution.py:25
  109.4 2.6 fusion.31
  111.9 50.2 %all-gather.12.cloned.1.call-done = bf16[4096,3,256]{0,2,1:T(8,128)(2,1)} async-done(((bf16[256,3,256]{0,2,1:T(8,128)(2,1)}), bf16[4096,3,256]{0,2,1:T(8,128)(2,1)}) %all-gather.12.cloned.1.call-update) | async-done | bytes 6291472 | tf_op jit(solution)/shard_map/all_gather | solution.py:30
  162.1 6.4 %fusion.55 = bf16[384,768]{1,0:T(8,128)(2,1)S(1)} fusion(bf16[4096,768]{0,1:T(8,128)(2,1)} %bitcast.126, bf16[384,4096]{1,0:T(8,128)(2,1)} %all-gather.10.cloned.1.call-done, f32[4096]{0:T(1024)S(1)} %copy-done.8, f32[384]{0:T(512)S(1)} %add_rsqrt_fusion.1), kind=kOutput, calls=%fused_computation.93 | convolution fusion | flops 2422505472 | bytes 10044928 | tf_op jit(solution)/shard_map/dot_general | solution.py:32
  168.6 3.6 collective-permute-start.1
  172.2 1.9 collective-permute-start
  174.2 3.6 collective-permute-done
  177.9 30.4 %while.17 = (s32[]{:T(128)}, f32[2,192,256]{2,1,0:T(8,128)S(1)}, s32[2,319]{1,0:T(2,128)S(1)}, s32[2,192]{1,0:T(2,128)S(1)}, f32[2,319,256]{2,1,0:T(8,128)S(1)},...) while((s32[]{:T(128)}, f32[2,192,256]{2,1,0:T(8,128)S(1)}, ...), condition=%wide.region_2.3_spmd.clone, body=%wide.region_1.2_spmd.clone.sunk | while | flops 4823171 | bytes 7167463 | solution.py:107
  178.3 1.1 constant_dynamic-slice_fusion.33
  179.4 2.3 fusion.76
  182.1 1.1 constant_dynamic-slice_fusion.33
  183.2 2.3 fusion.76
  185.9 1.1 constant_dynamic-slice_fusion.33
  187.0 2.3 fusion.76
  189.8 1.1 constant_dynamic-slice_fusion.33
  190.8 2.3 fusion.76
  193.6 1.1 constant_dynamic-slice_fusion.33
  194.6 2.3 fusion.76
  197.4 1.1 constant_dynamic-slice_fusion.33
  198.4 2.3 fusion.76
  201.2 1.1 constant_dynamic-slice_fusion.33
  202.2 2.3 fusion.76
  205.0 1.1 constant_dynamic-slice_fusion.33
  206.1 2.3 fusion.76
  209.2 96.7 %all-gather.14.cloned.1.call-done = bf16[384,4096]{1,0:T(8,128)(2,1)} async-done(((bf16[384,256]{1,0:T(8,128)(2,1)}), bf16[384,4096]{1,0:T(8,128)(2,1)}) %all-gather.14.cloned.1.call-update) | async-done | bytes 3145744 | tf_op jit(solution)/shard_map/all_gather | solution.py:50
  305.9 3.6 convert_reduce_fusion.1
  310.3 0.9 copy.27
  311.3 2.6 collective-permute-start.3
  314.1 2.5 gather_fusion.3
  316.8 2.5 gather_fusion.4
  319.4 9.3 %collective-permute-done.3 = bf16[256,256]{1,0:T(8,128)(2,1)S(1)} collective-permute-done((bf16[256,256]{1,0:T(8,128)(2,1)S(1)}, bf16[256,256]{1,0:T(8,128)(2,1)S(1)}, u32[]{:S(2)}, u32[]{:S(2)}) %collective-permute-start.3) | collective-permute-done | bytes 131104 | tf_op jit(solution)/shard_map/ppermute | solution.py:44
  331.6 71.9 %all-gather.18.cloned.1.call-done = bf16[384,4096]{1,0:T(8,128)(2,1)} async-done(((bf16[384,256]{1,0:T(8,128)(2,1)}), bf16[384,4096]{1,0:T(8,128)(2,1)}) %all-gather.18.cloned.1.call-update) | async-done | bytes 3145744 | tf_op jit(solution)/shard_map/all_gather | solution.py:25
  403.5 2.6 fusion.34
  406.1 50.0 %all-gather.20.cloned.1.call-done = bf16[4096,3,256]{0,2,1:T(8,128)(2,1)} async-done(((bf16[256,3,256]{0,2,1:T(8,128)(2,1)}), bf16[4096,3,256]{0,2,1:T(8,128)(2,1)}) %all-gather.20.cloned.1.call-update) | async-done | bytes 6291472 | tf_op jit(solution)/shard_map/all_gather | solution.py:30
  456.1 6.4 %fusion.58 = bf16[384,768]{1,0:T(8,128)(2,1)S(1)} fusion(bf16[4096,768]{0,1:T(8,128)(2,1)} %bitcast.127, bf16[384,4096]{1,0:T(8,128)(2,1)} %all-gather.18.cloned.1.call-done, f32[4096]{0:T(1024)S(1)} %copy-done.9, f32[384]{0:T(512)S(1)} %add_rsqrt_fusion), kind=kOutput, calls=%fused_computation.94 | convolution fusion | flops 2422505472 | bytes 10044928 | tf_op jit(solution)/shard_map/dot_general | solution.py:32
  462.6 0.8 convert.2.x_ref
  464.0 4.1 shard_map.109
  468.1 17.6 %all-gather = f32[32,16,256]{2,1,0:T(8,128)S(1)} all-gather(f32[2,16,256]{2,1,0:T(8,128)} %get-tuple-element.240), channel_id=2, replica_groups=mesh['ctx'=16,'ch'=16] {'ctx'}, dimensions={0}, use_global_device_ids=true | all-gather | bytes 557056 | tf_op jit(solution)/shard_map/all_gather | solution.py:158
  485.9 0.9 multiply_reduce_fusion.init_ref
  486.8 4.1 shard_map.110
  490.9 1.7 fusion.61
  492.7 2.6 all-gather.24.cloned.1.call-done
  495.2 98.3 %all-gather.22.cloned.1.call-done = bf16[384,4096]{1,0:T(8,128)(2,1)} async-done(((bf16[384,256]{1,0:T(8,128)(2,1)}), bf16[384,4096]{1,0:T(8,128)(2,1)}) %all-gather.22.cloned.1.call-update) | async-done | bytes 3145744 | tf_op jit(solution)/shard_map/all_gather | solution.py:50
  593.6 3.6 convert_reduce_fusion
  (91 shorter events, 10.9 us)
Async XLA Ops:
  6.5 8.0 %copy-start = (s32[6144]{0:T(1024)S(1)}, s32[6144]{0:T(1024)}, u32[]{:S(2)}) copy-start(s32[6144]{0:T(1024)} %param.25) | copy-start | bytes 73732
  6.5 102.8 %all-gather.10.cloned.1.call-start = ((), (), s32[]{:S(2)}) async-start(), calls=%async_computation | async-start | bytes 3342336 | tf_op jit(solution)/shard_map/all_gather | solution.py:25
  7.3 154.8 %all-gather.12.cloned.1.call-start = ((), (), s32[]{:S(2)}) async-start(), calls=%async_computation.1 | async-start | bytes 6684672 | tf_op jit(solution)/shard_map/all_gather | solution.py:30
  9.2 199.9 %all-gather.16.cloned.1.call-start = ((), (), s32[]{:S(2)}) async-start(), calls=%async_computation.3 | async-start | bytes 2228224 | tf_op jit(solution)/shard_map/all_gather | solution.py:45
  9.3 14.2 %collective-permute-start.2 = (bf16[256,256]{1,0:T(8,128)(2,1)}, bf16[256,256]{1,0:T(8,128)(2,1)S(1)}, u32[]{:S(2)}, u32[]{:S(2)}) collective-permute-start(bf16[256,256]{1,0:T(8,128)(2,1)} %param.18), channel_id=1, source_target_pairs={{0,0},{1,16},{2,32},{3,48},{4,64},{5,80},{6,96},{7,112},{8,128},{9... | collective-permute-start | bytes 393224 | tf_op jit(solution)/shard_map/ppermute | solution.py:44
  15.4 146.7 %copy-start.8 = (f32[4096]{0:T(1024)S(1)}, f32[4096]{0:T(1024)}, u32[]{:S(2)}) copy-start(f32[4096]{0:T(1024)} %param.16) | copy-start | bytes 49156
  23.5 0.6 copy-start.4
  24.1 281.7 %all-gather.14.cloned.1.call-start = ((), (), s32[]{:S(2)}) async-start(), calls=%async_computation.2 | async-start | bytes 3342336 | tf_op jit(solution)/shard_map/all_gather | solution.py:50
  168.6 5.6 collective-permute-start.1
  172.2 5.6 collective-permute-start
  209.1 194.5 %all-gather.18.cloned.1.call-start = ((), (), s32[]{:S(2)}) async-start(), calls=%async_computation.4 | async-start | bytes 3342336 | tf_op jit(solution)/shard_map/all_gather | solution.py:25
  305.8 3.6 copy-start.2
  305.8 4.4 copy-start.3
  305.8 5.4 copy-start.7
  310.2 20.8 %copy-start.6 = (f32[16,256]{1,0:T(8,128)S(1)}, f32[16,256]{1,0:T(8,128)}, u32[]{:S(2)}) copy-start(f32[16,256]{1,0:T(8,128)} %param.23) | copy-start | bytes 49156
  310.2 145.9 %all-gather.20.cloned.1.call-start = ((), (), s32[]{:S(2)}) async-start(), calls=%async_computation.5 | async-start | bytes 6684672 | tf_op jit(solution)/shard_map/all_gather | solution.py:30
  311.2 184.0 %all-gather.24.cloned.1.call-start = ((), (), s32[]{:S(2)}) async-start(), calls=%async_computation.7 | async-start | bytes 2228224 | tf_op jit(solution)/shard_map/all_gather | solution.py:45
  311.3 17.4 %collective-permute-start.3 = (bf16[256,256]{1,0:T(8,128)(2,1)S(1)}, bf16[256,256]{1,0:T(8,128)(2,1)S(1)}, u32[]{:S(2)}, u32[]{:S(2)}) collective-permute-start(bf16[256,256]{1,0:T(8,128)(2,1)S(1)} %copy-done.7), channel_id=1, source_target_pairs={{0,0},{1,16},{2,32},{3,48},{4,64},{5,80},{6,96},{7,112},{8,128},{9... | collective-permute-start | bytes 393224 | tf_op jit(solution)/shard_map/ppermute | solution.py:44
  316.6 139.5 %copy-start.9 = (f32[4096]{0:T(1024)S(1)}, f32[4096]{0:T(1024)}, u32[]{:S(2)}) copy-start(f32[4096]{0:T(1024)} %param.20) | copy-start | bytes 49156
  328.7 0.6 copy-start.5
  329.3 264.2 %all-gather.22.cloned.1.call-start = ((), (), s32[]{:S(2)}) async-start(), calls=%async_computation.6 | async-start | bytes 3342336 | tf_op jit(solution)/shard_map/all_gather | solution.py:50
  593.6 3.6 copy-start.1
Sparse Core Ops, SparseCore 0:
  9.8 99.5 all-gather.9
  111.1 50.9 all-gather.11
  164.0 36.6 all-gather.15
  209.2 96.5 all-gather.13
  310.3 93.1 all-gather.17
  405.2 50.9 all-gather.19
  458.0 37.2 all-gather.23
  497.7 95.8 all-gather.21

commit v2 on v1

--- a/solution.py
+++ b/solution.py
@@ -21,8 +21,16 @@
     return value
 
 
+CH = ("z", "yh")
+
+
+def gather_channels(value):
+    pair = lax.all_gather(value, "yh", axis=1, tiled=True)
+    return lax.all_gather(pair, "z", axis=1, tiled=True)
+
+
 def features_in(stream, gain, inproj):
-    whole = lax.all_gather(stream, "ch", axis=1, tiled=True)
+    whole = gather_channels(stream)
     floats = whole.astype(jnp.float32)
     scaled = lax.rsqrt(jnp.mean(floats * floats, axis=1, keepdims=True) + 1e-06)
     normed = (floats * scaled * gain[None, :]).astype(jnp.bfloat16)
@@ -38,16 +46,16 @@
 
 
 def outproj_columns(outproj):
-    ctx_count, ch_count = (lax.axis_size("ctx"), lax.axis_size("ch"))
+    ctx_count, ch_count = (lax.axis_size("ctx"), lax.axis_size(CH))
     assert ctx_count == ch_count
     pairs = [(i * ch_count + c, c * ch_count + i) for i in range(ctx_count) for c in range(ch_count)]
-    swapped = lax.ppermute(outproj, ("ctx", "ch"), pairs)
+    swapped = lax.ppermute(outproj, ("ctx",) + CH, pairs)
     return lax.all_gather(swapped, "ctx", axis=0, tiled=True)
 
 
 def features_out(stream, query, mixed, columns):
     gated = (query.astype(jnp.float32) * mixed).astype(jnp.bfloat16)
-    whole = lax.all_gather(gated, "ch", axis=1, tiled=True)
+    whole = gather_channels(gated)
     rows, width = gated.shape
     groups = whole.shape[1] // width
     parts = jnp.einsum(
@@ -192,18 +200,23 @@
 
 
 def solution(mesh):
+    ctx_count, ch_count = mesh.devices.shape
+    pair_count = 2 if ch_count % 2 == 0 else 1
+    view = jax.sharding.Mesh(
+        mesh.devices.reshape(ctx_count, ch_count // pair_count, pair_count), ("ctx",) + CH
+    )
     in_specs = (
-        P("ctx", "ch"),
+        P("ctx", CH),
         P(),
-        P("ctx", None, "ch"),
-        P("ch", "ctx"),
-        P(None, "ch"),
+        P("ctx", None, CH),
+        P(CH, "ctx"),
+        P(None, CH),
         P(),
-        P("ctx", None, "ch"),
-        P("ch", "ctx"),
-        P(None, "ch"),
-        P(None, "ch"),
+        P("ctx", None, CH),
+        P(CH, "ctx"),
+        P(None, CH),
+        P(None, CH),
         P(),
     )
-    out_specs = P("ctx", "ch")
-    return jax.shard_map(body, mesh=mesh, in_specs=in_specs, out_specs=out_specs, check_vma=False)
+    out_specs = P("ctx", CH)
+    return jax.shard_map(body, mesh=view, in_specs=in_specs, out_specs=out_specs, check_vma=False)

time: 606 us -> 443 us (0.73)
  waiting for transfers between devices: 473 us -> 274 us
  blocking collectives: 17.6 us -> 54.8 us
    all_gather x4, waiting for transfers between devices: 352 us -> 151 us  [gather_channels(): return lax.all_gather(pair, 'z', axis=1, tiled=True)]
    all_gather x0 -> x4, blocking collectives: none -> 36.6 us  [gather_channels(): pair = lax.all_gather(value, 'yh', axis=1, tiled=True)]
    all_gather x2, waiting for transfers between devices: 100 us -> 107 us  [features_in(): piece = lax.all_gather(inproj, 'ctx', axis=0, tiled=True)]
  transfers between devices with their start and end apart: 12 -> 12, of which waited for: 10 -> 9; matrix products, arithmetic and copies ran while one was open for 11% -> 15% of each run, Pallas kernels for 1% -> 2%
where the time goes in v2:
time: 443 us; the launch traced here: 442 us
  waiting for transfers between devices  274 us (62%)
  blocking collectives  54.8 us (12%)
  other arithmetic  30 us (7%)
  local copies, waits for them, and re-layouts  25 us (6%)
  matrix products  19 us (4%)
  starting transfers between devices  14.7 us (3%)
  between operations  13.8 us (3%)
  Pallas kernels  8.28 us (2%)
    all_gather x4, waiting for transfers between devices, gather_channels(): return lax.all_gather(pair, 'z', axis=1, tiled=True)  151 us
    all_gather x2, waiting for transfers between devices, features_in(): piece = lax.all_gather(inproj, 'ctx', axis=0, tiled=True)  107 us
    all_gather x4, blocking collectives, gather_channels(): pair = lax.all_gather(value, 'yh', axis=1, tiled=True)  36.6 us
    all_gather x1, blocking collectives, long_mix(): gathered = lax.all_gather(ends, 'ctx', axis=0, tiled=False)  18.2 us
    add x8, other arithmetic, tap_group(): running + jnp.where((source_docs == target_docs)[:, :, None], source, 0.0...  17.9 us
    ppermute x2, waiting for transfers between devices, outproj_columns(): swapped = lax.ppermute(outproj, ('ctx',) + CH, pairs)  12.9 us
    dot_general x2, matrix products, features_in(): jnp.dot(normed, flat, preferred_element_type=jnp.float32)  11.8 us
    ppermute x2, starting transfers between devices, outproj_columns(): swapped = lax.ppermute(outproj, ('ctx',) + CH, pairs)  8.89 us
  transfers between devices with their start and end apart: 12, of which 9 were waited for; matrix products, arithmetic and copies ran while one was open for 15% of the time, Pallas kernels for 2%

profile of v2, /device:TPU:4, one launch (start us, length us, event | category | flops | bytes accessed | tf_op | source)
XLA Modules:
  0.0 441.8 jit_solution(15284442360526173078)
XLA Ops:
  6.5 10.8 %all_gather.42 = bf16[384,512]{1,0:T(8,128)(2,1)} all-gather(bf16[384,256]{1,0:T(8,128)(2,1)} %param.15), channel_id=1, replica_groups=mesh['ctx'=16,'z'=8,'yh'=2] {'yh'}, dimensions={1}, use_global_device_ids=true | all-gather | bytes 589824 | tf_op jit(solution)/shard_map/all_gather | solution.py:28
  17.4 1.9 copy.25
  19.4 5.1 %collective-permute-start.2 = (bf16[256,256]{1,0:T(8,128)(2,1)}, bf16[256,256]{1,0:T(8,128)(2,1)S(1)}, u32[]{:S(2)}, u32[]{:S(2)}) collective-permute-start(bf16[256,256]{1,0:T(8,128)(2,1)} %param.18), channel_id=1, source_target_pairs={{0,0},{1,16},{2,32},{3,48},{4,64},{5,80},{6,96},{7,112},{8,128},{9... | collective-permute-start | bytes 393224 | tf_op jit(solution)/shard_map/ppermute | solution.py:52
  25.6 3.9 gather_fusion
  29.7 6.1 %collective-permute-done.2 = bf16[256,256]{1,0:T(8,128)(2,1)S(1)} collective-permute-done((bf16[256,256]{1,0:T(8,128)(2,1)}, bf16[256,256]{1,0:T(8,128)(2,1)S(1)}, u32[]{:S(2)}, u32[]{:S(2)}) %collective-permute-start.2) | collective-permute-done | bytes 131104 | tf_op jit(solution)/shard_map/ppermute | solution.py:52
  36.5 30.3 %all-gather.10.cloned.1.call-done = bf16[384,4096]{1,0:T(8,128)(2,1)} async-done(((bf16[384,512]{1,0:T(8,128)(2,1)}), bf16[384,4096]{1,0:T(8,128)(2,1)}) %all-gather.10.cloned.1.call-update) | async-done | bytes 3145744 | tf_op jit(solution)/shard_map/all_gather | solution.py:29
  66.8 2.6 fusion.31
  69.4 54.4 %all-gather.12.cloned.1.call-done = bf16[4096,3,256]{0,2,1:T(8,128)(2,1)} async-done(((bf16[256,3,256]{0,2,1:T(8,128)(2,1)}), bf16[4096,3,256]{0,2,1:T(8,128)(2,1)}) %all-gather.12.cloned.1.call-update) | async-done | bytes 6291472 | tf_op jit(solution)/shard_map/all_gather | solution.py:38
  123.9 6.4 %fusion.55 = bf16[384,768]{1,0:T(8,128)(2,1)S(1)} fusion(bf16[4096,768]{0,1:T(8,128)(2,1)} %bitcast.126, bf16[384,4096]{1,0:T(8,128)(2,1)} %all-gather.10.cloned.1.call-done, f32[4096]{0:T(1024)S(1)} %copy-done.9, f32[384]{0:T(512)S(1)} %add_rsqrt_fusion.1), kind=kOutput, calls=%fused_computation.93 | convolution fusion | flops 2422505472 | bytes 10044928 | tf_op jit(solution)/shard_map/dot_general | solution.py:40
  130.4 3.6 collective-permute-start.1
  134.0 1.9 collective-permute-start
  136.0 3.6 collective-permute-done
  139.7 30.2 %while.17 = (s32[]{:T(128)}, f32[2,192,256]{2,1,0:T(8,128)S(1)}, s32[2,319]{1,0:T(2,128)S(1)}, s32[2,192]{1,0:T(2,128)S(1)}, f32[2,319,256]{2,1,0:T(8,128)S(1)},...) while((s32[]{:T(128)}, f32[2,192,256]{2,1,0:T(8,128)S(1)}, ...), condition=%wide.region_2.3_spmd.clone, body=%wide.region_1.2_spmd.clone.sunk | while | flops 4823171 | bytes 7167463 | solution.py:115
  140.1 1.1 constant_dynamic-slice_fusion.33
  141.2 2.2 fusion.76
  143.9 1.1 constant_dynamic-slice_fusion.33
  145.0 2.2 fusion.76
  147.7 1.1 constant_dynamic-slice_fusion.33
  148.7 2.2 fusion.76
  151.4 1.1 constant_dynamic-slice_fusion.33
  152.5 2.2 fusion.76
  155.2 1.1 constant_dynamic-slice_fusion.33
  156.3 2.2 fusion.76
  159.0 1.1 constant_dynamic-slice_fusion.33
  160.1 2.2 fusion.76
  162.8 1.1 constant_dynamic-slice_fusion.33
  163.9 2.2 fusion.76
  166.5 1.1 constant_dynamic-slice_fusion.33
  167.6 2.2 fusion.76
  169.9 7.9 %all_gather.45 = bf16[384,512]{1,0:T(8,128)(2,1)} all-gather(bf16[384,256]{1,0:T(8,128)(2,1)S(1)} %fusion.62), channel_id=1, replica_groups=mesh['ctx'=16,'z'=8,'yh'=2] {'yh'}, dimensions={1}, use_global_device_ids=true | all-gather | bytes 589824 | tf_op jit(solution)/shard_map/all_gather | solution.py:28
  178.0 47.1 %all-gather.14.cloned.1.call-done = bf16[384,4096]{1,0:T(8,128)(2,1)} async-done(((bf16[384,512]{1,0:T(8,128)(2,1)}), bf16[384,4096]{1,0:T(8,128)(2,1)}) %all-gather.14.cloned.1.call-update) | async-done | bytes 3145744 | tf_op jit(solution)/shard_map/all_gather | solution.py:29
  225.1 3.6 convert_reduce_fusion.1
  228.8 8.3 %all_gather.48 = bf16[384,512]{1,0:T(8,128)(2,1)} all-gather(bf16[384,256]{1,0:T(8,128)(2,1)S(1)} %add_convert_fusion.1), channel_id=1, replica_groups=mesh['ctx'=16,'z'=8,'yh'=2] {'yh'}, dimensions={1}, use_global_device_ids=true | all-gather | bytes 589824 | tf_op jit(solution)/shard_map/all_gather | solution.py:28
  238.2 3.8 collective-permute-start.3
  242.2 2.5 gather_fusion.3
  244.9 2.5 gather_fusion.4
  247.5 6.8 %collective-permute-done.3 = bf16[256,256]{1,0:T(8,128)(2,1)S(1)} collective-permute-done((bf16[256,256]{1,0:T(8,128)(2,1)S(1)}, bf16[256,256]{1,0:T(8,128)(2,1)S(1)}, u32[]{:S(2)}, u32[]{:S(2)}) %collective-permute-start.3) | collective-permute-done | bytes 131104 | tf_op jit(solution)/shard_map/ppermute | solution.py:52
  257.3 27.2 %all-gather.18.cloned.1.call-done = bf16[384,4096]{1,0:T(8,128)(2,1)} async-done(((bf16[384,512]{1,0:T(8,128)(2,1)}), bf16[384,4096]{1,0:T(8,128)(2,1)}) %all-gather.18.cloned.1.call-update) | async-done | bytes 3145744 | tf_op jit(solution)/shard_map/all_gather | solution.py:29
  284.4 2.7 fusion.34
  287.2 52.2 %all-gather.20.cloned.1.call-done = bf16[4096,3,256]{0,2,1:T(8,128)(2,1)} async-done(((bf16[256,3,256]{0,2,1:T(8,128)(2,1)}), bf16[4096,3,256]{0,2,1:T(8,128)(2,1)}) %all-gather.20.cloned.1.call-update) | async-done | bytes 6291472 | tf_op jit(solution)/shard_map/all_gather | solution.py:38
  339.4 5.4 %fusion.58 = bf16[384,768]{1,0:T(8,128)(2,1)S(1)} fusion(bf16[4096,768]{0,1:T(8,128)(2,1)} %bitcast.127, bf16[384,4096]{1,0:T(8,128)(2,1)S(1)} %copy-done.1, f32[4096]{0:T(1024)S(1)} %copy-done.10, f32[384]{0:T(512)S(1)} %add_rsqrt_fusion), kind=kOutput, calls=%fused_computation.94 | convolution fusion | flops 2422505472 | bytes 10044928 | tf_op jit(solution)/shard_map/dot_general | solution.py:40
  346.4 4.1 shard_map.109
  350.6 18.2 %all-gather = f32[32,16,256]{2,1,0:T(8,128)S(1)} all-gather(f32[2,16,256]{2,1,0:T(8,128)} %get-tuple-element.240), channel_id=2, replica_groups=mesh['ctx'=16,'z'=8,'yh'=2] {'ctx'}, dimensions={0}, use_global_device_ids=true | all-gather | bytes 557056 | tf_op jit(solution)/shard_map/all_gather | solution.py:166
  369.8 4.1 shard_map.110
  374.0 1.1 fusion.61
  375.1 9.4 %all_gather.53 = bf16[384,512]{1,0:T(8,128)(2,1)} all-gather(bf16[384,256]{1,0:T(8,128)(2,1)S(1)} %fusion.61), channel_id=1, replica_groups=mesh['ctx'=16,'z'=8,'yh'=2] {'yh'}, dimensions={1}, use_global_device_ids=true | all-gather | bytes 589824 | tf_op jit(solution)/shard_map/all_gather | solution.py:28
  384.6 46.1 %all-gather.22.cloned.1.call-done = bf16[384,4096]{1,0:T(8,128)(2,1)} async-done(((bf16[384,512]{1,0:T(8,128)(2,1)}), bf16[384,4096]{1,0:T(8,128)(2,1)}) %all-gather.22.cloned.1.call-update) | async-done | bytes 3145744 | tf_op jit(solution)/shard_map/all_gather | solution.py:29
  430.7 3.5 convert_reduce_fusion
  (97 shorter events, 11.8 us)
Async XLA Ops:
  6.5 18.2 %copy-start = (s32[6144]{0:T(1024)S(1)}, s32[6144]{0:T(1024)}, u32[]{:S(2)}) copy-start(s32[6144]{0:T(1024)} %param.25) | copy-start | bytes 73732
  6.5 60.3 %all-gather.10.cloned.1.call-start = ((), (), s32[]{:S(2)}) async-start(), calls=%async_computation | async-start | bytes 3538944 | tf_op jit(solution)/shard_map/all_gather | solution.py:29
  17.4 106.5 %all-gather.12.cloned.1.call-start = ((), (), s32[]{:S(2)}) async-start(), calls=%async_computation.1 | async-start | bytes 6684672 | tf_op jit(solution)/shard_map/all_gather | solution.py:38
  19.4 158.6 %all-gather.16.cloned.1.call-start = ((), (), s32[]{:S(2)}) async-start(), calls=%async_computation.3 | async-start | bytes 2228224 | tf_op jit(solution)/shard_map/all_gather | solution.py:53
  19.4 16.3 %collective-permute-start.2 = (bf16[256,256]{1,0:T(8,128)(2,1)}, bf16[256,256]{1,0:T(8,128)(2,1)S(1)}, u32[]{:S(2)}, u32[]{:S(2)}) collective-permute-start(bf16[256,256]{1,0:T(8,128)(2,1)} %param.18), channel_id=1, source_target_pairs={{0,0},{1,16},{2,32},{3,48},{4,64},{5,80},{6,96},{7,112},{8,128},{9... | collective-permute-start | bytes 393224 | tf_op jit(solution)/shard_map/ppermute | solution.py:52
  25.6 98.3 %copy-start.9 = (f32[4096]{0:T(1024)S(1)}, f32[4096]{0:T(1024)}, u32[]{:S(2)}) copy-start(f32[4096]{0:T(1024)} %param.16) | copy-start | bytes 49156
  35.8 0.7 copy-start.5
  36.5 188.6 %all-gather.14.cloned.1.call-start = ((), (), s32[]{:S(2)}) async-start(), calls=%async_computation.2 | async-start | bytes 3538944 | tf_op jit(solution)/shard_map/all_gather | solution.py:29
  130.4 5.5 %collective-permute-start.1 = (bf16[127,256]{1,0:T(8,128)(2,1)S(1)}, bf16[127,256]{1,0:T(8,128)(2,1)S(1)}, u32[]{:S(2)}, u32[]{:S(2)}) collective-permute-start(bf16[127,256]{1,0:T(8,128)(2,1)S(1)} %get-tuple-element.312), channel_id=1, source_target_pairs={{16,0},{32,16},{48,32},{64,48},{80,64},{96,80},{112,96},{128,112},... | collective-permute-start | bytes 195080 | tf_op jit(solution)/shard_map/ppermute | solution.py:19
  134.0 5.6 %collective-permute-start = (bf16[127,256]{1,0:T(8,128)(2,1)S(1)}, bf16[127,256]{1,0:T(8,128)(2,1)S(1)}, u32[]{:S(2)}, u32[]{:S(2)}) collective-permute-start(bf16[127,256]{1,0:T(8,128)(2,1)S(1)} %get-tuple-element.311), channel_id=1, source_target_pairs={{0,16},{16,32},{32,48},{48,64},{64,80},{80,96},{96,112},{112,128},... | collective-permute-start | bytes 195080 | tf_op jit(solution)/shard_map/ppermute | solution.py:18
  177.9 106.5 %all-gather.18.cloned.1.call-start = ((), (), s32[]{:S(2)}) async-start(), calls=%async_computation.4 | async-start | bytes 3538944 | tf_op jit(solution)/shard_map/all_gather | solution.py:29
  225.1 3.6 copy-start.2
  225.1 12.1 %copy-start.4 = (bf16[256,3,256]{2,0,1:T(8,128)(2,1)S(1)}, bf16[256,3,256]{2,0,1:T(8,128)(2,1)}, u32[]{:S(2)}) copy-start(bf16[256,3,256]{2,0,1:T(8,128)(2,1)} %param.21) | copy-start | bytes 1179652
  225.1 13.1 %copy-start.8 = (bf16[256,256]{1,0:T(8,128)(2,1)S(1)}, bf16[256,256]{1,0:T(8,128)(2,1)}, u32[]{:S(2)}) copy-start(bf16[256,256]{1,0:T(8,128)(2,1)} %param.22) | copy-start | bytes 393220
  237.1 19.5 %copy-start.7 = (f32[16,256]{1,0:T(8,128)S(1)}, f32[16,256]{1,0:T(8,128)}, u32[]{:S(2)}) copy-start(f32[16,256]{1,0:T(8,128)} %param.23) | copy-start | bytes 49156
  237.2 102.2 %all-gather.20.cloned.1.call-start = ((), (), s32[]{:S(2)}) async-start(), calls=%async_computation.5 | async-start | bytes 6684672 | tf_op jit(solution)/shard_map/all_gather | solution.py:38
  238.2 146.4 %all-gather.24.cloned.1.call-start = ((), (), s32[]{:S(2)}) async-start(), calls=%async_computation.7 | async-start | bytes 2228224 | tf_op jit(solution)/shard_map/all_gather | solution.py:53
  238.2 16.1 %collective-permute-start.3 = (bf16[256,256]{1,0:T(8,128)(2,1)S(1)}, bf16[256,256]{1,0:T(8,128)(2,1)S(1)}, u32[]{:S(2)}, u32[]{:S(2)}) collective-permute-start(bf16[256,256]{1,0:T(8,128)(2,1)S(1)} %copy-done.8), channel_id=1, source_target_pairs={{0,0},{1,16},{2,32},{3,48},{4,64},{5,80},{6,96},{7,112},{8,128},{9... | collective-permute-start | bytes 393224 | tf_op jit(solution)/shard_map/ppermute | solution.py:52
  244.7 94.6 %copy-start.10 = (f32[4096]{0:T(1024)S(1)}, f32[4096]{0:T(1024)}, u32[]{:S(2)}) copy-start(f32[4096]{0:T(1024)} %param.20) | copy-start | bytes 49156
  254.3 0.7 copy-start.6
  255.0 175.7 %all-gather.22.cloned.1.call-start = ((), (), s32[]{:S(2)}) async-start(), calls=%async_computation.6 | async-start | bytes 3538944 | tf_op jit(solution)/shard_map/all_gather | solution.py:29
  284.4 54.9 %copy-start.1 = (bf16[384,4096]{1,0:T(8,128)(2,1)S(1)}, bf16[384,4096]{1,0:T(8,128)(2,1)}, u32[]{:S(2)}) copy-start(bf16[384,4096]{1,0:T(8,128)(2,1)} %all-gather.18.cloned.1.call-done) | copy-start | bytes 9437188
  344.8 1.0 copy-start.3
Sparse Core Ops, SparseCore 0:
  17.5 49.2 all-gather.9
  68.6 55.2 all-gather.11
  125.7 36.6 all-gather.15
  178.0 47.0 all-gather.13
  237.3 47.1 all-gather.17
  286.1 53.2 all-gather.19
  341.2 37.2 all-gather.23
  384.7 45.9 all-gather.21

commit v3 on v2

--- a/solution.py
+++ b/solution.py
@@ -29,13 +29,16 @@
     return lax.all_gather(pair, "z", axis=1, tiled=True)
 
 
-def features_in(stream, gain, inproj):
+def gather_weights(inproj):
+    return lax.all_gather(inproj, "ctx", axis=0, tiled=True)
+
+
+def features_in(stream, gain, piece):
     whole = gather_channels(stream)
     floats = whole.astype(jnp.float32)
     scaled = lax.rsqrt(jnp.mean(floats * floats, axis=1, keepdims=True) + 1e-06)
     normed = (floats * scaled * gain[None, :]).astype(jnp.bfloat16)
-    channels = inproj.shape[2]
-    piece = lax.all_gather(inproj, "ctx", axis=0, tiled=True)
+    channels = piece.shape[2]
     flat = piece.reshape(piece.shape[0], 3 * channels)
     joined = jnp.dot(normed, flat, preferred_element_type=jnp.float32).astype(jnp.bfloat16)
     product = (
@@ -79,7 +82,7 @@
 
 def short_mix(product, mr_filter, doc_ids):
     shard_rows, channels = product.shape
-    ctx_count, ctx_index, span_rows, span_starts, positions = span_layout(shard_rows)
+    ctx_count, ctx_index, span_rows, span_starts, _ = span_layout(shard_rows)
     tap_count = mr_filter.shape[0]
     reach_rows = tap_count - 1
     halves = product.reshape(2, span_rows, channels)
@@ -154,7 +157,7 @@
 
 def long_mix(product, li_decay, li_residue, doc_ids):
     shard_rows, channels = product.shape
-    ctx_count, ctx_index, span_rows, span_starts, positions = span_layout(shard_rows)
+    ctx_count, _, span_rows, span_starts, positions = span_layout(shard_rows)
     modes = li_decay.shape[0]
     own_docs = jnp.take(doc_ids, positions)
     prior_docs = jnp.take(doc_ids, jnp.clip(positions - 1, 0, None))
@@ -191,11 +194,14 @@
     li_residue,
     doc_ids,
 ):
+    mr_piece = gather_weights(mr_inproj)
+    li_piece = gather_weights(li_inproj)
     mr_columns = outproj_columns(mr_outproj)
     li_columns = outproj_columns(li_outproj)
-    query, product = features_in(tokens, mr_gain, mr_inproj)
-    stream = features_out(tokens, query, short_mix(product, mr_filter, doc_ids), mr_columns)
-    query, product = features_in(stream, li_gain, li_inproj)
+    query, product = features_in(tokens, mr_gain, mr_piece)
+    mixed = short_mix(product, mr_filter, doc_ids)
+    stream = features_out(tokens, query, mixed, mr_columns)
+    query, product = features_in(stream, li_gain, li_piece)
     return features_out(stream, query, long_mix(product, li_decay, li_residue, doc_ids), li_columns)
 
 

time: 443 us -> 443 us (level)
  no operation moved by 1% of the time
where the time goes in v3:
time: 443 us; the launch traced here: 442 us
  waiting for transfers between devices  274 us (62%)
  blocking collectives  54.8 us (12%)
  other arithmetic  30 us (7%)
  local copies, waits for them, and re-layouts  25 us (6%)
  matrix products  19 us (4%)
  starting transfers between devices  14.7 us (3%)
  between operations  13.8 us (3%)
  Pallas kernels  8.28 us (2%)
    all_gather x4, waiting for transfers between devices, gather_channels(): return lax.all_gather(pair, 'z', axis=1, tiled=True)  151 us
    all_gather x2, waiting for transfers between devices, gather_weights(): return lax.all_gather(inproj, 'ctx', axis=0, tiled=True)  107 us
    all_gather x4, blocking collectives, gather_channels(): pair = lax.all_gather(value, 'yh', axis=1, tiled=True)  36.6 us
    all_gather x1, blocking collectives, long_mix(): gathered = lax.all_gather(ends, 'ctx', axis=0, tiled=False)  18.2 us
    add x8, other arithmetic, tap_group(): running + jnp.where((source_docs == target_docs)[:, :, None], source, 0.0...  17.9 us
    ppermute x2, waiting for transfers between devices, outproj_columns(): swapped = lax.ppermute(outproj, ('ctx',) + CH, pairs)  12.9 us
    dot_general x2, matrix products, features_in(): jnp.dot(normed, flat, preferred_element_type=jnp.float32)  11.8 us
    ppermute x2, starting transfers between devices, outproj_columns(): swapped = lax.ppermute(outproj, ('ctx',) + CH, pairs)  8.89 us
  transfers between devices with their start and end apart: 12, of which 9 were waited for; matrix products, arithmetic and copies ran while one was open for 15% of the time, Pallas kernels for 2%

profile of v3, /device:TPU:4, one launch (start us, length us, event | category | flops | bytes accessed | tf_op | source)
XLA Modules:
  0.0 441.8 jit_solution(15284442360526173078)
XLA Ops:
  6.5 10.8 %all_gather.42 = bf16[384,512]{1,0:T(8,128)(2,1)} all-gather(bf16[384,256]{1,0:T(8,128)(2,1)} %param.15), channel_id=1, replica_groups=mesh['ctx'=16,'z'=8,'yh'=2] {'yh'}, dimensions={1}, use_global_device_ids=true | all-gather | bytes 589824 | tf_op jit(solution)/shard_map/all_gather | solution.py:28
  17.4 1.9 copy.25
  19.4 5.1 %collective-permute-start.2 = (bf16[256,256]{1,0:T(8,128)(2,1)}, bf16[256,256]{1,0:T(8,128)(2,1)S(1)}, u32[]{:S(2)}, u32[]{:S(2)}) collective-permute-start(bf16[256,256]{1,0:T(8,128)(2,1)} %param.18), channel_id=1, source_target_pairs={{0,0},{1,16},{2,32},{3,48},{4,64},{5,80},{6,96},{7,112},{8,128},{9... | collective-permute-start | bytes 393224 | tf_op jit(solution)/shard_map/ppermute | solution.py:55
  25.6 3.9 gather_fusion
  29.7 6.1 %collective-permute-done.2 = bf16[256,256]{1,0:T(8,128)(2,1)S(1)} collective-permute-done((bf16[256,256]{1,0:T(8,128)(2,1)}, bf16[256,256]{1,0:T(8,128)(2,1)S(1)}, u32[]{:S(2)}, u32[]{:S(2)}) %collective-permute-start.2) | collective-permute-done | bytes 131104 | tf_op jit(solution)/shard_map/ppermute | solution.py:55
  36.5 30.3 %all-gather.10.cloned.1.call-done = bf16[384,4096]{1,0:T(8,128)(2,1)} async-done(((bf16[384,512]{1,0:T(8,128)(2,1)}), bf16[384,4096]{1,0:T(8,128)(2,1)}) %all-gather.10.cloned.1.call-update) | async-done | bytes 3145744 | tf_op jit(solution)/shard_map/all_gather | solution.py:29
  66.8 2.6 fusion.31
  69.4 54.4 %all-gather.12.cloned.1.call-done = bf16[4096,3,256]{0,2,1:T(8,128)(2,1)} async-done(((bf16[256,3,256]{0,2,1:T(8,128)(2,1)}), bf16[4096,3,256]{0,2,1:T(8,128)(2,1)}) %all-gather.12.cloned.1.call-update) | async-done | bytes 6291472 | tf_op jit(solution)/shard_map/all_gather | solution.py:33
  123.9 6.4 %fusion.55 = bf16[384,768]{1,0:T(8,128)(2,1)S(1)} fusion(bf16[4096,768]{0,1:T(8,128)(2,1)} %bitcast.126, bf16[384,4096]{1,0:T(8,128)(2,1)} %all-gather.10.cloned.1.call-done, f32[4096]{0:T(1024)S(1)} %copy-done.9, f32[384]{0:T(512)S(1)} %add_rsqrt_fusion.1), kind=kOutput, calls=%fused_computation.93 | convolution fusion | flops 2422505472 | bytes 10044928 | tf_op jit(solution)/shard_map/dot_general | solution.py:43
  130.4 3.6 collective-permute-start.1
  134.0 1.9 collective-permute-start
  136.0 3.6 collective-permute-done
  139.7 30.2 %while.17 = (s32[]{:T(128)}, f32[2,192,256]{2,1,0:T(8,128)S(1)}, s32[2,319]{1,0:T(2,128)S(1)}, s32[2,192]{1,0:T(2,128)S(1)}, f32[2,319,256]{2,1,0:T(8,128)S(1)},...) while((s32[]{:T(128)}, f32[2,192,256]{2,1,0:T(8,128)S(1)}, ...), condition=%wide.region_2.3_spmd.clone, body=%wide.region_1.2_spmd.clone.sunk | while | flops 4823171 | bytes 7167463 | solution.py:118
  140.1 1.1 constant_dynamic-slice_fusion.33
  141.2 2.2 fusion.76
  143.9 1.1 constant_dynamic-slice_fusion.33
  145.0 2.2 fusion.76
  147.7 1.1 constant_dynamic-slice_fusion.33
  148.7 2.2 fusion.76
  151.4 1.1 constant_dynamic-slice_fusion.33
  152.5 2.2 fusion.76
  155.2 1.1 constant_dynamic-slice_fusion.33
  156.3 2.2 fusion.76
  159.0 1.1 constant_dynamic-slice_fusion.33
  160.1 2.2 fusion.76
  162.8 1.1 constant_dynamic-slice_fusion.33
  163.9 2.2 fusion.76
  166.5 1.1 constant_dynamic-slice_fusion.33
  167.6 2.2 fusion.76
  169.9 7.9 %all_gather.45 = bf16[384,512]{1,0:T(8,128)(2,1)} all-gather(bf16[384,256]{1,0:T(8,128)(2,1)S(1)} %fusion.62), channel_id=1, replica_groups=mesh['ctx'=16,'z'=8,'yh'=2] {'yh'}, dimensions={1}, use_global_device_ids=true | all-gather | bytes 589824 | tf_op jit(solution)/shard_map/all_gather | solution.py:28
  178.0 47.1 %all-gather.14.cloned.1.call-done = bf16[384,4096]{1,0:T(8,128)(2,1)} async-done(((bf16[384,512]{1,0:T(8,128)(2,1)}), bf16[384,4096]{1,0:T(8,128)(2,1)}) %all-gather.14.cloned.1.call-update) | async-done | bytes 3145744 | tf_op jit(solution)/shard_map/all_gather | solution.py:29
  225.1 3.6 convert_reduce_fusion.1
  228.8 8.3 %all_gather.48 = bf16[384,512]{1,0:T(8,128)(2,1)} all-gather(bf16[384,256]{1,0:T(8,128)(2,1)S(1)} %add_convert_fusion.1), channel_id=1, replica_groups=mesh['ctx'=16,'z'=8,'yh'=2] {'yh'}, dimensions={1}, use_global_device_ids=true | all-gather | bytes 589824 | tf_op jit(solution)/shard_map/all_gather | solution.py:28
  238.2 3.8 collective-permute-start.3
  242.2 2.5 gather_fusion.3
  244.9 2.5 gather_fusion.4
  247.5 6.8 %collective-permute-done.3 = bf16[256,256]{1,0:T(8,128)(2,1)S(1)} collective-permute-done((bf16[256,256]{1,0:T(8,128)(2,1)S(1)}, bf16[256,256]{1,0:T(8,128)(2,1)S(1)}, u32[]{:S(2)}, u32[]{:S(2)}) %collective-permute-start.3) | collective-permute-done | bytes 131104 | tf_op jit(solution)/shard_map/ppermute | solution.py:55
  257.3 27.2 %all-gather.18.cloned.1.call-done = bf16[384,4096]{1,0:T(8,128)(2,1)} async-done(((bf16[384,512]{1,0:T(8,128)(2,1)}), bf16[384,4096]{1,0:T(8,128)(2,1)}) %all-gather.18.cloned.1.call-update) | async-done | bytes 3145744 | tf_op jit(solution)/shard_map/all_gather | solution.py:29
  284.4 2.7 fusion.34
  287.2 52.2 %all-gather.20.cloned.1.call-done = bf16[4096,3,256]{0,2,1:T(8,128)(2,1)} async-done(((bf16[256,3,256]{0,2,1:T(8,128)(2,1)}), bf16[4096,3,256]{0,2,1:T(8,128)(2,1)}) %all-gather.20.cloned.1.call-update) | async-done | bytes 6291472 | tf_op jit(solution)/shard_map/all_gather | solution.py:33
  339.4 5.4 %fusion.58 = bf16[384,768]{1,0:T(8,128)(2,1)S(1)} fusion(bf16[4096,768]{0,1:T(8,128)(2,1)} %bitcast.127, bf16[384,4096]{1,0:T(8,128)(2,1)S(1)} %copy-done.1, f32[4096]{0:T(1024)S(1)} %copy-done.10, f32[384]{0:T(512)S(1)} %add_rsqrt_fusion), kind=kOutput, calls=%fused_computation.94 | convolution fusion | flops 2422505472 | bytes 10044928 | tf_op jit(solution)/shard_map/dot_general | solution.py:43
  346.4 4.1 shard_map.109
  350.6 18.2 %all-gather = f32[32,16,256]{2,1,0:T(8,128)S(1)} all-gather(f32[2,16,256]{2,1,0:T(8,128)} %get-tuple-element.240), channel_id=2, replica_groups=mesh['ctx'=16,'z'=8,'yh'=2] {'ctx'}, dimensions={0}, use_global_device_ids=true | all-gather | bytes 557056 | tf_op jit(solution)/shard_map/all_gather | solution.py:169
  369.8 4.1 shard_map.110
  374.0 1.1 fusion.61
  375.1 9.4 %all_gather.53 = bf16[384,512]{1,0:T(8,128)(2,1)} all-gather(bf16[384,256]{1,0:T(8,128)(2,1)S(1)} %fusion.61), channel_id=1, replica_groups=mesh['ctx'=16,'z'=8,'yh'=2] {'yh'}, dimensions={1}, use_global_device_ids=true | all-gather | bytes 589824 | tf_op jit(solution)/shard_map/all_gather | solution.py:28
  384.6 46.1 %all-gather.22.cloned.1.call-done = bf16[384,4096]{1,0:T(8,128)(2,1)} async-done(((bf16[384,512]{1,0:T(8,128)(2,1)}), bf16[384,4096]{1,0:T(8,128)(2,1)}) %all-gather.22.cloned.1.call-update) | async-done | bytes 3145744 | tf_op jit(solution)/shard_map/all_gather | solution.py:29
  430.7 3.5 convert_reduce_fusion
  (97 shorter events, 11.8 us)
Async XLA Ops:
  6.5 18.2 %copy-start = (s32[6144]{0:T(1024)S(1)}, s32[6144]{0:T(1024)}, u32[]{:S(2)}) copy-start(s32[6144]{0:T(1024)} %param.25) | copy-start | bytes 73732
  6.5 60.3 %all-gather.10.cloned.1.call-start = ((), (), s32[]{:S(2)}) async-start(), calls=%async_computation | async-start | bytes 3538944 | tf_op jit(solution)/shard_map/all_gather | solution.py:29
  17.4 106.5 %all-gather.12.cloned.1.call-start = ((), (), s32[]{:S(2)}) async-start(), calls=%async_computation.1 | async-start | bytes 6684672 | tf_op jit(solution)/shard_map/all_gather | solution.py:33
  19.4 158.6 %all-gather.16.cloned.1.call-start = ((), (), s32[]{:S(2)}) async-start(), calls=%async_computation.3 | async-start | bytes 2228224 | tf_op jit(solution)/shard_map/all_gather | solution.py:56
  19.4 16.3 %collective-permute-start.2 = (bf16[256,256]{1,0:T(8,128)(2,1)}, bf16[256,256]{1,0:T(8,128)(2,1)S(1)}, u32[]{:S(2)}, u32[]{:S(2)}) collective-permute-start(bf16[256,256]{1,0:T(8,128)(2,1)} %param.18), channel_id=1, source_target_pairs={{0,0},{1,16},{2,32},{3,48},{4,64},{5,80},{6,96},{7,112},{8,128},{9... | collective-permute-start | bytes 393224 | tf_op jit(solution)/shard_map/ppermute | solution.py:55
  25.6 98.3 %copy-start.9 = (f32[4096]{0:T(1024)S(1)}, f32[4096]{0:T(1024)}, u32[]{:S(2)}) copy-start(f32[4096]{0:T(1024)} %param.16) | copy-start | bytes 49156
  35.8 0.7 copy-start.5
  36.5 188.6 %all-gather.14.cloned.1.call-start = ((), (), s32[]{:S(2)}) async-start(), calls=%async_computation.2 | async-start | bytes 3538944 | tf_op jit(solution)/shard_map/all_gather | solution.py:29
  130.4 5.5 %collective-permute-start.1 = (bf16[127,256]{1,0:T(8,128)(2,1)S(1)}, bf16[127,256]{1,0:T(8,128)(2,1)S(1)}, u32[]{:S(2)}, u32[]{:S(2)}) collective-permute-start(bf16[127,256]{1,0:T(8,128)(2,1)S(1)} %get-tuple-element.312), channel_id=1, source_target_pairs={{16,0},{32,16},{48,32},{64,48},{80,64},{96,80},{112,96},{128,112},... | collective-permute-start | bytes 195080 | tf_op jit(solution)/shard_map/ppermute | solution.py:19
  134.0 5.6 %collective-permute-start = (bf16[127,256]{1,0:T(8,128)(2,1)S(1)}, bf16[127,256]{1,0:T(8,128)(2,1)S(1)}, u32[]{:S(2)}, u32[]{:S(2)}) collective-permute-start(bf16[127,256]{1,0:T(8,128)(2,1)S(1)} %get-tuple-element.311), channel_id=1, source_target_pairs={{0,16},{16,32},{32,48},{48,64},{64,80},{80,96},{96,112},{112,128},... | collective-permute-start | bytes 195080 | tf_op jit(solution)/shard_map/ppermute | solution.py:18
  177.9 106.5 %all-gather.18.cloned.1.call-start = ((), (), s32[]{:S(2)}) async-start(), calls=%async_computation.4 | async-start | bytes 3538944 | tf_op jit(solution)/shard_map/all_gather | solution.py:29
  225.1 3.6 copy-start.2
  225.1 12.1 %copy-start.4 = (bf16[256,3,256]{2,0,1:T(8,128)(2,1)S(1)}, bf16[256,3,256]{2,0,1:T(8,128)(2,1)}, u32[]{:S(2)}) copy-start(bf16[256,3,256]{2,0,1:T(8,128)(2,1)} %param.21) | copy-start | bytes 1179652
  225.1 13.1 %copy-start.8 = (bf16[256,256]{1,0:T(8,128)(2,1)S(1)}, bf16[256,256]{1,0:T(8,128)(2,1)}, u32[]{:S(2)}) copy-start(bf16[256,256]{1,0:T(8,128)(2,1)} %param.22) | copy-start | bytes 393220
  237.1 19.5 %copy-start.7 = (f32[16,256]{1,0:T(8,128)S(1)}, f32[16,256]{1,0:T(8,128)}, u32[]{:S(2)}) copy-start(f32[16,256]{1,0:T(8,128)} %param.23) | copy-start | bytes 49156
  237.2 102.2 %all-gather.20.cloned.1.call-start = ((), (), s32[]{:S(2)}) async-start(), calls=%async_computation.5 | async-start | bytes 6684672 | tf_op jit(solution)/shard_map/all_gather | solution.py:33
  238.2 146.4 %all-gather.24.cloned.1.call-start = ((), (), s32[]{:S(2)}) async-start(), calls=%async_computation.7 | async-start | bytes 2228224 | tf_op jit(solution)/shard_map/all_gather | solution.py:56
  238.2 16.1 %collective-permute-start.3 = (bf16[256,256]{1,0:T(8,128)(2,1)S(1)}, bf16[256,256]{1,0:T(8,128)(2,1)S(1)}, u32[]{:S(2)}, u32[]{:S(2)}) collective-permute-start(bf16[256,256]{1,0:T(8,128)(2,1)S(1)} %copy-done.8), channel_id=1, source_target_pairs={{0,0},{1,16},{2,32},{3,48},{4,64},{5,80},{6,96},{7,112},{8,128},{9... | collective-permute-start | bytes 393224 | tf_op jit(solution)/shard_map/ppermute | solution.py:55
  244.7 94.6 %copy-start.10 = (f32[4096]{0:T(1024)S(1)}, f32[4096]{0:T(1024)}, u32[]{:S(2)}) copy-start(f32[4096]{0:T(1024)} %param.20) | copy-start | bytes 49156
  254.3 0.7 copy-start.6
  255.0 175.7 %all-gather.22.cloned.1.call-start = ((), (), s32[]{:S(2)}) async-start(), calls=%async_computation.6 | async-start | bytes 3538944 | tf_op jit(solution)/shard_map/all_gather | solution.py:29
  284.4 54.9 %copy-start.1 = (bf16[384,4096]{1,0:T(8,128)(2,1)S(1)}, bf16[384,4096]{1,0:T(8,128)(2,1)}, u32[]{:S(2)}) copy-start(bf16[384,4096]{1,0:T(8,128)(2,1)} %all-gather.18.cloned.1.call-done) | copy-start | bytes 9437188
  344.8 1.0 copy-start.3
Sparse Core Ops, SparseCore 0:
  17.5 49.2 all-gather.9
  68.6 55.2 all-gather.11
  125.7 36.6 all-gather.15
  178.0 47.0 all-gather.13
  237.3 47.1 all-gather.17
  286.1 53.2 all-gather.19
  341.2 37.2 all-gather.23
  384.7 45.9 all-gather.21

commit v4 on v3

--- a/solution.py
+++ b/solution.py
@@ -31,6 +31,17 @@
 
 def gather_weights(inproj):
     return lax.all_gather(inproj, "ctx", axis=0, tiled=True)
+
+
+def gather_by_fanout(value):
+    count = lax.axis_size("ctx")
+    index = lax.axis_index("ctx")
+    received = [value] + [
+        lax.ppermute(value, "ctx", [(i, i ^ shift) for i in range(count)]) for shift in range(1, count)
+    ]
+    order = jnp.bitwise_xor(jnp.arange(count), index)
+    blocks = jnp.take(jnp.stack(received), order, axis=0)
+    return blocks.reshape((count * value.shape[0],) + value.shape[1:])
 
 
 def features_in(stream, gain, piece):
@@ -48,11 +59,13 @@
     return (joined[:, :channels], product)
 
 
-def outproj_columns(outproj):
+def outproj_columns(outproj, gather=None):
     ctx_count, ch_count = (lax.axis_size("ctx"), lax.axis_size(CH))
     assert ctx_count == ch_count
     pairs = [(i * ch_count + c, c * ch_count + i) for i in range(ctx_count) for c in range(ch_count)]
     swapped = lax.ppermute(outproj, ("ctx",) + CH, pairs)
+    if gather is not None:
+        return gather(swapped)
     return lax.all_gather(swapped, "ctx", axis=0, tiled=True)
 
 
@@ -195,7 +208,7 @@
     doc_ids,
 ):
     mr_piece = gather_weights(mr_inproj)
-    li_piece = gather_weights(li_inproj)
+    li_piece = gather_by_fanout(li_inproj)
     mr_columns = outproj_columns(mr_outproj)
     li_columns = outproj_columns(li_outproj)
     query, product = features_in(tokens, mr_gain, mr_piece)

time: 443 us -> 480 us (1.084)
  local copies, waits for them, and re-layouts: 25 us -> 61.4 us
  waiting for transfers between devices: 274 us -> 240 us
  starting transfers between devices: 14.7 us -> 39.9 us
  blocking collectives: 54.8 us -> 62.5 us
    ppermute x0 -> x15, waiting for transfers between devices: none -> 54.9 us  [gather_by_fanout(): lax.ppermute(value, 'ctx', [(i, i ^ shift) for i in range(count)])]
    all_gather x2 -> x1, waiting for transfers between devices: 107 us -> 54.4 us  [gather_weights(): return lax.all_gather(inproj, 'ctx', axis=0, tiled=True)]
    all_gather x4, waiting for transfers between devices: 151 us -> 120 us  [gather_channels(): return lax.all_gather(pair, 'z', axis=1, tiled=True)]
    ppermute x0 -> x15, starting transfers between devices: none -> 22.9 us  [gather_by_fanout(): lax.ppermute(value, 'ctx', [(i, i ^ shift) for i in range(count)])]
    unnamed x24 -> x35, local copies, waits for them, and re-layouts: 4.27 us -> 24.2 us
    gather x0 -> x2, local copies, waits for them, and re-layouts: none -> 15.6 us  [gather_by_fanout(): blocks = jnp.take(jnp.stack(received), order, axis=0)]
    ppermute x2, waiting for transfers between devices: 12.9 us -> 7.17 us  [outproj_columns(): swapped = lax.ppermute(outproj, ('ctx',) + CH, pairs)]
  transfers between devices with their start and end apart: 12 -> 26, of which waited for: 9 -> 14; matrix products, arithmetic and copies ran while one was open for 15% -> 21% of each run, Pallas kernels for 2% -> 2%
where the time goes in v4:
time: 480 us; the launch traced here: 478 us
  waiting for transfers between devices  240 us (50%)
  blocking collectives  62.5 us (13%)
  local copies, waits for them, and re-layouts  61.4 us (13%)
  starting transfers between devices  39.9 us (8%)
  other arithmetic  29.8 us (6%)
  matrix products  19.9 us (4%)
  between operations  13.8 us (3%)
  Pallas kernels  8.32 us (2%)
    all_gather x4, waiting for transfers between devices, gather_channels(): return lax.all_gather(pair, 'z', axis=1, tiled=True)  120 us
    ppermute x15, waiting for transfers between devices, gather_by_fanout(): lax.ppermute(value, 'ctx', [(i, i ^ shift) for i in range(count)])  54.9 us
    all_gather x1, waiting for transfers between devices, gather_weights(): return lax.all_gather(inproj, 'ctx', axis=0, tiled=True)  54.4 us
    all_gather x4, blocking collectives, gather_channels(): pair = lax.all_gather(value, 'yh', axis=1, tiled=True)  39.5 us
    unnamed x35, local copies, waits for them, and re-layouts  24.2 us
    all_gather x1, blocking collectives, long_mix(): gathered = lax.all_gather(ends, 'ctx', axis=0, tiled=False)  23 us
    ppermute x15, starting transfers between devices, gather_by_fanout(): lax.ppermute(value, 'ctx', [(i, i ^ shift) for i in range(count)])  22.9 us
    add x8, other arithmetic, tap_group(): running + jnp.where((source_docs == target_docs)[:, :, None], source, 0.0...  18 us
  transfers between devices with their start and end apart: 26, of which 14 were waited for; matrix products, arithmetic and copies ran while one was open for 21% of the time, Pallas kernels for 2%

profile of v4, /device:TPU:4, one launch (start us, length us, event | category | flops | bytes accessed | tf_op | source)
XLA Modules:
  0.0 478.4 jit_solution(11174541647269789956)
XLA Ops:
  6.5 10.8 %all_gather.39 = bf16[384,512]{1,0:T(8,128)(2,1)} all-gather(bf16[384,256]{1,0:T(8,128)(2,1)} %param.15), channel_id=1, replica_groups=mesh['ctx'=16,'z'=8,'yh'=2] {'yh'}, dimensions={1}, use_global_device_ids=true | all-gather | bytes 589824 | tf_op jit(solution)/shard_map/all_gather | solution.py:28
  19.5 5.1 %collective-permute-start.2 = (bf16[256,256]{1,0:T(8,128)(2,1)}, bf16[256,256]{1,0:T(8,128)(2,1)S(1)}, u32[]{:S(2)}, u32[]{:S(2)}) collective-permute-start(bf16[256,256]{1,0:T(8,128)(2,1)} %param.18), channel_id=1, source_target_pairs={{0,0},{1,16},{2,32},{3,48},{4,64},{5,80},{6,96},{7,112},{8,128},{9... | collective-permute-start | bytes 393224 | tf_op jit(solution)/shard_map/ppermute | solution.py:66
  25.6 3.9 gather_fusion
  29.7 6.2 %collective-permute-done.2 = bf16[256,256]{1,0:T(8,128)(2,1)S(1)} collective-permute-done((bf16[256,256]{1,0:T(8,128)(2,1)}, bf16[256,256]{1,0:T(8,128)(2,1)S(1)}, u32[]{:S(2)}, u32[]{:S(2)}) %collective-permute-start.2) | collective-permute-done | bytes 131104 | tf_op jit(solution)/shard_map/ppermute | solution.py:66
  36.6 30.2 %all-gather.9.cloned.1.call-done = bf16[384,4096]{1,0:T(8,128)(2,1)} async-done(((bf16[384,512]{1,0:T(8,128)(2,1)}), bf16[384,4096]{1,0:T(8,128)(2,1)}) %all-gather.9.cloned.1.call-update) | async-done | bytes 3145744 | tf_op jit(solution)/shard_map/all_gather | solution.py:29
  66.9 2.6 fusion.31
  69.5 54.4 %all-gather.11.cloned.1.call-done = bf16[4096,3,256]{0,2,1:T(8,128)(2,1)} async-done(((bf16[256,3,256]{0,2,1:T(8,128)(2,1)}), bf16[4096,3,256]{0,2,1:T(8,128)(2,1)}) %all-gather.11.cloned.1.call-update) | async-done | bytes 6291472 | tf_op jit(solution)/shard_map/all_gather | solution.py:33
  123.9 6.4 %fusion.58 = bf16[384,768]{1,0:T(8,128)(2,1)S(1)} fusion(bf16[4096,768]{0,1:T(8,128)(2,1)} %bitcast.165, bf16[384,4096]{1,0:T(8,128)(2,1)} %all-gather.9.cloned.1.call-done, f32[4096]{0:T(1024)S(1)} %copy-done.7, f32[384]{0:T(512)S(1)} %add_rsqrt_fusion.1), kind=kOutput, calls=%fused_computation.97 | convolution fusion | flops 2422505472 | bytes 10044928 | tf_op jit(solution)/shard_map/dot_general | solution.py:54
  130.4 3.6 collective-permute-start.1
  136.0 3.6 collective-permute-done
  139.7 30.4 %while.17 = (s32[]{:T(128)}, f32[2,192,256]{2,1,0:T(8,128)S(1)}, s32[2,319]{1,0:T(2,128)S(1)}, s32[2,192]{1,0:T(2,128)S(1)}, f32[2,319,256]{2,1,0:T(8,128)S(1)},...) while((s32[]{:T(128)}, f32[2,192,256]{2,1,0:T(8,128)S(1)}, ...), condition=%wide.region_2.3_spmd.clone, body=%wide.region_1.2_spmd.clone.sunk | while | flops 4823171 | bytes 7167463 | solution.py:131
  141.2 2.3 fusion.82
  145.0 2.3 fusion.82
  148.8 2.3 fusion.82
  152.6 2.3 fusion.82
  156.4 2.3 fusion.82
  160.2 2.3 fusion.82
  164.0 2.3 fusion.82
  167.8 2.3 fusion.82
  170.1 8.1 %all_gather.42 = bf16[384,512]{1,0:T(8,128)(2,1)} all-gather(bf16[384,256]{1,0:T(8,128)(2,1)S(1)} %fusion.67), channel_id=1, replica_groups=mesh['ctx'=16,'z'=8,'yh'=2] {'yh'}, dimensions={1}, use_global_device_ids=true | all-gather | bytes 589824 | tf_op jit(solution)/shard_map/all_gather | solution.py:28
  178.3 47.1 %all-gather.13.cloned.1.call-done = bf16[384,4096]{1,0:T(8,128)(2,1)} async-done(((bf16[384,512]{1,0:T(8,128)(2,1)}), bf16[384,4096]{1,0:T(8,128)(2,1)}) %all-gather.13.cloned.1.call-update) | async-done | bytes 3145744 | tf_op jit(solution)/shard_map/all_gather | solution.py:29
  225.4 3.5 convert_reduce_fusion.1
  229.0 8.3 %all_gather.45 = bf16[384,512]{1,0:T(8,128)(2,1)} all-gather(bf16[384,256]{1,0:T(8,128)(2,1)S(1)} %add_convert_fusion.1), channel_id=1, replica_groups=mesh['ctx'=16,'z'=8,'yh'=2] {'yh'}, dimensions={1}, use_global_device_ids=true | all-gather | bytes 589824 | tf_op jit(solution)/shard_map/all_gather | solution.py:28
  239.9 6.2 %collective-permute-start.18 = (bf16[256,256]{1,0:T(8,128)(2,1)S(1)}, bf16[256,256]{1,0:T(8,128)(2,1)S(1)}, u32[]{:S(2)}, u32[]{:S(2)}) collective-permute-start(bf16[256,256]{1,0:T(8,128)(2,1)S(1)} %copy-done.6), channel_id=1, source_target_pairs={{0,0},{1,16},{2,32},{3,48},{4,64},{5,80},{6,96},{7,112},{8,128},{9... | collective-permute-start | bytes 393224 | tf_op jit(solution)/shard_map/ppermute | solution.py:66
  246.4 2.5 gather_fusion.4
  249.0 2.5 gather_fusion.5
  256.4 4.8 collective-permute-start.8
  263.2 6.7 %collective-permute-start.10 = (bf16[256,3,256]{2,0,1:T(8,128)(2,1)S(1)}, bf16[256,3,256]{2,0,1:T(8,128)(2,1)S(1)}, u32[]{:S(2)}, u32[]{:S(2)}) collective-permute-start(bf16[256,3,256]{2,0,1:T(8,128)(2,1)S(1)} %copy-done.2), channel_id=1, source_target_pairs={{0,128},{16,144},{32,160},{48,176},{64,192},{80,208},{96,224},{112... | collective-permute-start | bytes 1179656 | tf_op jit(solution)/shard_map/ppermute | solution.py:40
  270.8 7.0 %collective-permute-done.6 = bf16[256,3,256]{2,0,1:T(8,128)(2,1)S(1)} collective-permute-done((bf16[256,3,256]{2,0,1:T(8,128)(2,1)S(1)}, bf16[256,3,256]{2,0,1:T(8,128)(2,1)S(1)}, u32[]{:S(2)}, u32[]{:S(2)}) %collective-permute-start.6) | collective-permute-done | bytes 393248 | tf_op jit(solution)/shard_map/ppermute | solution.py:40
  278.6 6.5 %collective-permute-done.7 = bf16[256,3,256]{2,0,1:T(8,128)(2,1)S(1)} collective-permute-done((bf16[256,3,256]{2,0,1:T(8,128)(2,1)S(1)}, bf16[256,3,256]{2,0,1:T(8,128)(2,1)S(1)}, u32[]{:S(2)}, u32[]{:S(2)}) %collective-permute-start.7) | collective-permute-done | bytes 393248 | tf_op jit(solution)/shard_map/ppermute | solution.py:40
  285.9 2.0 collective-permute-done.8
  289.4 7.1 %collective-permute-done.9 = bf16[256,3,256]{2,0,1:T(8,128)(2,1)S(1)} collective-permute-done((bf16[256,3,256]{2,0,1:T(8,128)(2,1)S(1)}, bf16[256,3,256]{2,0,1:T(8,128)(2,1)S(1)}, u32[]{:S(2)}, u32[]{:S(2)}) %collective-permute-start.9) | collective-permute-done | bytes 393248 | tf_op jit(solution)/shard_map/ppermute | solution.py:40
  297.3 3.7 collective-permute-start.15
  301.8 19.0 %collective-permute-done.11 = bf16[256,3,256]{2,0,1:T(8,128)(2,1)S(1)} collective-permute-done((bf16[256,3,256]{2,0,1:T(8,128)(2,1)S(1)}, bf16[256,3,256]{2,0,1:T(8,128)(2,1)S(1)}, u32[]{:S(2)}, u32[]{:S(2)}) %collective-permute-start.11) | collective-permute-done | bytes 393248 | tf_op jit(solution)/shard_map/ppermute | solution.py:40
  320.8 3.5 collective-permute-start.16
  328.2 6.3 %collective-permute-done.16 = bf16[256,3,256]{2,0,1:T(8,128)(2,1)S(1)} collective-permute-done((bf16[256,3,256]{2,0,1:T(8,128)(2,1)S(1)}, bf16[256,3,256]{2,0,1:T(8,128)(2,1)S(1)}, u32[]{:S(2)}, u32[]{:S(2)}) %collective-permute-start.16) | collective-permute-done | bytes 393248 | tf_op jit(solution)/shard_map/ppermute | solution.py:40
  335.4 6.8 %collective-permute-done.17 = bf16[256,3,256]{2,0,1:T(8,128)(2,1)S(1)} collective-permute-done((bf16[256,3,256]{2,0,1:T(8,128)(2,1)S(1)}, bf16[256,3,256]{2,0,1:T(8,128)(2,1)S(1)}, u32[]{:S(2)}, u32[]{:S(2)}) %collective-permute-start.17) | collective-permute-done | bytes 393248 | tf_op jit(solution)/shard_map/ppermute | solution.py:40
  342.9 6.4 %gather_fusion.1 = bf16[16,256,3,256]{3,1,2,0:T(8,128)(2,1)} fusion(bf16[16,256,3,256]{3,1,2,0:T(8,128)(2,1)} %bitcast_dynamic-update-slice_fusion, s32[1024]{0:T(1024)S(1)} %pad_clamp_fusion.4), kind=kCustom, calls=%fused_computation.3 | custom fusion | bytes 12582976 | tf_op jit(solution)/shard_map/jit(_take)/gather | solution.py:43
  349.3 9.2 %copy.27 = bf16[16,256,3,256]{1,0,3,2:T(8,128)(2,1)} copy(bf16[16,256,3,256]{3,1,2,0:T(8,128)(2,1)} %gather_fusion.1) | data formatting | bytes 12582912 | tf_op jit(solution)/shard_map/jit(_take)/gather | solution.py:43
  358.5 9.7 %copy.33 = bf16[96,8,16,256]{3,1,2,0:T(8,128)(2,1)} copy(bf16[96,8,16,256]{3,2,1,0:T(8,128)(2,1)} %bitcast.143) | data formatting | bytes 12582912
  368.2 2.6 fusion.34
  370.8 6.4 %fusion.61 = bf16[384,768]{1,0:T(8,128)(2,1)S(1)} fusion(bf16[4096,768]{0,1:T(8,128)(2,1)} %bitcast.144, pred[4096]{0:T(1024)(128)(4,1)S(1)} %broadcast_in_dim.468, bf16[384,4096]{1,0:T(8,128)(2,1)} %all-gather.17.cloned.1.call-done, f32[4096]{0:T(1024)S(1)} %copy-done.8, f32[384]{0:T(512)S(1)} %add_rsqrt_fusion), kind=kOutput, calls=%fused_computation.98 | convolution fusion | flops 2425651200 | bytes 10049024 | tf_op jit(solution)/shard_map/dot_general | solution.py:54
  378.7 4.2 shard_map.109
  382.8 23.0 %all-gather = f32[32,16,256]{2,1,0:T(8,128)S(1)} all-gather(f32[2,16,256]{2,1,0:T(8,128)} %get-tuple-element.240), channel_id=2, replica_groups=mesh['ctx'=16,'z'=8,'yh'=2] {'ctx'}, dimensions={0}, use_global_device_ids=true | all-gather | bytes 557056 | tf_op jit(solution)/shard_map/all_gather | solution.py:182
  406.8 4.2 shard_map.110
  412.0 12.3 %all_gather.49 = bf16[384,512]{1,0:T(8,128)(2,1)} all-gather(bf16[384,256]{1,0:T(8,128)(2,1)S(1)} %fusion.66), channel_id=1, replica_groups=mesh['ctx'=16,'z'=8,'yh'=2] {'yh'}, dimensions={1}, use_global_device_ids=true | all-gather | bytes 589824 | tf_op jit(solution)/shard_map/all_gather | solution.py:28
  424.4 42.9 %all-gather.19.cloned.1.call-done = bf16[384,4096]{1,0:T(8,128)(2,1)} async-done(((bf16[384,512]{1,0:T(8,128)(2,1)}), bf16[384,4096]{1,0:T(8,128)(2,1)}) %all-gather.19.cloned.1.call-update) | async-done | bytes 3145744 | tf_op jit(solution)/shard_map/all_gather | solution.py:29
  467.3 3.5 convert_reduce_fusion
  (141 shorter events, 41.4 us)
Async XLA Ops:
  6.5 18.2 %copy-start = (s32[6144]{0:T(1024)S(1)}, s32[6144]{0:T(1024)}, u32[]{:S(2)}) copy-start(s32[6144]{0:T(1024)} %param.25) | copy-start | bytes 73732
  6.5 117.3 %copy-start.7 = (f32[4096]{0:T(1024)S(1)}, f32[4096]{0:T(1024)}, u32[]{:S(2)}) copy-start(f32[4096]{0:T(1024)} %param.16) | copy-start | bytes 49156
  6.5 60.3 %all-gather.9.cloned.1.call-start = ((), (), s32[]{:S(2)}) async-start(), calls=%async_computation | async-start | bytes 3538944 | tf_op jit(solution)/shard_map/all_gather | solution.py:29
  17.4 106.5 %all-gather.11.cloned.1.call-start = ((), (), s32[]{:S(2)}) async-start(), calls=%async_computation.1 | async-start | bytes 6684672 | tf_op jit(solution)/shard_map/all_gather | solution.py:33
  19.4 158.9 %all-gather.15.cloned.1.call-start = ((), (), s32[]{:S(2)}) async-start(), calls=%async_computation.3 | async-start | bytes 2228224 | tf_op jit(solution)/shard_map/all_gather | solution.py:69
  19.5 16.4 %collective-permute-start.2 = (bf16[256,256]{1,0:T(8,128)(2,1)}, bf16[256,256]{1,0:T(8,128)(2,1)S(1)}, u32[]{:S(2)}, u32[]{:S(2)}) collective-permute-start(bf16[256,256]{1,0:T(8,128)(2,1)} %param.18), channel_id=1, source_target_pairs={{0,0},{1,16},{2,32},{3,48},{4,64},{5,80},{6,96},{7,112},{8,128},{9... | collective-permute-start | bytes 393224 | tf_op jit(solution)/shard_map/ppermute | solution.py:66
  35.9 0.7 copy-start.3
  36.6 188.8 %all-gather.13.cloned.1.call-start = ((), (), s32[]{:S(2)}) async-start(), calls=%async_computation.2 | async-start | bytes 3538944 | tf_op jit(solution)/shard_map/all_gather | solution.py:29
  130.4 5.6 %collective-permute-start.1 = (bf16[127,256]{1,0:T(8,128)(2,1)S(1)}, bf16[127,256]{1,0:T(8,128)(2,1)S(1)}, u32[]{:S(2)}, u32[]{:S(2)}) collective-permute-start(bf16[127,256]{1,0:T(8,128)(2,1)S(1)} %get-tuple-element.312), channel_id=1, source_target_pairs={{16,0},{32,16},{48,32},{64,48},{80,64},{96,80},{112,96},{128,112},... | collective-permute-start | bytes 195080 | tf_op jit(solution)/shard_map/ppermute | solution.py:19
  134.0 5.6 %collective-permute-start = (bf16[127,256]{1,0:T(8,128)(2,1)S(1)}, bf16[127,256]{1,0:T(8,128)(2,1)S(1)}, u32[]{:S(2)}, u32[]{:S(2)}) collective-permute-start(bf16[127,256]{1,0:T(8,128)(2,1)S(1)} %get-tuple-element.311), channel_id=1, source_target_pairs={{0,16},{16,32},{32,48},{48,64},{64,80},{80,96},{96,112},{112,128},... | collective-permute-start | bytes 195080 | tf_op jit(solution)/shard_map/ppermute | solution.py:18
  170.0 58.9 %copy-start.1 = (bf16[384,256]{1,0:T(8,128)(2,1)S(1)}, bf16[384,256]{1,0:T(8,128)(2,1)}, u32[]{:S(2)}) copy-start(bf16[384,256]{1,0:T(8,128)(2,1)} %param.15) | copy-start | bytes 589828
  170.1 67.4 %copy-start.2 = (bf16[256,3,256]{2,0,1:T(8,128)(2,1)S(1)}, bf16[256,3,256]{2,0,1:T(8,128)(2,1)}, u32[]{:S(2)}) copy-start(bf16[256,3,256]{2,0,1:T(8,128)(2,1)} %param.21) | copy-start | bytes 1179652
  170.1 69.9 %copy-start.6 = (bf16[256,256]{1,0:T(8,128)(2,1)S(1)}, bf16[256,256]{1,0:T(8,128)(2,1)}, u32[]{:S(2)}) copy-start(bf16[256,256]{1,0:T(8,128)(2,1)} %param.22) | copy-start | bytes 393220
  178.2 190.0 %all-gather.17.cloned.1.call-start = ((), (), s32[]{:S(2)}) async-start(), calls=%async_computation.4 | async-start | bytes 3538944 | tf_op jit(solution)/shard_map/all_gather | solution.py:29
  225.4 27.1 %copy-start.5 = (f32[16,256]{1,0:T(8,128)S(1)}, f32[16,256]{1,0:T(8,128)}, u32[]{:S(2)}) copy-start(f32[16,256]{1,0:T(8,128)} %param.23) | copy-start | bytes 49156
  237.4 187.0 %all-gather.21.cloned.1.call-start = ((), (), s32[]{:S(2)}) async-start(), calls=%async_computation.6 | async-start | bytes 2228224 | tf_op jit(solution)/shard_map/all_gather | solution.py:69
  237.4 19.0 %collective-permute-start.3 = (bf16[256,3,256]{2,0,1:T(8,128)(2,1)S(1)}, bf16[256,3,256]{2,0,1:T(8,128)(2,1)S(1)}, u32[]{:S(2)}, u32[]{:S(2)}) collective-permute-start(bf16[256,3,256]{2,0,1:T(8,128)(2,1)S(1)} %copy-done.2), channel_id=1, source_target_pairs={{0,16},{16,0},{32,48},{48,32},{64,80},{80,64},{96,112},{112,96},{1... | collective-permute-start | bytes 1179656 | tf_op jit(solution)/shard_map/ppermute | solution.py:40
  237.5 24.5 %collective-permute-start.4 = (bf16[256,3,256]{2,0,1:T(8,128)(2,1)S(1)}, bf16[256,3,256]{2,0,1:T(8,128)(2,1)S(1)}, u32[]{:S(2)}, u32[]{:S(2)}) collective-permute-start(bf16[256,3,256]{2,0,1:T(8,128)(2,1)S(1)} %copy-done.2), channel_id=1, source_target_pairs={{0,32},{16,48},{32,0},{48,16},{64,96},{80,112},{96,64},{112,80},{1... | collective-permute-start | bytes 1179656 | tf_op jit(solution)/shard_map/ppermute | solution.py:40
  238.8 24.4 %collective-permute-start.5 = (bf16[256,3,256]{2,0,1:T(8,128)(2,1)S(1)}, bf16[256,3,256]{2,0,1:T(8,128)(2,1)S(1)}, u32[]{:S(2)}, u32[]{:S(2)}) collective-permute-start(bf16[256,3,256]{2,0,1:T(8,128)(2,1)S(1)} %copy-done.2), channel_id=1, source_target_pairs={{0,48},{16,32},{32,16},{48,0},{64,112},{80,96},{96,80},{112,64},{1... | collective-permute-start | bytes 1179656 | tf_op jit(solution)/shard_map/ppermute | solution.py:40
  239.4 38.4 %collective-permute-start.6 = (bf16[256,3,256]{2,0,1:T(8,128)(2,1)S(1)}, bf16[256,3,256]{2,0,1:T(8,128)(2,1)S(1)}, u32[]{:S(2)}, u32[]{:S(2)}) collective-permute-start(bf16[256,3,256]{2,0,1:T(8,128)(2,1)S(1)} %copy-done.2), channel_id=1, source_target_pairs={{0,64},{16,80},{32,96},{48,112},{64,0},{80,16},{96,32},{112,48},{1... | collective-permute-start | bytes 1179656 | tf_op jit(solution)/shard_map/ppermute | solution.py:40
  239.9 15.8 %collective-permute-start.18 = (bf16[256,256]{1,0:T(8,128)(2,1)S(1)}, bf16[256,256]{1,0:T(8,128)(2,1)S(1)}, u32[]{:S(2)}, u32[]{:S(2)}) collective-permute-start(bf16[256,256]{1,0:T(8,128)(2,1)S(1)} %copy-done.6), channel_id=1, source_target_pairs={{0,0},{1,16},{2,32},{3,48},{4,64},{5,80},{6,96},{7,112},{8,128},{9... | collective-permute-start | bytes 393224 | tf_op jit(solution)/shard_map/ppermute | solution.py:66
  255.7 0.7 copy-start.4
  255.7 29.4 %collective-permute-start.7 = (bf16[256,3,256]{2,0,1:T(8,128)(2,1)S(1)}, bf16[256,3,256]{2,0,1:T(8,128)(2,1)S(1)}, u32[]{:S(2)}, u32[]{:S(2)}) collective-permute-start(bf16[256,3,256]{2,0,1:T(8,128)(2,1)S(1)} %copy-done.2), channel_id=1, source_target_pairs={{0,80},{16,64},{32,112},{48,96},{64,16},{80,0},{96,48},{112,32},{1... | collective-permute-start | bytes 1179656 | tf_op jit(solution)/shard_map/ppermute | solution.py:40
  256.4 210.9 %all-gather.19.cloned.1.call-start = ((), (), s32[]{:S(2)}) async-start(), calls=%async_computation.5 | async-start | bytes 3538944 | tf_op jit(solution)/shard_map/all_gather | solution.py:29
  256.4 31.5 %collective-permute-start.8 = (bf16[256,3,256]{2,0,1:T(8,128)(2,1)S(1)}, bf16[256,3,256]{2,0,1:T(8,128)(2,1)S(1)}, u32[]{:S(2)}, u32[]{:S(2)}) collective-permute-start(bf16[256,3,256]{2,0,1:T(8,128)(2,1)S(1)} %copy-done.2), channel_id=1, source_target_pairs={{0,96},{16,112},{32,64},{48,80},{64,32},{80,48},{96,0},{112,16},{1... | collective-permute-start | bytes 1179656 | tf_op jit(solution)/shard_map/ppermute | solution.py:40
  262.0 34.5 %collective-permute-start.9 = (bf16[256,3,256]{2,0,1:T(8,128)(2,1)S(1)}, bf16[256,3,256]{2,0,1:T(8,128)(2,1)S(1)}, u32[]{:S(2)}, u32[]{:S(2)}) collective-permute-start(bf16[256,3,256]{2,0,1:T(8,128)(2,1)S(1)} %copy-done.2), channel_id=1, source_target_pairs={{0,112},{16,96},{32,80},{48,64},{64,48},{80,32},{96,16},{112,0},{1... | collective-permute-start | bytes 1179656 | tf_op jit(solution)/shard_map/ppermute | solution.py:40
  263.2 34.0 %collective-permute-start.10 = (bf16[256,3,256]{2,0,1:T(8,128)(2,1)S(1)}, bf16[256,3,256]{2,0,1:T(8,128)(2,1)S(1)}, u32[]{:S(2)}, u32[]{:S(2)}) collective-permute-start(bf16[256,3,256]{2,0,1:T(8,128)(2,1)S(1)} %copy-done.2), channel_id=1, source_target_pairs={{0,128},{16,144},{32,160},{48,176},{64,192},{80,208},{96,224},{112... | collective-permute-start | bytes 1179656 | tf_op jit(solution)/shard_map/ppermute | solution.py:40
  277.8 43.0 %collective-permute-start.11 = (bf16[256,3,256]{2,0,1:T(8,128)(2,1)S(1)}, bf16[256,3,256]{2,0,1:T(8,128)(2,1)S(1)}, u32[]{:S(2)}, u32[]{:S(2)}) collective-permute-start(bf16[256,3,256]{2,0,1:T(8,128)(2,1)S(1)} %copy-done.2), channel_id=1, source_target_pairs={{0,144},{16,128},{32,176},{48,160},{64,208},{80,192},{96,240},{112... | collective-permute-start | bytes 1179656 | tf_op jit(solution)/shard_map/ppermute | solution.py:40
  285.1 39.9 %collective-permute-start.12 = (bf16[256,3,256]{2,0,1:T(8,128)(2,1)S(1)}, bf16[256,3,256]{2,0,1:T(8,128)(2,1)S(1)}, u32[]{:S(2)}, u32[]{:S(2)}) collective-permute-start(bf16[256,3,256]{2,0,1:T(8,128)(2,1)S(1)} %copy-done.2), channel_id=1, source_target_pairs={{0,160},{16,176},{32,128},{48,144},{64,224},{80,240},{96,192},{112... | collective-permute-start | bytes 1179656 | tf_op jit(solution)/shard_map/ppermute | solution.py:40
  287.9 37.9 %collective-permute-start.13 = (bf16[256,3,256]{2,0,1:T(8,128)(2,1)S(1)}, bf16[256,3,256]{2,0,1:T(8,128)(2,1)S(1)}, u32[]{:S(2)}, u32[]{:S(2)}) collective-permute-start(bf16[256,3,256]{2,0,1:T(8,128)(2,1)S(1)} %copy-done.2), channel_id=1, source_target_pairs={{0,176},{16,160},{32,144},{48,128},{64,240},{80,224},{96,208},{112... | collective-permute-start | bytes 1179656 | tf_op jit(solution)/shard_map/ppermute | solution.py:40
  296.5 30.1 %collective-permute-start.14 = (bf16[256,3,256]{2,0,1:T(8,128)(2,1)S(1)}, bf16[256,3,256]{2,0,1:T(8,128)(2,1)S(1)}, u32[]{:S(2)}, u32[]{:S(2)}) collective-permute-start(bf16[256,3,256]{2,0,1:T(8,128)(2,1)S(1)} %copy-done.2), channel_id=1, source_target_pairs={{0,192},{16,208},{32,224},{48,240},{64,128},{80,144},{96,160},{112... | collective-permute-start | bytes 1179656 | tf_op jit(solution)/shard_map/ppermute | solution.py:40
  297.3 30.2 %collective-permute-start.15 = (bf16[256,3,256]{2,0,1:T(8,128)(2,1)S(1)}, bf16[256,3,256]{2,0,1:T(8,128)(2,1)S(1)}, u32[]{:S(2)}, u32[]{:S(2)}) collective-permute-start(bf16[256,3,256]{2,0,1:T(8,128)(2,1)S(1)} %copy-done.2), channel_id=1, source_target_pairs={{0,208},{16,192},{32,240},{48,224},{64,144},{80,128},{96,176},{112... | collective-permute-start | bytes 1179656 | tf_op jit(solution)/shard_map/ppermute | solution.py:40
  320.8 13.8 %collective-permute-start.16 = (bf16[256,3,256]{2,0,1:T(8,128)(2,1)S(1)}, bf16[256,3,256]{2,0,1:T(8,128)(2,1)S(1)}, u32[]{:S(2)}, u32[]{:S(2)}) collective-permute-start(bf16[256,3,256]{2,0,1:T(8,128)(2,1)S(1)} %copy-done.2), channel_id=1, source_target_pairs={{0,224},{16,240},{32,192},{48,208},{64,160},{80,176},{96,128},{112... | collective-permute-start | bytes 1179656 | tf_op jit(solution)/shard_map/ppermute | solution.py:40
  325.0 17.1 %collective-permute-start.17 = (bf16[256,3,256]{2,0,1:T(8,128)(2,1)S(1)}, bf16[256,3,256]{2,0,1:T(8,128)(2,1)S(1)}, u32[]{:S(2)}, u32[]{:S(2)}) collective-permute-start(bf16[256,3,256]{2,0,1:T(8,128)(2,1)S(1)} %copy-done.2), channel_id=1, source_target_pairs={{0,240},{16,224},{32,208},{48,192},{64,176},{80,160},{96,144},{112... | collective-permute-start | bytes 1179656 | tf_op jit(solution)/shard_map/ppermute | solution.py:40
  358.5 12.3 %copy-start.8 = (f32[4096]{0:T(1024)S(1)}, f32[4096]{0:T(1024)}, u32[]{:S(2)}) copy-start(f32[4096]{0:T(1024)} %param.20) | copy-start | bytes 49156
Sparse Core Ops, SparseCore 0:
  17.5 49.2 all-gather.8
  68.6 55.1 all-gather.10
  125.7 36.6 all-gather.14
  178.4 46.9 all-gather.12
  237.5 50.0 all-gather.16
  289.3 74.6 all-gather.20
  424.5 42.7 all-gather.18

commit v5 on v3

--- a/solution.py
+++ b/solution.py
@@ -48,12 +48,23 @@
     return (joined[:, :channels], product)
 
 
-def outproj_columns(outproj):
+def swap_blocks(outproj):
     ctx_count, ch_count = (lax.axis_size("ctx"), lax.axis_size(CH))
     assert ctx_count == ch_count
     pairs = [(i * ch_count + c, c * ch_count + i) for i in range(ctx_count) for c in range(ch_count)]
-    swapped = lax.ppermute(outproj, ("ctx",) + CH, pairs)
-    return lax.all_gather(swapped, "ctx", axis=0, tiled=True)
+    return lax.ppermute(outproj, ("ctx",) + CH, pairs)
+
+
+def outproj_columns(outproj):
+    return lax.all_gather(swap_blocks(outproj), "ctx", axis=0, tiled=True)
+
+
+def gather_layer_weights(inproj, outproj):
+    rows, parts, channels = inproj.shape
+    joined = jnp.concatenate([inproj.reshape(rows, parts * channels), swap_blocks(outproj)], 1)
+    whole = lax.all_gather(joined, "ctx", axis=0, tiled=True)
+    piece = whole[:, : parts * channels].reshape(whole.shape[0], parts, channels)
+    return piece, whole[:, parts * channels :]
 
 
 def features_out(stream, query, mixed, columns):
@@ -194,9 +205,8 @@
     li_residue,
     doc_ids,
 ):
-    mr_piece = gather_weights(mr_inproj)
+    mr_piece, mr_columns = gather_layer_weights(mr_inproj, mr_outproj)
     li_piece = gather_weights(li_inproj)
-    mr_columns = outproj_columns(mr_outproj)
     li_columns = outproj_columns(li_outproj)
     query, product = features_in(tokens, mr_gain, mr_piece)
     mixed = short_mix(product, mr_filter, doc_ids)

time: 443 us -> 449 us (1.014)
    all_gather x2, waiting for transfers between devices: 0.04 us -> 62.7 us  [the longest x1 62.7 us: gather_layer_weights(): whole = lax.all_gather(joined, 'ctx', axis=0, tiled=True)]
    all_gather x2 -> x1, waiting for transfers between devices: 107 us -> 52.2 us  [gather_weights(): return lax.all_gather(inproj, 'ctx', axis=0, tiled=True)]
    all_gather x4, waiting for transfers between devices: 151 us -> 143 us  [gather_channels(): return lax.all_gather(pair, 'z', axis=1, tiled=True)]
  transfers between devices with their start and end apart: 12 -> 11, of which waited for: 9 -> 9; matrix products, arithmetic and copies ran while one was open for 15% -> 8% of each run, Pallas kernels for 2% -> 2%
where the time goes in v5:
time: 449 us; the launch traced here: 447 us
  waiting for transfers between devices  277 us (62%)
  blocking collectives  54.4 us (12%)
  other arithmetic  30.8 us (7%)
  local copies, waits for them, and re-layouts  27.1 us (6%)
  matrix products  19 us (4%)
  starting transfers between devices  14.4 us (3%)
  between operations  13.8 us (3%)
  Pallas kernels  8.29 us (2%)
    all_gather x4, waiting for transfers between devices, gather_channels(): return lax.all_gather(pair, 'z', axis=1, tiled=True)  143 us
    all_gather x1, waiting for transfers between devices, gather_layer_weights(): whole = lax.all_gather(joined, 'ctx', axis=0, tiled=True)  62.7 us
    all_gather x1, waiting for transfers between devices, gather_weights(): return lax.all_gather(inproj, 'ctx', axis=0, tiled=True)  52.2 us
    all_gather x4, blocking collectives, gather_channels(): pair = lax.all_gather(value, 'yh', axis=1, tiled=True)  36.7 us
    add x8, other arithmetic, tap_group(): running + jnp.where((source_docs == target_docs)[:, :, None], source, 0.0...  17.8 us
    all_gather x1, blocking collectives, long_mix(): gathered = lax.all_gather(ends, 'ctx', axis=0, tiled=False)  17.8 us
    ppermute x2, waiting for transfers between devices, swap_blocks(): return lax.ppermute(outproj, ('ctx',) + CH, pairs)  16.1 us
    dot_general x2, matrix products, features_in(): jnp.dot(normed, flat, preferred_element_type=jnp.float32)  11.9 us
  transfers between devices with their start and end apart: 11, of which 9 were waited for; matrix products, arithmetic and copies ran while one was open for 8% of the time, Pallas kernels for 2%

profile of v5, /device:TPU:4, one launch (start us, length us, event | category | flops | bytes accessed | tf_op | source)
XLA Modules:
  0.0 447.3 jit_solution(532834378121110361)
XLA Ops:
  6.5 10.8 %all_gather.39 = bf16[384,512]{1,0:T(8,128)(2,1)} all-gather(bf16[384,256]{1,0:T(8,128)(2,1)} %param.15), channel_id=1, replica_groups=mesh['ctx'=16,'z'=8,'yh'=2] {'yh'}, dimensions={1}, use_global_device_ids=true | all-gather | bytes 589824 | tf_op jit(solution)/shard_map/all_gather | solution.py:28
  18.4 5.1 %collective-permute-start = (bf16[256,256]{0,1:T(8,128)(2,1)S(1)}, bf16[256,256]{0,1:T(8,128)(2,1)S(1)}, u32[]{:S(2)}, u32[]{:S(2)}) collective-permute-start(bf16[256,256]{0,1:T(8,128)(2,1)S(1)} %copy.30), channel_id=1, source_target_pairs={{0,0},{1,16},{2,32},{3,48},{4,64},{5,80},{6,96},{7,112},{8,128},{9... | collective-permute-start | bytes 393224 | tf_op jit(solution)/shard_map/ppermute | solution.py:55
  23.6 1.2 copy.29
  24.7 9.3 %collective-permute-done = bf16[256,256]{0,1:T(8,128)(2,1)S(1)} collective-permute-done((bf16[256,256]{0,1:T(8,128)(2,1)S(1)}, bf16[256,256]{0,1:T(8,128)(2,1)S(1)}, u32[]{:S(2)}, u32[]{:S(2)}) %collective-permute-start) | collective-permute-done | bytes 131104 | tf_op jit(solution)/shard_map/ppermute | solution.py:55
  36.0 3.9 gather_fusion
  40.0 25.6 %all-gather.9.cloned.1.call-done = bf16[384,4096]{1,0:T(8,128)(2,1)} async-done(((bf16[384,512]{1,0:T(8,128)(2,1)}), bf16[384,4096]{1,0:T(8,128)(2,1)}) %all-gather.9.cloned.1.call-update) | async-done | bytes 3145744 | tf_op jit(solution)/shard_map/all_gather | solution.py:29
  65.7 2.6 fusion.31
  68.3 62.7 %all-gather.11.cloned.1.call-done = bf16[4096,1024]{0,1:T(8,128)(2,1)} async-done(((bf16[256,1024]{0,1:T(8,128)(2,1)}), bf16[4096,1024]{0,1:T(8,128)(2,1)}) %all-gather.11.cloned.1.call-update) | async-done | bytes 8388624 | tf_op jit(solution)/shard_map/all_gather | solution.py:65
  130.9 6.4 %fusion.59 = bf16[384,768]{1,0:T(8,128)(2,1)S(1)} fusion(bf16[4096,1024]{0,1:T(8,128)(2,1)} %all-gather.11.cloned.1.call-done, bf16[384,4096]{1,0:T(8,128)(2,1)} %all-gather.9.cloned.1.call-done, f32[4096]{0:T(1024)S(1)} %copy-done.8, f32[384]{0:T(512)S(1)} %add_rsqrt_fusion.1), kind=kOutput, calls=%fused_computation.95 | convolution fusion | flops 2422505472 | bytes 10044928 | tf_op jit(solution)/shard_map/dot_general | solution.py:43
  137.5 3.4 collective-permute-start.2
  140.8 1.9 collective-permute-start.1
  142.8 3.6 collective-permute-done.1
  146.5 30.2 %while.17 = (s32[]{:T(128)}, f32[2,192,256]{2,1,0:T(8,128)S(1)}, s32[2,319]{1,0:T(2,128)S(1)}, s32[2,192]{1,0:T(2,128)S(1)}, f32[2,319,256]{2,1,0:T(8,128)S(1)},...) while((s32[]{:T(128)}, f32[2,192,256]{2,1,0:T(8,128)S(1)}, ...), condition=%wide.region_2.3_spmd.clone, body=%wide.region_1.2_spmd.clone.sunk | while | flops 4823171 | bytes 7167463 | solution.py:129
  147.0 1.1 constant_dynamic-slice_fusion.33
  148.1 2.2 fusion.78
  150.7 1.1 constant_dynamic-slice_fusion.33
  151.8 2.2 fusion.78
  154.5 1.1 constant_dynamic-slice_fusion.33
  155.6 2.2 fusion.78
  158.3 1.1 constant_dynamic-slice_fusion.33
  159.4 2.2 fusion.78
  162.1 1.1 constant_dynamic-slice_fusion.33
  163.1 2.2 fusion.78
  165.8 1.1 constant_dynamic-slice_fusion.33
  166.9 2.2 fusion.78
  170.7 2.2 fusion.78
  173.4 1.1 constant_dynamic-slice_fusion.33
  174.4 2.2 fusion.78
  176.8 8.1 %all_gather.42 = bf16[384,512]{1,0:T(8,128)(2,1)} all-gather(bf16[384,256]{1,0:T(8,128)(2,1)S(1)} %fusion.65), channel_id=1, replica_groups=mesh['ctx'=16,'z'=8,'yh'=2] {'yh'}, dimensions={1}, use_global_device_ids=true | all-gather | bytes 589824 | tf_op jit(solution)/shard_map/all_gather | solution.py:28
  184.9 2.5 copy.31
  187.4 43.1 %all-gather.13.cloned.1.call-done = bf16[384,4096]{1,0:T(8,128)(2,1)} async-done(((bf16[384,512]{1,0:T(8,128)(2,1)}), bf16[384,4096]{1,0:T(8,128)(2,1)}) %all-gather.13.cloned.1.call-update) | async-done | bytes 3145744 | tf_op jit(solution)/shard_map/all_gather | solution.py:29
  230.5 3.6 convert_reduce_fusion.1
  234.2 8.3 %all_gather.44 = bf16[384,512]{1,0:T(8,128)(2,1)} all-gather(bf16[384,256]{1,0:T(8,128)(2,1)S(1)} %add_convert_fusion.1), channel_id=1, replica_groups=mesh['ctx'=16,'z'=8,'yh'=2] {'yh'}, dimensions={1}, use_global_device_ids=true | all-gather | bytes 589824 | tf_op jit(solution)/shard_map/all_gather | solution.py:28
  243.7 3.8 collective-permute-start.3
  247.6 2.5 gather_fusion.3
  250.4 2.5 gather_fusion.4
  253.0 6.8 %collective-permute-done.3 = bf16[256,256]{1,0:T(8,128)(2,1)S(1)} collective-permute-done((bf16[256,256]{1,0:T(8,128)(2,1)S(1)}, bf16[256,256]{1,0:T(8,128)(2,1)S(1)}, u32[]{:S(2)}, u32[]{:S(2)}) %collective-permute-start.3) | collective-permute-done | bytes 131104 | tf_op jit(solution)/shard_map/ppermute | solution.py:55
  262.8 27.1 %all-gather.15.cloned.1.call-done = bf16[384,4096]{1,0:T(8,128)(2,1)} async-done(((bf16[384,512]{1,0:T(8,128)(2,1)}), bf16[384,4096]{1,0:T(8,128)(2,1)}) %all-gather.15.cloned.1.call-update) | async-done | bytes 3145744 | tf_op jit(solution)/shard_map/all_gather | solution.py:29
  289.9 2.7 fusion.34
  292.6 52.2 %all-gather.17.cloned.1.call-done = bf16[4096,3,256]{0,2,1:T(8,128)(2,1)} async-done(((bf16[256,3,256]{0,2,1:T(8,128)(2,1)}), bf16[4096,3,256]{0,2,1:T(8,128)(2,1)}) %all-gather.17.cloned.1.call-update) | async-done | bytes 6291472 | tf_op jit(solution)/shard_map/all_gather | solution.py:33
  344.8 5.5 %fusion.56 = bf16[384,768]{1,0:T(8,128)(2,1)S(1)} fusion(bf16[4096,768]{0,1:T(8,128)(2,1)} %bitcast.127, bf16[384,4096]{1,0:T(8,128)(2,1)S(1)} %copy-done.1, f32[4096]{0:T(1024)S(1)} %copy-done.9, f32[384]{0:T(512)S(1)} %add_rsqrt_fusion), kind=kOutput, calls=%fused_computation.94 | convolution fusion | flops 2422505472 | bytes 10044928 | tf_op jit(solution)/shard_map/dot_general | solution.py:43
  351.8 4.1 shard_map.109
  356.0 17.8 %all-gather = f32[32,16,256]{2,1,0:T(8,128)S(1)} all-gather(f32[2,16,256]{2,1,0:T(8,128)} %get-tuple-element.240), channel_id=2, replica_groups=mesh['ctx'=16,'z'=8,'yh'=2] {'ctx'}, dimensions={0}, use_global_device_ids=true | all-gather | bytes 557056 | tf_op jit(solution)/shard_map/all_gather | solution.py:180
  374.7 4.1 shard_map.110
  378.9 1.1 fusion.64
  380.0 9.4 %all_gather.49 = bf16[384,512]{1,0:T(8,128)(2,1)} all-gather(bf16[384,256]{1,0:T(8,128)(2,1)S(1)} %fusion.64), channel_id=1, replica_groups=mesh['ctx'=16,'z'=8,'yh'=2] {'yh'}, dimensions={1}, use_global_device_ids=true | all-gather | bytes 589824 | tf_op jit(solution)/shard_map/all_gather | solution.py:28
  389.5 46.7 %all-gather.19.cloned.1.call-done = bf16[384,4096]{1,0:T(8,128)(2,1)} async-done(((bf16[384,512]{1,0:T(8,128)(2,1)}), bf16[384,4096]{1,0:T(8,128)(2,1)}) %all-gather.19.cloned.1.call-update) | async-done | bytes 3145744 | tf_op jit(solution)/shard_map/all_gather | solution.py:29
  436.2 3.5 convert_reduce_fusion
  (97 shorter events, 13.9 us)
Async XLA Ops:
  6.5 28.5 %copy-start = (s32[6144]{0:T(1024)S(1)}, s32[6144]{0:T(1024)}, u32[]{:S(2)}) copy-start(s32[6144]{0:T(1024)} %param.25) | copy-start | bytes 73732
  6.5 59.2 %all-gather.9.cloned.1.call-start = ((), (), s32[]{:S(2)}) async-start(), calls=%async_computation | async-start | bytes 3538944 | tf_op jit(solution)/shard_map/all_gather | solution.py:29
  17.4 113.6 %all-gather.11.cloned.1.call-start = ((), (), s32[]{:S(2)}) async-start(), calls=%async_computation.1 | async-start | bytes 8912896 | tf_op jit(solution)/shard_map/all_gather | solution.py:65
  18.4 15.6 %collective-permute-start = (bf16[256,256]{0,1:T(8,128)(2,1)S(1)}, bf16[256,256]{0,1:T(8,128)(2,1)S(1)}, u32[]{:S(2)}, u32[]{:S(2)}) collective-permute-start(bf16[256,256]{0,1:T(8,128)(2,1)S(1)} %copy.30), channel_id=1, source_target_pairs={{0,0},{1,16},{2,32},{3,48},{4,64},{5,80},{6,96},{7,112},{8,128},{9... | collective-permute-start | bytes 393224 | tf_op jit(solution)/shard_map/ppermute | solution.py:55
  34.9 195.6 %all-gather.13.cloned.1.call-start = ((), (), s32[]{:S(2)}) async-start(), calls=%async_computation.2 | async-start | bytes 3538944 | tf_op jit(solution)/shard_map/all_gather | solution.py:29
  35.9 95.0 %copy-start.8 = (f32[4096]{0:T(1024)S(1)}, f32[4096]{0:T(1024)}, u32[]{:S(2)}) copy-start(f32[4096]{0:T(1024)} %param.16) | copy-start | bytes 49156
  137.5 5.3 %collective-permute-start.2 = (bf16[127,256]{1,0:T(8,128)(2,1)S(1)}, bf16[127,256]{1,0:T(8,128)(2,1)S(1)}, u32[]{:S(2)}, u32[]{:S(2)}) collective-permute-start(bf16[127,256]{1,0:T(8,128)(2,1)S(1)} %get-tuple-element.312), channel_id=1, source_target_pairs={{16,0},{32,16},{48,32},{64,48},{80,64},{96,80},{112,96},{128,112},... | collective-permute-start | bytes 195080 | tf_op jit(solution)/shard_map/ppermute | solution.py:19
  140.8 5.6 %collective-permute-start.1 = (bf16[127,256]{1,0:T(8,128)(2,1)S(1)}, bf16[127,256]{1,0:T(8,128)(2,1)S(1)}, u32[]{:S(2)}, u32[]{:S(2)}) collective-permute-start(bf16[127,256]{1,0:T(8,128)(2,1)S(1)} %get-tuple-element.311), channel_id=1, source_target_pairs={{0,16},{16,32},{32,48},{48,64},{64,80},{80,96},{96,112},{112,128},... | collective-permute-start | bytes 195080 | tf_op jit(solution)/shard_map/ppermute | solution.py:18
  176.7 8.2 %slice-start = ((bf16[4096,1024]{0,1:T(8,128)(2,1)}), bf16[4096,256]{0,1:T(8,128)(2,1)S(1)}, s32[]{:S(2)}) async-start(bf16[4096,1024]{0,1:T(8,128)(2,1)} %all-gather.11.cloned.1.call-done), calls=%async_computation.7 | async-start | bytes 4194304 | tf_op jit(solution)/shard_map/slice | solution.py:67
  184.9 105.0 %all-gather.15.cloned.1.call-start = ((), (), s32[]{:S(2)}) async-start(), calls=%async_computation.3 | async-start | bytes 3538944 | tf_op jit(solution)/shard_map/all_gather | solution.py:29
  230.5 3.6 copy-start.2
  230.5 12.1 %copy-start.4 = (bf16[256,3,256]{2,0,1:T(8,128)(2,1)S(1)}, bf16[256,3,256]{2,0,1:T(8,128)(2,1)}, u32[]{:S(2)}) copy-start(bf16[256,3,256]{2,0,1:T(8,128)(2,1)} %param.21) | copy-start | bytes 1179652
  230.5 13.1 %copy-start.7 = (bf16[256,256]{1,0:T(8,128)(2,1)S(1)}, bf16[256,256]{1,0:T(8,128)(2,1)}, u32[]{:S(2)}) copy-start(bf16[256,256]{1,0:T(8,128)(2,1)} %param.22) | copy-start | bytes 393220
  242.6 19.5 %copy-start.6 = (f32[16,256]{1,0:T(8,128)S(1)}, f32[16,256]{1,0:T(8,128)}, u32[]{:S(2)}) copy-start(f32[16,256]{1,0:T(8,128)} %param.23) | copy-start | bytes 49156
  242.6 102.2 %all-gather.17.cloned.1.call-start = ((), (), s32[]{:S(2)}) async-start(), calls=%async_computation.4 | async-start | bytes 6684672 | tf_op jit(solution)/shard_map/all_gather | solution.py:33
  243.6 145.8 %all-gather.21.cloned.1.call-start = ((), (), s32[]{:S(2)}) async-start(), calls=%async_computation.6 | async-start | bytes 2228224 | tf_op jit(solution)/shard_map/all_gather | solution.py:59
  243.7 16.1 %collective-permute-start.3 = (bf16[256,256]{1,0:T(8,128)(2,1)S(1)}, bf16[256,256]{1,0:T(8,128)(2,1)S(1)}, u32[]{:S(2)}, u32[]{:S(2)}) collective-permute-start(bf16[256,256]{1,0:T(8,128)(2,1)S(1)} %copy-done.7), channel_id=1, source_target_pairs={{0,0},{1,16},{2,32},{3,48},{4,64},{5,80},{6,96},{7,112},{8,128},{9... | collective-permute-start | bytes 393224 | tf_op jit(solution)/shard_map/ppermute | solution.py:55
  250.2 94.6 %copy-start.9 = (f32[4096]{0:T(1024)S(1)}, f32[4096]{0:T(1024)}, u32[]{:S(2)}) copy-start(f32[4096]{0:T(1024)} %param.20) | copy-start | bytes 49156
  259.8 0.7 copy-start.5
  260.5 175.7 %all-gather.19.cloned.1.call-start = ((), (), s32[]{:S(2)}) async-start(), calls=%async_computation.5 | async-start | bytes 3538944 | tf_op jit(solution)/shard_map/all_gather | solution.py:29
  289.9 54.9 %copy-start.1 = (bf16[384,4096]{1,0:T(8,128)(2,1)S(1)}, bf16[384,4096]{1,0:T(8,128)(2,1)}, u32[]{:S(2)}) copy-start(bf16[384,4096]{1,0:T(8,128)(2,1)} %all-gather.15.cloned.1.call-done) | copy-start | bytes 9437188
  350.3 1.0 copy-start.3
Sparse Core Ops, SparseCore 0:
  17.5 48.1 all-gather.8
  67.5 63.4 all-gather.10
  185.0 45.5 all-gather.12
  242.7 47.1 all-gather.14
  291.5 53.2 all-gather.16
  346.5 37.3 all-gather.20
  389.6 46.5 all-gather.18

commit v6 on v5

--- a/solution.py
+++ b/solution.py
@@ -76,8 +76,8 @@
         "tgk,gkj->gtj",
         whole.reshape(rows, groups, width),
         columns.reshape(groups, width, columns.shape[1]),
-        preferred_element_type=jnp.float32,
-    ).astype(jnp.bfloat16)
+        preferred_element_type=jnp.bfloat16,
+    )
     summed = jnp.sum(parts.astype(jnp.float32), axis=0)
     return (stream.astype(jnp.float32) + summed).astype(jnp.bfloat16)
 
@@ -166,19 +166,12 @@
     )(flags, values, factor, init, residue)
 
 
-def long_mix(product, li_decay, li_residue, doc_ids):
-    shard_rows, channels = product.shape
+def li_tables(doc_ids, li_decay, shard_rows):
     ctx_count, _, span_rows, span_starts, positions = span_layout(shard_rows)
-    modes = li_decay.shape[0]
-    own_docs = jnp.take(doc_ids, positions)
-    prior_docs = jnp.take(doc_ids, jnp.clip(positions - 1, 0, None))
+    own_docs = jnp.stack([lax.dynamic_slice_in_dim(doc_ids, start, span_rows) for start in span_starts])
+    padded = jnp.concatenate([doc_ids[:1], doc_ids])
+    prior_docs = jnp.stack([lax.dynamic_slice_in_dim(padded, start, span_rows) for start in span_starts])
     flags = ((positions > 0) & (own_docs == prior_docs)).astype(jnp.float32).reshape(-1)
-    factor = jnp.exp(-li_decay)
-    values = product.reshape(2, span_rows, channels).astype(jnp.float32)
-    zeros = jnp.zeros((2, modes, channels), jnp.float32)
-    _, ends = run_scan(flags, values, factor, zeros, li_residue)
-    gathered = lax.all_gather(ends, "ctx", axis=0, tiled=False)
-    block_ends = jnp.concatenate([gathered[:, 0], gathered[::-1, 1]], 0)
     block_count = 2 * ctx_count
     blocks = jnp.arange(block_count)
     end_docs = jnp.take(doc_ids, (blocks + 1) * span_rows - 1)
@@ -187,6 +180,20 @@
     linked = (blocks[None, :] < targets[:, None]) & (end_docs[None, :] == entry_docs[:, None])
     distance = jnp.where(linked, (targets[:, None] - blocks[None, :] - 1) * span_rows, 0).astype(jnp.float32)
     weights = jnp.exp(-li_decay[None, None] * distance[:, :, None, None]) * linked.astype(jnp.float32)[:, :, None, None]
+    return flags, weights
+
+
+def long_mix(product, li_decay, li_residue, tables):
+    flags, weights = tables
+    shard_rows, channels = product.shape
+    span_rows = shard_rows // 2
+    modes = li_decay.shape[0]
+    factor = jnp.exp(-li_decay)
+    values = product.reshape(2, span_rows, channels).astype(jnp.float32)
+    zeros = jnp.zeros((2, modes, channels), jnp.float32)
+    _, ends = run_scan(flags, values, factor, zeros, li_residue)
+    gathered = lax.all_gather(ends, "ctx", axis=0, tiled=False)
+    block_ends = jnp.concatenate([gathered[:, 0], gathered[::-1, 1]], 0)
     entry = jnp.sum(weights * block_ends[None], axis=1)
     mixed, _ = run_scan(flags, values, factor, entry, li_residue)
     return mixed.reshape(shard_rows, channels)
@@ -207,12 +214,13 @@
 ):
     mr_piece, mr_columns = gather_layer_weights(mr_inproj, mr_outproj)
     li_piece = gather_weights(li_inproj)
+    tables = li_tables(doc_ids, li_decay, tokens.shape[0])
     li_columns = outproj_columns(li_outproj)
     query, product = features_in(tokens, mr_gain, mr_piece)
     mixed = short_mix(product, mr_filter, doc_ids)
     stream = features_out(tokens, query, mixed, mr_columns)
     query, product = features_in(stream, li_gain, li_piece)
-    return features_out(stream, query, long_mix(product, li_decay, li_residue, doc_ids), li_columns)
+    return features_out(stream, query, long_mix(product, li_decay, li_residue, tables), li_columns)
 
 
 def solution(mesh):

time: 449 us -> 449 us (level)
  local copies, waits for them, and re-layouts: 27.1 us -> 22.3 us
    gather x6 -> x2, local copies, waits for them, and re-layouts: 6.55 us -> 1.33 us  [the longest x1 0.7 us: li_tables(): end_docs = jnp.take(doc_ids, (blocks + 1) * span_rows - 1)]
  transfers between devices with their start and end apart: 11 -> 11, of which waited for: 9 -> 9; matrix products, arithmetic and copies ran while one was open for 8% -> 7% of each run, Pallas kernels for 2% -> 2%
where the time goes in v6:
time: 449 us; the launch traced here: 447 us
  waiting for transfers between devices  281 us (63%)
  blocking collectives  54.5 us (12%)
  other arithmetic  31.5 us (7%)
  local copies, waits for them, and re-layouts  22.3 us (5%)
  matrix products  19 us (4%)
  starting transfers between devices  14.4 us (3%)
  between operations  13.8 us (3%)
  Pallas kernels  8.3 us (2%)
    all_gather x4, waiting for transfers between devices, gather_channels(): return lax.all_gather(pair, 'z', axis=1, tiled=True)  143 us
    all_gather x1, waiting for transfers between devices, gather_layer_weights(): whole = lax.all_gather(joined, 'ctx', axis=0, tiled=True)  62.7 us
    all_gather x1, waiting for transfers between devices, gather_weights(): return lax.all_gather(inproj, 'ctx', axis=0, tiled=True)  52.2 us
    all_gather x4, blocking collectives, gather_channels(): pair = lax.all_gather(value, 'yh', axis=1, tiled=True)  36.7 us
    ppermute x2, waiting for transfers between devices, swap_blocks(): return lax.ppermute(outproj, ('ctx',) + CH, pairs)  20.3 us
    add x8, other arithmetic, tap_group(): running + jnp.where((source_docs == target_docs)[:, :, None], source, 0.0...  17.9 us
    all_gather x1, blocking collectives, long_mix(): gathered = lax.all_gather(ends, 'ctx', axis=0, tiled=False)  17.9 us
    dot_general x2, matrix products, features_in(): jnp.dot(normed, flat, preferred_element_type=jnp.float32)  11.8 us
  transfers between devices with their start and end apart: 11, of which 9 were waited for; matrix products, arithmetic and copies ran while one was open for 7% of the time, Pallas kernels for 2%

profile of v6, /device:TPU:4, one launch (start us, length us, event | category | flops | bytes accessed | tf_op | source)
XLA Modules:
  0.0 447.5 jit_solution(9230522059204691830)
XLA Ops:
  6.5 10.8 %all_gather.39 = bf16[384,512]{1,0:T(8,128)(2,1)} all-gather(bf16[384,256]{1,0:T(8,128)(2,1)} %param.13), channel_id=1, replica_groups=mesh['ctx'=16,'z'=8,'yh'=2] {'yh'}, dimensions={1}, use_global_device_ids=true | all-gather | bytes 589824 | tf_op jit(solution)/shard_map/all_gather | solution.py:28
  17.4 1.0 copy.30
  18.4 5.1 %collective-permute-start = (bf16[256,256]{0,1:T(8,128)(2,1)S(1)}, bf16[256,256]{0,1:T(8,128)(2,1)S(1)}, u32[]{:S(2)}, u32[]{:S(2)}) collective-permute-start(bf16[256,256]{0,1:T(8,128)(2,1)S(1)} %copy.30), channel_id=1, source_target_pairs={{0,0},{1,16},{2,32},{3,48},{4,64},{5,80},{6,96},{7,112},{8,128},{9... | collective-permute-start | bytes 393224 | tf_op jit(solution)/shard_map/ppermute | solution.py:55
  23.6 1.2 copy.29
  24.7 9.3 %collective-permute-done = bf16[256,256]{0,1:T(8,128)(2,1)S(1)} collective-permute-done((bf16[256,256]{0,1:T(8,128)(2,1)S(1)}, bf16[256,256]{0,1:T(8,128)(2,1)S(1)}, u32[]{:S(2)}, u32[]{:S(2)}) %collective-permute-start) | collective-permute-done | bytes 131104 | tf_op jit(solution)/shard_map/ppermute | solution.py:55
  36.0 3.9 gather_fusion
  40.1 25.6 %all-gather.9.cloned.1.call-done = bf16[384,4096]{1,0:T(8,128)(2,1)} async-done(((bf16[384,512]{1,0:T(8,128)(2,1)}), bf16[384,4096]{1,0:T(8,128)(2,1)}) %all-gather.9.cloned.1.call-update) | async-done | bytes 3145744 | tf_op jit(solution)/shard_map/all_gather | solution.py:29
  65.7 2.6 fusion.31
  68.3 62.7 %all-gather.11.cloned.1.call-done = bf16[4096,1024]{0,1:T(8,128)(2,1)} async-done(((bf16[256,1024]{0,1:T(8,128)(2,1)}), bf16[4096,1024]{0,1:T(8,128)(2,1)}) %all-gather.11.cloned.1.call-update) | async-done | bytes 8388624 | tf_op jit(solution)/shard_map/all_gather | solution.py:65
  130.9 6.4 %fusion.55 = bf16[384,768]{1,0:T(8,128)(2,1)S(1)} fusion(bf16[4096,1024]{0,1:T(8,128)(2,1)} %all-gather.11.cloned.1.call-done, bf16[384,4096]{1,0:T(8,128)(2,1)} %all-gather.9.cloned.1.call-done, f32[4096]{0:T(1024)S(1)} %copy-done.8, f32[384]{0:T(512)S(1)} %add_rsqrt_fusion.1), kind=kOutput, calls=%fused_computation.93 | convolution fusion | flops 2422505472 | bytes 10044928 | tf_op jit(solution)/shard_map/dot_general | solution.py:43
  137.5 3.4 collective-permute-start.2
  140.8 1.9 collective-permute-start.1
  142.8 3.6 collective-permute-done.1
  146.5 30.3 %while.17 = (s32[]{:T(128)}, f32[2,192,256]{2,1,0:T(8,128)S(1)}, s32[2,319]{1,0:T(2,128)S(1)}, s32[2,192]{1,0:T(2,128)S(1)}, f32[2,319,256]{2,1,0:T(8,128)S(1)},...) while((s32[]{:T(128)}, f32[2,192,256]{2,1,0:T(8,128)S(1)}, ...), condition=%wide.region_2.3_spmd.clone, body=%wide.region_1.2_spmd.clone.sunk | while | flops 4823171 | bytes 7167463 | solution.py:129
  147.0 1.1 constant_dynamic-slice_fusion.33
  148.0 2.2 fusion.80
  150.7 1.1 constant_dynamic-slice_fusion.33
  151.8 2.2 fusion.80
  154.5 1.1 constant_dynamic-slice_fusion.33
  155.6 2.2 fusion.80
  158.3 1.1 constant_dynamic-slice_fusion.33
  159.4 2.2 fusion.80
  162.1 1.1 constant_dynamic-slice_fusion.33
  163.2 2.2 fusion.80
  165.9 1.1 constant_dynamic-slice_fusion.33
  167.0 2.2 fusion.80
  169.7 1.1 constant_dynamic-slice_fusion.33
  170.8 2.2 fusion.80
  173.5 1.1 constant_dynamic-slice_fusion.33
  174.5 2.2 fusion.80
  176.9 8.1 %all_gather.42 = bf16[384,512]{1,0:T(8,128)(2,1)} all-gather(bf16[384,256]{1,0:T(8,128)(2,1)S(1)} %fusion.65), channel_id=1, replica_groups=mesh['ctx'=16,'z'=8,'yh'=2] {'yh'}, dimensions={1}, use_global_device_ids=true | all-gather | bytes 589824 | tf_op jit(solution)/shard_map/all_gather | solution.py:28
  185.0 2.5 copy.31
  187.5 43.1 %all-gather.13.cloned.1.call-done = bf16[384,4096]{1,0:T(8,128)(2,1)} async-done(((bf16[384,512]{1,0:T(8,128)(2,1)}), bf16[384,4096]{1,0:T(8,128)(2,1)}) %all-gather.13.cloned.1.call-update) | async-done | bytes 3145744 | tf_op jit(solution)/shard_map/all_gather | solution.py:29
  230.7 3.6 convert_reduce_fusion.1
  234.4 8.3 %all_gather.44 = bf16[384,512]{1,0:T(8,128)(2,1)} all-gather(bf16[384,256]{1,0:T(8,128)(2,1)S(1)} %add_convert_fusion.1), channel_id=1, replica_groups=mesh['ctx'=16,'z'=8,'yh'=2] {'yh'}, dimensions={1}, use_global_device_ids=true | all-gather | bytes 589824 | tf_op jit(solution)/shard_map/all_gather | solution.py:28
  243.8 3.8 collective-permute-start.3
  248.9 11.0 %collective-permute-done.3 = bf16[256,256]{1,0:T(8,128)(2,1)S(1)} collective-permute-done((bf16[256,256]{1,0:T(8,128)(2,1)S(1)}, bf16[256,256]{1,0:T(8,128)(2,1)S(1)}, u32[]{:S(2)}, u32[]{:S(2)}) %collective-permute-start.3) | collective-permute-done | bytes 131104 | tf_op jit(solution)/shard_map/ppermute | solution.py:55
  262.9 27.1 %all-gather.15.cloned.1.call-done = bf16[384,4096]{1,0:T(8,128)(2,1)} async-done(((bf16[384,512]{1,0:T(8,128)(2,1)}), bf16[384,4096]{1,0:T(8,128)(2,1)}) %all-gather.15.cloned.1.call-update) | async-done | bytes 3145744 | tf_op jit(solution)/shard_map/all_gather | solution.py:29
  290.0 2.7 fusion.34
  292.8 52.2 %all-gather.17.cloned.1.call-done = bf16[4096,3,256]{0,2,1:T(8,128)(2,1)} async-done(((bf16[256,3,256]{0,2,1:T(8,128)(2,1)}), bf16[4096,3,256]{0,2,1:T(8,128)(2,1)}) %all-gather.17.cloned.1.call-update) | async-done | bytes 6291472 | tf_op jit(solution)/shard_map/all_gather | solution.py:33
  344.9 5.4 %fusion.52 = bf16[384,768]{1,0:T(8,128)(2,1)S(1)} fusion(bf16[4096,768]{0,1:T(8,128)(2,1)} %bitcast.135, bf16[384,4096]{1,0:T(8,128)(2,1)S(1)} %copy-done.1, f32[4096]{0:T(1024)S(1)} %copy-done.9, f32[384]{0:T(512)S(1)} %add_rsqrt_fusion), kind=kOutput, calls=%fused_computation.92 | convolution fusion | flops 2422505472 | bytes 10044928 | tf_op jit(solution)/shard_map/dot_general | solution.py:43
  351.9 4.1 shard_map.109
  356.1 17.9 %all-gather = f32[32,16,256]{2,1,0:T(8,128)S(1)} all-gather(f32[2,16,256]{2,1,0:T(8,128)} %get-tuple-element.239), channel_id=2, replica_groups=mesh['ctx'=16,'z'=8,'yh'=2] {'ctx'}, dimensions={0}, use_global_device_ids=true | all-gather | bytes 557056 | tf_op jit(solution)/shard_map/all_gather | solution.py:195
  375.0 4.2 shard_map.110
  379.1 1.1 fusion.64
  380.2 9.4 %all_gather.49 = bf16[384,512]{1,0:T(8,128)(2,1)} all-gather(bf16[384,256]{1,0:T(8,128)(2,1)S(1)} %fusion.64), channel_id=1, replica_groups=mesh['ctx'=16,'z'=8,'yh'=2] {'yh'}, dimensions={1}, use_global_device_ids=true | all-gather | bytes 589824 | tf_op jit(solution)/shard_map/all_gather | solution.py:28
  389.7 46.6 %all-gather.19.cloned.1.call-done = bf16[384,4096]{1,0:T(8,128)(2,1)} async-done(((bf16[384,512]{1,0:T(8,128)(2,1)}), bf16[384,4096]{1,0:T(8,128)(2,1)}) %all-gather.19.cloned.1.call-update) | async-done | bytes 3145744 | tf_op jit(solution)/shard_map/all_gather | solution.py:29
  436.3 3.5 convert_reduce_fusion
  (90 shorter events, 12.7 us)
Async XLA Ops:
  6.5 28.5 %copy-start = (s32[6144]{0:T(1024)S(1)}, s32[6144]{0:T(1024)}, u32[]{:S(2)}) copy-start(s32[6144]{0:T(1024)} %param.23) | copy-start | bytes 73732
  6.5 59.2 %all-gather.9.cloned.1.call-start = ((), (), s32[]{:S(2)}) async-start(), calls=%async_computation | async-start | bytes 3538944 | tf_op jit(solution)/shard_map/all_gather | solution.py:29
  17.4 113.6 %all-gather.11.cloned.1.call-start = ((), (), s32[]{:S(2)}) async-start(), calls=%async_computation.1 | async-start | bytes 8912896 | tf_op jit(solution)/shard_map/all_gather | solution.py:65
  18.4 15.6 %collective-permute-start = (bf16[256,256]{0,1:T(8,128)(2,1)S(1)}, bf16[256,256]{0,1:T(8,128)(2,1)S(1)}, u32[]{:S(2)}, u32[]{:S(2)}) collective-permute-start(bf16[256,256]{0,1:T(8,128)(2,1)S(1)} %copy.30), channel_id=1, source_target_pairs={{0,0},{1,16},{2,32},{3,48},{4,64},{5,80},{6,96},{7,112},{8,128},{9... | collective-permute-start | bytes 393224 | tf_op jit(solution)/shard_map/ppermute | solution.py:55
  34.9 195.8 %all-gather.13.cloned.1.call-start = ((), (), s32[]{:S(2)}) async-start(), calls=%async_computation.2 | async-start | bytes 3538944 | tf_op jit(solution)/shard_map/all_gather | solution.py:29
  36.0 95.0 %copy-start.8 = (f32[4096]{0:T(1024)S(1)}, f32[4096]{0:T(1024)}, u32[]{:S(2)}) copy-start(f32[4096]{0:T(1024)} %param.14) | copy-start | bytes 49156
  137.5 5.3 %collective-permute-start.2 = (bf16[127,256]{1,0:T(8,128)(2,1)S(1)}, bf16[127,256]{1,0:T(8,128)(2,1)S(1)}, u32[]{:S(2)}, u32[]{:S(2)}) collective-permute-start(bf16[127,256]{1,0:T(8,128)(2,1)S(1)} %get-tuple-element.311), channel_id=1, source_target_pairs={{16,0},{32,16},{48,32},{64,48},{80,64},{96,80},{112,96},{128,112},... | collective-permute-start | bytes 195080 | tf_op jit(solution)/shard_map/ppermute | solution.py:19
  140.8 5.6 %collective-permute-start.1 = (bf16[127,256]{1,0:T(8,128)(2,1)S(1)}, bf16[127,256]{1,0:T(8,128)(2,1)S(1)}, u32[]{:S(2)}, u32[]{:S(2)}) collective-permute-start(bf16[127,256]{1,0:T(8,128)(2,1)S(1)} %get-tuple-element.310), channel_id=1, source_target_pairs={{0,16},{16,32},{32,48},{48,64},{64,80},{80,96},{96,112},{112,128},... | collective-permute-start | bytes 195080 | tf_op jit(solution)/shard_map/ppermute | solution.py:18
  176.8 8.2 %slice-start = ((bf16[4096,1024]{0,1:T(8,128)(2,1)}), bf16[4096,256]{0,1:T(8,128)(2,1)S(1)}, s32[]{:S(2)}) async-start(bf16[4096,1024]{0,1:T(8,128)(2,1)} %all-gather.11.cloned.1.call-done), calls=%async_computation.7 | async-start | bytes 4194304 | tf_op jit(solution)/shard_map/slice | solution.py:67
  185.0 105.0 %all-gather.15.cloned.1.call-start = ((), (), s32[]{:S(2)}) async-start(), calls=%async_computation.3 | async-start | bytes 3538944 | tf_op jit(solution)/shard_map/all_gather | solution.py:29
  230.7 3.6 copy-start.2
  230.7 12.1 %copy-start.4 = (bf16[256,3,256]{2,0,1:T(8,128)(2,1)S(1)}, bf16[256,3,256]{2,0,1:T(8,128)(2,1)}, u32[]{:S(2)}) copy-start(bf16[256,3,256]{2,0,1:T(8,128)(2,1)} %param.19) | copy-start | bytes 1179652
  230.7 13.1 %copy-start.7 = (bf16[256,256]{1,0:T(8,128)(2,1)S(1)}, bf16[256,256]{1,0:T(8,128)(2,1)}, u32[]{:S(2)}) copy-start(bf16[256,256]{1,0:T(8,128)(2,1)} %param.20) | copy-start | bytes 393220
  234.3 28.0 %copy-start.6 = (f32[16,256]{1,0:T(8,128)S(1)}, f32[16,256]{1,0:T(8,128)}, u32[]{:S(2)}) copy-start(f32[16,256]{1,0:T(8,128)} %param.21) | copy-start | bytes 49156
  234.3 110.6 %copy-start.9 = (f32[4096]{0:T(1024)S(1)}, f32[4096]{0:T(1024)}, u32[]{:S(2)}) copy-start(f32[4096]{0:T(1024)} %param.18) | copy-start | bytes 49156
  242.7 102.2 %all-gather.17.cloned.1.call-start = ((), (), s32[]{:S(2)}) async-start(), calls=%async_computation.4 | async-start | bytes 6684672 | tf_op jit(solution)/shard_map/all_gather | solution.py:33
  243.8 145.9 %all-gather.21.cloned.1.call-start = ((), (), s32[]{:S(2)}) async-start(), calls=%async_computation.6 | async-start | bytes 2228224 | tf_op jit(solution)/shard_map/all_gather | solution.py:59
  243.8 16.1 %collective-permute-start.3 = (bf16[256,256]{1,0:T(8,128)(2,1)S(1)}, bf16[256,256]{1,0:T(8,128)(2,1)S(1)}, u32[]{:S(2)}, u32[]{:S(2)}) collective-permute-start(bf16[256,256]{1,0:T(8,128)(2,1)S(1)} %copy-done.7), channel_id=1, source_target_pairs={{0,0},{1,16},{2,32},{3,48},{4,64},{5,80},{6,96},{7,112},{8,128},{9... | collective-permute-start | bytes 393224 | tf_op jit(solution)/shard_map/ppermute | solution.py:55
  259.9 0.7 copy-start.5
  260.6 175.8 %all-gather.19.cloned.1.call-start = ((), (), s32[]{:S(2)}) async-start(), calls=%async_computation.5 | async-start | bytes 3538944 | tf_op jit(solution)/shard_map/all_gather | solution.py:29
  290.0 54.9 %copy-start.1 = (bf16[384,4096]{1,0:T(8,128)(2,1)S(1)}, bf16[384,4096]{1,0:T(8,128)(2,1)}, u32[]{:S(2)}) copy-start(bf16[384,4096]{1,0:T(8,128)(2,1)} %all-gather.15.cloned.1.call-done) | copy-start | bytes 9437188
  350.4 1.0 copy-start.3
Sparse Core Ops, SparseCore 0:
  17.5 48.1 all-gather.8
  67.5 63.4 all-gather.10
  185.1 45.5 all-gather.12
  242.9 47.1 all-gather.14
  291.6 53.2 all-gather.16
  346.6 37.4 all-gather.20
  389.8 46.5 all-gather.18

commit v7 on v6

--- a/solution.py
+++ b/solution.py
@@ -136,15 +136,19 @@
     halves, span_rows, _ = x_ref.shape
     factor = factor_ref[...]
     residue = residue_ref[...]
+
+    def step(t, states):
+        updated = []
+        for half in range(halves):
+            kept = factor * flags_ref[half * span_rows + t]
+            state = kept * states[half] + x_ref[half, pl.ds(t, 1), :]
+            mixed_ref[half, pl.ds(t, 1), :] = jnp.sum(residue * state, axis=0, keepdims=True)
+            updated.append(state)
+        return tuple(updated)
+
+    ends = lax.fori_loop(0, span_rows, step, tuple(init_ref[half] for half in range(halves)), unroll=8)
     for half in range(halves):
-
-        def step(t, state):
-            kept = factor * flags_ref[half * span_rows + t]
-            state = kept * state + x_ref[half, pl.ds(t, 1), :]
-            mixed_ref[half, pl.ds(t, 1), :] = jnp.sum(residue * state, axis=0, keepdims=True)
-            return state
-
-        end_ref[half] = lax.fori_loop(0, span_rows, step, init_ref[half], unroll=8)
+        end_ref[half] = ends[half]
 
 
 def run_scan(flags, values, factor, init, residue):

time: 449 us -> 448 us (level)
  no operation moved by 1% of the time
where the time goes in v7:
time: 448 us; the launch traced here: 447 us
  waiting for transfers between devices  281 us (63%)
  blocking collectives  55.3 us (12%)
  other arithmetic  31.5 us (7%)
  local copies, waits for them, and re-layouts  22.3 us (5%)
  matrix products  19 us (4%)
  starting transfers between devices  14.4 us (3%)
  between operations  13.8 us (3%)
  Pallas kernels  7.6 us (2%)
    all_gather x4, waiting for transfers between devices, gather_channels(): return lax.all_gather(pair, 'z', axis=1, tiled=True)  142 us
    all_gather x1, waiting for transfers between devices, gather_layer_weights(): whole = lax.all_gather(joined, 'ctx', axis=0, tiled=True)  62.7 us
    all_gather x1, waiting for transfers between devices, gather_weights(): return lax.all_gather(inproj, 'ctx', axis=0, tiled=True)  52.2 us
    all_gather x4, blocking collectives, gather_channels(): pair = lax.all_gather(value, 'yh', axis=1, tiled=True)  36.7 us
    ppermute x2, waiting for transfers between devices, swap_blocks(): return lax.ppermute(outproj, ('ctx',) + CH, pairs)  20.3 us
    all_gather x1, blocking collectives, long_mix(): gathered = lax.all_gather(ends, 'ctx', axis=0, tiled=False)  18.7 us
    add x8, other arithmetic, tap_group(): running + jnp.where((source_docs == target_docs)[:, :, None], source, 0.0...  17.9 us
    dot_general x2, matrix products, features_in(): jnp.dot(normed, flat, preferred_element_type=jnp.float32)  11.8 us
  transfers between devices with their start and end apart: 11, of which 9 were waited for; matrix products, arithmetic and copies ran while one was open for 7% of the time, Pallas kernels for 2%

profile of v7, /device:TPU:4, one launch (start us, length us, event | category | flops | bytes accessed | tf_op | source)
XLA Modules:
  0.0 446.8 jit_solution(3080084125058022123)
XLA Ops:
  6.5 10.8 %all_gather.39 = bf16[384,512]{1,0:T(8,128)(2,1)} all-gather(bf16[384,256]{1,0:T(8,128)(2,1)} %param.13), channel_id=1, replica_groups=mesh['ctx'=16,'z'=8,'yh'=2] {'yh'}, dimensions={1}, use_global_device_ids=true | all-gather | bytes 589824 | tf_op jit(solution)/shard_map/all_gather | solution.py:28
  17.4 1.0 copy.30
  18.4 5.1 %collective-permute-start = (bf16[256,256]{0,1:T(8,128)(2,1)S(1)}, bf16[256,256]{0,1:T(8,128)(2,1)S(1)}, u32[]{:S(2)}, u32[]{:S(2)}) collective-permute-start(bf16[256,256]{0,1:T(8,128)(2,1)S(1)} %copy.30), channel_id=1, source_target_pairs={{0,0},{1,16},{2,32},{3,48},{4,64},{5,80},{6,96},{7,112},{8,128},{9... | collective-permute-start | bytes 393224 | tf_op jit(solution)/shard_map/ppermute | solution.py:55
  23.6 1.2 copy.29
  24.7 9.3 %collective-permute-done = bf16[256,256]{0,1:T(8,128)(2,1)S(1)} collective-permute-done((bf16[256,256]{0,1:T(8,128)(2,1)S(1)}, bf16[256,256]{0,1:T(8,128)(2,1)S(1)}, u32[]{:S(2)}, u32[]{:S(2)}) %collective-permute-start) | collective-permute-done | bytes 131104 | tf_op jit(solution)/shard_map/ppermute | solution.py:55
  36.0 3.9 gather_fusion
  40.1 25.6 %all-gather.9.cloned.1.call-done = bf16[384,4096]{1,0:T(8,128)(2,1)} async-done(((bf16[384,512]{1,0:T(8,128)(2,1)}), bf16[384,4096]{1,0:T(8,128)(2,1)}) %all-gather.9.cloned.1.call-update) | async-done | bytes 3145744 | tf_op jit(solution)/shard_map/all_gather | solution.py:29
  65.7 2.6 fusion.31
  68.3 62.7 %all-gather.11.cloned.1.call-done = bf16[4096,1024]{0,1:T(8,128)(2,1)} async-done(((bf16[256,1024]{0,1:T(8,128)(2,1)}), bf16[4096,1024]{0,1:T(8,128)(2,1)}) %all-gather.11.cloned.1.call-update) | async-done | bytes 8388624 | tf_op jit(solution)/shard_map/all_gather | solution.py:65
  130.9 6.4 %fusion.55 = bf16[384,768]{1,0:T(8,128)(2,1)S(1)} fusion(bf16[4096,1024]{0,1:T(8,128)(2,1)} %all-gather.11.cloned.1.call-done, bf16[384,4096]{1,0:T(8,128)(2,1)} %all-gather.9.cloned.1.call-done, f32[4096]{0:T(1024)S(1)} %copy-done.8, f32[384]{0:T(512)S(1)} %add_rsqrt_fusion.1), kind=kOutput, calls=%fused_computation.93 | convolution fusion | flops 2422505472 | bytes 10044928 | tf_op jit(solution)/shard_map/dot_general | solution.py:43
  137.5 3.4 collective-permute-start.2
  140.8 1.9 collective-permute-start.1
  142.8 3.6 collective-permute-done.1
  146.5 30.3 %while.17 = (s32[]{:T(128)}, f32[2,192,256]{2,1,0:T(8,128)S(1)}, s32[2,319]{1,0:T(2,128)S(1)}, s32[2,192]{1,0:T(2,128)S(1)}, f32[2,319,256]{2,1,0:T(8,128)S(1)},...) while((s32[]{:T(128)}, f32[2,192,256]{2,1,0:T(8,128)S(1)}, ...), condition=%wide.region_2.3_spmd.clone, body=%wide.region_1.2_spmd.clone.sunk | while | flops 4823171 | bytes 7167463 | solution.py:129
  147.0 1.1 constant_dynamic-slice_fusion.33
  148.0 2.2 fusion.80
  150.7 1.1 constant_dynamic-slice_fusion.33
  151.8 2.2 fusion.80
  154.5 1.1 constant_dynamic-slice_fusion.33
  155.6 2.2 fusion.80
  158.3 1.1 constant_dynamic-slice_fusion.33
  159.4 2.2 fusion.80
  162.1 1.1 constant_dynamic-slice_fusion.33
  163.2 2.2 fusion.80
  165.9 1.1 constant_dynamic-slice_fusion.33
  167.0 2.2 fusion.80
  169.7 1.1 constant_dynamic-slice_fusion.33
  170.8 2.2 fusion.80
  173.5 1.1 constant_dynamic-slice_fusion.33
  174.5 2.2 fusion.80
  176.9 8.1 %all_gather.42 = bf16[384,512]{1,0:T(8,128)(2,1)} all-gather(bf16[384,256]{1,0:T(8,128)(2,1)S(1)} %fusion.65), channel_id=1, replica_groups=mesh['ctx'=16,'z'=8,'yh'=2] {'yh'}, dimensions={1}, use_global_device_ids=true | all-gather | bytes 589824 | tf_op jit(solution)/shard_map/all_gather | solution.py:28
  185.0 2.5 copy.31
  187.5 43.1 %all-gather.13.cloned.1.call-done = bf16[384,4096]{1,0:T(8,128)(2,1)} async-done(((bf16[384,512]{1,0:T(8,128)(2,1)}), bf16[384,4096]{1,0:T(8,128)(2,1)}) %all-gather.13.cloned.1.call-update) | async-done | bytes 3145744 | tf_op jit(solution)/shard_map/all_gather | solution.py:29
  230.7 3.6 convert_reduce_fusion.1
  234.4 8.3 %all_gather.44 = bf16[384,512]{1,0:T(8,128)(2,1)} all-gather(bf16[384,256]{1,0:T(8,128)(2,1)S(1)} %add_convert_fusion.1), channel_id=1, replica_groups=mesh['ctx'=16,'z'=8,'yh'=2] {'yh'}, dimensions={1}, use_global_device_ids=true | all-gather | bytes 589824 | tf_op jit(solution)/shard_map/all_gather | solution.py:28
  243.8 3.8 collective-permute-start.3
  248.9 11.0 %collective-permute-done.3 = bf16[256,256]{1,0:T(8,128)(2,1)S(1)} collective-permute-done((bf16[256,256]{1,0:T(8,128)(2,1)S(1)}, bf16[256,256]{1,0:T(8,128)(2,1)S(1)}, u32[]{:S(2)}, u32[]{:S(2)}) %collective-permute-start.3) | collective-permute-done | bytes 131104 | tf_op jit(solution)/shard_map/ppermute | solution.py:55
  262.9 27.1 %all-gather.15.cloned.1.call-done = bf16[384,4096]{1,0:T(8,128)(2,1)} async-done(((bf16[384,512]{1,0:T(8,128)(2,1)}), bf16[384,4096]{1,0:T(8,128)(2,1)}) %all-gather.15.cloned.1.call-update) | async-done | bytes 3145744 | tf_op jit(solution)/shard_map/all_gather | solution.py:29
  290.0 2.7 fusion.34
  292.8 52.2 %all-gather.17.cloned.1.call-done = bf16[4096,3,256]{0,2,1:T(8,128)(2,1)} async-done(((bf16[256,3,256]{0,2,1:T(8,128)(2,1)}), bf16[4096,3,256]{0,2,1:T(8,128)(2,1)}) %all-gather.17.cloned.1.call-update) | async-done | bytes 6291472 | tf_op jit(solution)/shard_map/all_gather | solution.py:33
  344.9 5.4 %fusion.52 = bf16[384,768]{1,0:T(8,128)(2,1)S(1)} fusion(bf16[4096,768]{0,1:T(8,128)(2,1)} %bitcast.135, bf16[384,4096]{1,0:T(8,128)(2,1)S(1)} %copy-done.1, f32[4096]{0:T(1024)S(1)} %copy-done.9, f32[384]{0:T(512)S(1)} %add_rsqrt_fusion), kind=kOutput, calls=%fused_computation.92 | convolution fusion | flops 2422505472 | bytes 10044928 | tf_op jit(solution)/shard_map/dot_general | solution.py:43
  351.9 3.8 shard_map.109
  355.7 18.7 %all-gather = f32[32,16,256]{2,1,0:T(8,128)S(1)} all-gather(f32[2,16,256]{2,1,0:T(8,128)} %get-tuple-element.239), channel_id=2, replica_groups=mesh['ctx'=16,'z'=8,'yh'=2] {'ctx'}, dimensions={0}, use_global_device_ids=true | all-gather | bytes 557056 | tf_op jit(solution)/shard_map/all_gather | solution.py:199
  375.4 3.8 shard_map.110
  379.2 1.1 fusion.64
  380.3 9.4 %all_gather.49 = bf16[384,512]{1,0:T(8,128)(2,1)} all-gather(bf16[384,256]{1,0:T(8,128)(2,1)S(1)} %fusion.64), channel_id=1, replica_groups=mesh['ctx'=16,'z'=8,'yh'=2] {'yh'}, dimensions={1}, use_global_device_ids=true | all-gather | bytes 589824 | tf_op jit(solution)/shard_map/all_gather | solution.py:28
  389.8 45.9 %all-gather.19.cloned.1.call-done = bf16[384,4096]{1,0:T(8,128)(2,1)} async-done(((bf16[384,512]{1,0:T(8,128)(2,1)}), bf16[384,4096]{1,0:T(8,128)(2,1)}) %all-gather.19.cloned.1.call-update) | async-done | bytes 3145744 | tf_op jit(solution)/shard_map/all_gather | solution.py:29
  435.7 3.5 convert_reduce_fusion
  (90 shorter events, 12.7 us)
Async XLA Ops:
  6.5 28.5 %copy-start = (s32[6144]{0:T(1024)S(1)}, s32[6144]{0:T(1024)}, u32[]{:S(2)}) copy-start(s32[6144]{0:T(1024)} %param.23) | copy-start | bytes 73732
  6.5 59.2 %all-gather.9.cloned.1.call-start = ((), (), s32[]{:S(2)}) async-start(), calls=%async_computation | async-start | bytes 3538944 | tf_op jit(solution)/shard_map/all_gather | solution.py:29
  17.4 113.6 %all-gather.11.cloned.1.call-start = ((), (), s32[]{:S(2)}) async-start(), calls=%async_computation.1 | async-start | bytes 8912896 | tf_op jit(solution)/shard_map/all_gather | solution.py:65
  18.4 15.6 %collective-permute-start = (bf16[256,256]{0,1:T(8,128)(2,1)S(1)}, bf16[256,256]{0,1:T(8,128)(2,1)S(1)}, u32[]{:S(2)}, u32[]{:S(2)}) collective-permute-start(bf16[256,256]{0,1:T(8,128)(2,1)S(1)} %copy.30), channel_id=1, source_target_pairs={{0,0},{1,16},{2,32},{3,48},{4,64},{5,80},{6,96},{7,112},{8,128},{9... | collective-permute-start | bytes 393224 | tf_op jit(solution)/shard_map/ppermute | solution.py:55
  34.9 195.8 %all-gather.13.cloned.1.call-start = ((), (), s32[]{:S(2)}) async-start(), calls=%async_computation.2 | async-start | bytes 3538944 | tf_op jit(solution)/shard_map/all_gather | solution.py:29
  36.0 95.0 %copy-start.8 = (f32[4096]{0:T(1024)S(1)}, f32[4096]{0:T(1024)}, u32[]{:S(2)}) copy-start(f32[4096]{0:T(1024)} %param.14) | copy-start | bytes 49156
  137.5 5.3 %collective-permute-start.2 = (bf16[127,256]{1,0:T(8,128)(2,1)S(1)}, bf16[127,256]{1,0:T(8,128)(2,1)S(1)}, u32[]{:S(2)}, u32[]{:S(2)}) collective-permute-start(bf16[127,256]{1,0:T(8,128)(2,1)S(1)} %get-tuple-element.311), channel_id=1, source_target_pairs={{16,0},{32,16},{48,32},{64,48},{80,64},{96,80},{112,96},{128,112},... | collective-permute-start | bytes 195080 | tf_op jit(solution)/shard_map/ppermute | solution.py:19
  140.8 5.6 %collective-permute-start.1 = (bf16[127,256]{1,0:T(8,128)(2,1)S(1)}, bf16[127,256]{1,0:T(8,128)(2,1)S(1)}, u32[]{:S(2)}, u32[]{:S(2)}) collective-permute-start(bf16[127,256]{1,0:T(8,128)(2,1)S(1)} %get-tuple-element.310), channel_id=1, source_target_pairs={{0,16},{16,32},{32,48},{48,64},{64,80},{80,96},{96,112},{112,128},... | collective-permute-start | bytes 195080 | tf_op jit(solution)/shard_map/ppermute | solution.py:18
  176.8 8.2 %slice-start = ((bf16[4096,1024]{0,1:T(8,128)(2,1)}), bf16[4096,256]{0,1:T(8,128)(2,1)S(1)}, s32[]{:S(2)}) async-start(bf16[4096,1024]{0,1:T(8,128)(2,1)} %all-gather.11.cloned.1.call-done), calls=%async_computation.7 | async-start | bytes 4194304 | tf_op jit(solution)/shard_map/slice | solution.py:67
  185.0 105.0 %all-gather.15.cloned.1.call-start = ((), (), s32[]{:S(2)}) async-start(), calls=%async_computation.3 | async-start | bytes 3538944 | tf_op jit(solution)/shard_map/all_gather | solution.py:29
  230.7 3.6 copy-start.2
  230.7 12.1 %copy-start.4 = (bf16[256,3,256]{2,0,1:T(8,128)(2,1)S(1)}, bf16[256,3,256]{2,0,1:T(8,128)(2,1)}, u32[]{:S(2)}) copy-start(bf16[256,3,256]{2,0,1:T(8,128)(2,1)} %param.19) | copy-start | bytes 1179652
  230.7 13.1 %copy-start.7 = (bf16[256,256]{1,0:T(8,128)(2,1)S(1)}, bf16[256,256]{1,0:T(8,128)(2,1)}, u32[]{:S(2)}) copy-start(bf16[256,256]{1,0:T(8,128)(2,1)} %param.20) | copy-start | bytes 393220
  234.3 28.0 %copy-start.6 = (f32[16,256]{1,0:T(8,128)S(1)}, f32[16,256]{1,0:T(8,128)}, u32[]{:S(2)}) copy-start(f32[16,256]{1,0:T(8,128)} %param.21) | copy-start | bytes 49156
  234.3 110.6 %copy-start.9 = (f32[4096]{0:T(1024)S(1)}, f32[4096]{0:T(1024)}, u32[]{:S(2)}) copy-start(f32[4096]{0:T(1024)} %param.18) | copy-start | bytes 49156
  242.7 102.2 %all-gather.17.cloned.1.call-start = ((), (), s32[]{:S(2)}) async-start(), calls=%async_computation.4 | async-start | bytes 6684672 | tf_op jit(solution)/shard_map/all_gather | solution.py:33
  243.8 146.0 %all-gather.21.cloned.1.call-start = ((), (), s32[]{:S(2)}) async-start(), calls=%async_computation.6 | async-start | bytes 2228224 | tf_op jit(solution)/shard_map/all_gather | solution.py:59
  243.8 16.1 %collective-permute-start.3 = (bf16[256,256]{1,0:T(8,128)(2,1)S(1)}, bf16[256,256]{1,0:T(8,128)(2,1)S(1)}, u32[]{:S(2)}, u32[]{:S(2)}) collective-permute-start(bf16[256,256]{1,0:T(8,128)(2,1)S(1)} %copy-done.7), channel_id=1, source_target_pairs={{0,0},{1,16},{2,32},{3,48},{4,64},{5,80},{6,96},{7,112},{8,128},{9... | collective-permute-start | bytes 393224 | tf_op jit(solution)/shard_map/ppermute | solution.py:55
  259.9 0.7 copy-start.5
  260.6 175.1 %all-gather.19.cloned.1.call-start = ((), (), s32[]{:S(2)}) async-start(), calls=%async_computation.5 | async-start | bytes 3538944 | tf_op jit(solution)/shard_map/all_gather | solution.py:29
  290.0 54.9 %copy-start.1 = (bf16[384,4096]{1,0:T(8,128)(2,1)S(1)}, bf16[384,4096]{1,0:T(8,128)(2,1)}, u32[]{:S(2)}) copy-start(bf16[384,4096]{1,0:T(8,128)(2,1)} %all-gather.15.cloned.1.call-done) | copy-start | bytes 9437188
  350.4 1.0 copy-start.3
Sparse Core Ops, SparseCore 0:
  17.5 48.1 all-gather.8
  67.5 63.4 all-gather.10
  185.1 45.5 all-gather.12
  242.9 47.1 all-gather.14
  291.6 53.2 all-gather.16
  346.6 37.3 all-gather.20
  389.9 45.8 all-gather.18

commit v8 on v7

--- a/solution.py
+++ b/solution.py
@@ -67,19 +67,40 @@
     return piece, whole[:, parts * channels :]
 
 
+def outproj_kernel(whole_ref, columns_ref, stream_ref, out_ref):
+    width = columns_ref.shape[1]
+    groups = whole_ref.shape[1] // width
+    summed = None
+    for group in range(groups):
+        part = jnp.dot(
+            whole_ref[:, group * width : (group + 1) * width],
+            columns_ref[group * width : (group + 1) * width, :],
+            preferred_element_type=jnp.float32,
+        ).astype(jnp.bfloat16).astype(jnp.float32)
+        summed = part if summed is None else summed + part
+    out_ref[...] = (stream_ref[...].astype(jnp.float32) + summed).astype(jnp.bfloat16)
+
+
+def project_groups(whole, columns, stream):
+    vmem = pl.BlockSpec(memory_space=pltpu.VMEM)
+    rows, depth = whole.shape
+    return pl.pallas_call(
+        outproj_kernel,
+        out_shape=jax.ShapeDtypeStruct(stream.shape, jnp.bfloat16),
+        in_specs=[vmem, vmem, vmem],
+        out_specs=vmem,
+        cost_estimate=pl.CostEstimate(
+            flops=2 * rows * depth * columns.shape[1],
+            transcendentals=0,
+            bytes_accessed=2 * (whole.size + columns.size + 2 * stream.size),
+        ),
+    )(whole, columns, stream)
+
+
 def features_out(stream, query, mixed, columns):
     gated = (query.astype(jnp.float32) * mixed).astype(jnp.bfloat16)
     whole = gather_channels(gated)
-    rows, width = gated.shape
-    groups = whole.shape[1] // width
-    parts = jnp.einsum(
-        "tgk,gkj->gtj",
-        whole.reshape(rows, groups, width),
-        columns.reshape(groups, width, columns.shape[1]),
-        preferred_element_type=jnp.bfloat16,
-    )
-    summed = jnp.sum(parts.astype(jnp.float32), axis=0)
-    return (stream.astype(jnp.float32) + summed).astype(jnp.bfloat16)
+    return project_groups(whole, columns, stream)
 
 
 def span_layout(shard_rows):

time: 448 us -> 442 us (0.987)
  Pallas kernels: 7.6 us -> 16 us
  waiting for transfers between devices: 281 us -> 273 us
  matrix products: 19 us -> 12.8 us
    all_gather x1, waiting for transfers between devices: 62.7 us -> 54.1 us  [gather_layer_weights(): whole = lax.all_gather(joined, 'ctx', axis=0, tiled=True)]
    pallas_call x0 -> x2, Pallas kernels: none -> 8.37 us  [project_groups(): pl.pallas_call(outproj_kernel, out_shape=jax.ShapeDtypeStruct(stream.shap...]
    dot_general x2 -> x0, matrix products: 7.15 us -> none  [features_out(): jnp.einsum('tgk,gkj->gtj', whole.reshape(rows, groups, width), columns.re...]
where the time goes in v8:
time: 442 us; the launch traced here: 441 us
  waiting for transfers between devices  273 us (62%)
  blocking collectives  56.2 us (13%)
  other arithmetic  30.4 us (7%)
  local copies, waits for them, and re-layouts  22.8 us (5%)
  Pallas kernels  16 us (4%)
  starting transfers between devices  13.7 us (3%)
  between operations  13.7 us (3%)
  matrix products  12.8 us (3%)
    all_gather x4, waiting for transfers between devices, gather_channels(): return lax.all_gather(pair, 'z', axis=1, tiled=True)  143 us
    all_gather x1, waiting for transfers between devices, gather_layer_weights(): whole = lax.all_gather(joined, 'ctx', axis=0, tiled=True)  54.1 us
    all_gather x1, waiting for transfers between devices, gather_weights(): return lax.all_gather(inproj, 'ctx', axis=0, tiled=True)  51.9 us
    all_gather x4, blocking collectives, gather_channels(): pair = lax.all_gather(value, 'yh', axis=1, tiled=True)  38.3 us
    ppermute x2, waiting for transfers between devices, swap_blocks(): return lax.ppermute(outproj, ('ctx',) + CH, pairs)  20.8 us
    all_gather x1, blocking collectives, long_mix(): gathered = lax.all_gather(ends, 'ctx', axis=0, tiled=False)  17.9 us
    add x8, other arithmetic, tap_group(): running + jnp.where((source_docs == target_docs)[:, :, None], source, 0.0...  17.8 us
    dot_general x2, matrix products, features_in(): jnp.dot(normed, flat, preferred_element_type=jnp.float32)  12.8 us
  transfers between devices with their start and end apart: 11, of which 9 were waited for; matrix products, arithmetic and copies ran while one was open for 7% of the time, Pallas kernels for 2%

profile of v8, /device:TPU:4, one launch (start us, length us, event | category | flops | bytes accessed | tf_op | source)
XLA Modules:
  0.0 440.9 jit_solution(11639827054152073647)
XLA Ops:
  6.5 10.8 %all_gather.39 = bf16[384,512]{1,0:T(8,128)(2,1)} all-gather(bf16[384,256]{1,0:T(8,128)(2,1)} %stream_ref.1), channel_id=1, replica_groups=mesh['ctx'=16,'z'=8,'yh'=2] {'yh'}, dimensions={1}, use_global_device_ids=true | all-gather | bytes 589824 | tf_op jit(solution)/shard_map/all_gather | solution.py:28
  17.5 5.1 %collective-permute-start = (bf16[256,256]{1,0:T(8,128)(2,1)}, bf16[256,256]{1,0:T(8,128)(2,1)S(1)}, u32[]{:S(2)}, u32[]{:S(2)}) collective-permute-start(bf16[256,256]{1,0:T(8,128)(2,1)} %param.16), channel_id=1, source_target_pairs={{0,0},{1,16},{2,32},{3,48},{4,64},{5,80},{6,96},{7,112},{8,128},{9... | collective-permute-start | bytes 393224 | tf_op jit(solution)/shard_map/ppermute | solution.py:55
  22.6 1.2 copy.22
  23.9 9.4 %collective-permute-done = bf16[256,256]{1,0:T(8,128)(2,1)S(1)} collective-permute-done((bf16[256,256]{1,0:T(8,128)(2,1)}, bf16[256,256]{1,0:T(8,128)(2,1)S(1)}, u32[]{:S(2)}, u32[]{:S(2)}) %collective-permute-start) | collective-permute-done | bytes 131104 | tf_op jit(solution)/shard_map/ppermute | solution.py:55
  34.3 1.4 gather_fusion.2
  36.0 3.9 gather_fusion
  40.1 24.9 %all-gather.9.cloned.1.call-done = bf16[384,4096]{1,0:T(8,128)(2,1)} async-done(((bf16[384,512]{1,0:T(8,128)(2,1)}), bf16[384,4096]{1,0:T(8,128)(2,1)}) %all-gather.9.cloned.1.call-update) | async-done | bytes 3145744 | tf_op jit(solution)/shard_map/all_gather | solution.py:29
  64.9 2.6 fusion.31
  67.5 54.1 %all-gather.11.cloned.1.call-done = bf16[4096,1024]{1,0:T(8,128)(2,1)} async-done(((bf16[256,1024]{1,0:T(8,128)(2,1)}), bf16[4096,1024]{1,0:T(8,128)(2,1)}) %all-gather.11.cloned.1.call-update) | async-done | bytes 8388624 | tf_op jit(solution)/shard_map/all_gather | solution.py:65
  121.6 6.4 %fusion.49 = bf16[384,768]{1,0:T(8,128)(2,1)S(1)} fusion(bf16[4096,1024]{1,0:T(8,128)(2,1)} %all-gather.11.cloned.1.call-done, bf16[384,4096]{1,0:T(8,128)(2,1)} %all-gather.9.cloned.1.call-done, f32[4096]{0:T(1024)S(1)} %copy-done.5, f32[384]{0:T(512)S(1)} %add_rsqrt_fusion.1), kind=kOutput, calls=%fused_computation.85 | convolution fusion | flops 2422505472 | bytes 10044928 | tf_op jit(solution)/shard_map/dot_general | solution.py:43
  128.1 2.6 collective-permute-start.2
  130.7 1.9 collective-permute-start.1
  132.8 3.6 collective-permute-done.1
  136.4 30.2 %while.17 = (s32[]{:T(128)}, f32[2,192,256]{2,1,0:T(8,128)S(1)}, s32[2,319]{1,0:T(2,128)S(1)}, s32[2,192]{1,0:T(2,128)S(1)}, f32[2,319,256]{2,1,0:T(8,128)S(1)},...) while((s32[]{:T(128)}, f32[2,192,256]{2,1,0:T(8,128)S(1)}, ...), condition=%wide.region_2.3_spmd.clone, body=%wide.region_1.2_spmd.clone.sunk | while | flops 4823171 | bytes 7167463 | solution.py:150
  136.9 1.1 constant_dynamic-slice_fusion.33
  138.0 2.2 fusion.68
  140.6 1.1 constant_dynamic-slice_fusion.33
  141.7 2.2 fusion.68
  144.4 1.1 constant_dynamic-slice_fusion.33
  145.5 2.2 fusion.68
  148.2 1.1 constant_dynamic-slice_fusion.33
  149.3 2.2 fusion.68
  152.0 1.1 constant_dynamic-slice_fusion.33
  153.0 2.2 fusion.68
  155.7 1.1 constant_dynamic-slice_fusion.33
  156.8 2.2 fusion.68
  159.5 1.1 constant_dynamic-slice_fusion.33
  160.6 2.2 fusion.68
  163.3 1.1 constant_dynamic-slice_fusion.33
  164.4 2.2 fusion.68
  166.7 8.2 %all_gather.42 = bf16[384,512]{1,0:T(8,128)(2,1)} all-gather(bf16[384,256]{1,0:T(8,128)(2,1)S(1)} %fusion.55), channel_id=1, replica_groups=mesh['ctx'=16,'z'=8,'yh'=2] {'yh'}, dimensions={1}, use_global_device_ids=true | all-gather | bytes 589824 | tf_op jit(solution)/shard_map/all_gather | solution.py:28
  174.9 3.1 slice.82.columns_ref
  178.0 44.9 %all-gather.13.cloned.1.call-done.whole_ref = bf16[384,4096]{1,0:T(8,128)(2,1)} async-done(((bf16[384,512]{1,0:T(8,128)(2,1)}), bf16[384,4096]{1,0:T(8,128)(2,1)}) %all-gather.13.cloned.1.call-update) | async-done | bytes 3145744 | tf_op jit(solution)/shard_map/all_gather | solution.py:29
  223.0 4.2 shard_map.109.stream_ref
  227.1 9.9 %all_gather.44 = bf16[384,512]{1,0:T(8,128)(2,1)} all-gather(bf16[384,256]{1,0:T(8,128)(2,1)} %shard_map.109.stream_ref), channel_id=1, replica_groups=mesh['ctx'=16,'z'=8,'yh'=2] {'yh'}, dimensions={1}, use_global_device_ids=true | all-gather | bytes 589824 | tf_op jit(solution)/shard_map/all_gather | solution.py:28
  238.2 3.8 collective-permute-start.3
  243.3 11.5 %collective-permute-done.3 = bf16[256,256]{1,0:T(8,128)(2,1)S(1)} collective-permute-done((bf16[256,256]{1,0:T(8,128)(2,1)S(1)}, bf16[256,256]{1,0:T(8,128)(2,1)S(1)}, u32[]{:S(2)}, u32[]{:S(2)}) %collective-permute-start.3) | collective-permute-done | bytes 131104 | tf_op jit(solution)/shard_map/ppermute | solution.py:55
  257.7 26.1 %all-gather.15.cloned.1.call-done = bf16[384,4096]{1,0:T(8,128)(2,1)} async-done(((bf16[384,512]{1,0:T(8,128)(2,1)}), bf16[384,4096]{1,0:T(8,128)(2,1)}) %all-gather.15.cloned.1.call-update) | async-done | bytes 3145744 | tf_op jit(solution)/shard_map/all_gather | solution.py:29
  283.9 2.6 fusion.34
  286.5 51.9 %all-gather.17.cloned.1.call-done = bf16[4096,3,256]{0,2,1:T(8,128)(2,1)} async-done(((bf16[256,3,256]{0,2,1:T(8,128)(2,1)}), bf16[4096,3,256]{0,2,1:T(8,128)(2,1)}) %all-gather.17.cloned.1.call-update) | async-done | bytes 6291472 | tf_op jit(solution)/shard_map/all_gather | solution.py:33
  338.4 6.4 %fusion.46 = bf16[384,768]{1,0:T(8,128)(2,1)S(1)} fusion(bf16[4096,768]{0,1:T(8,128)(2,1)} %bitcast.118, bf16[384,4096]{1,0:T(8,128)(2,1)} %all-gather.15.cloned.1.call-done, f32[4096]{0:T(1024)S(1)} %copy-done.6, f32[384]{0:T(512)S(1)} %add_rsqrt_fusion), kind=kOutput, calls=%fused_computation.84 | convolution fusion | flops 2422505472 | bytes 10044928 | tf_op jit(solution)/shard_map/dot_general | solution.py:43
  346.2 3.8 shard_map.110
  350.0 17.9 %all-gather = f32[32,16,256]{2,1,0:T(8,128)S(1)} all-gather(f32[2,16,256]{2,1,0:T(8,128)} %get-tuple-element.239), channel_id=2, replica_groups=mesh['ctx'=16,'z'=8,'yh'=2] {'ctx'}, dimensions={0}, use_global_device_ids=true | all-gather | bytes 557056 | tf_op jit(solution)/shard_map/all_gather | solution.py:220
  368.9 3.8 shard_map.111
  372.7 1.1 fusion.54
  373.7 9.4 %all_gather.49 = bf16[384,512]{1,0:T(8,128)(2,1)} all-gather(bf16[384,256]{1,0:T(8,128)(2,1)S(1)} %fusion.54), channel_id=1, replica_groups=mesh['ctx'=16,'z'=8,'yh'=2] {'yh'}, dimensions={1}, use_global_device_ids=true | all-gather | bytes 589824 | tf_op jit(solution)/shard_map/all_gather | solution.py:28
  383.2 46.7 %all-gather.19.cloned.1.call-done.whole_ref = bf16[384,4096]{1,0:T(8,128)(2,1)} async-done(((bf16[384,512]{1,0:T(8,128)(2,1)}), bf16[384,4096]{1,0:T(8,128)(2,1)}) %all-gather.19.cloned.1.call-update) | async-done | bytes 3145744 | tf_op jit(solution)/shard_map/all_gather | solution.py:29
  429.9 4.2 shard_map.112
  (80 shorter events, 11.4 us)
Async XLA Ops:
  6.5 29.4 %copy-start = (s32[6144]{0:T(1024)S(1)}, s32[6144]{0:T(1024)}, u32[]{:S(2)}) copy-start(s32[6144]{0:T(1024)} %param.23) | copy-start | bytes 73732
  6.5 115.1 %copy-start.5 = (f32[4096]{0:T(1024)S(1)}, f32[4096]{0:T(1024)}, u32[]{:S(2)}) copy-start(f32[4096]{0:T(1024)} %param.14) | copy-start | bytes 49156
  6.5 58.4 %all-gather.9.cloned.1.call-start = ((), (), s32[]{:S(2)}) async-start(), calls=%async_computation | async-start | bytes 3538944 | tf_op jit(solution)/shard_map/all_gather | solution.py:29
  17.4 104.2 %all-gather.11.cloned.1.call-start = ((), (), s32[]{:S(2)}) async-start(), calls=%async_computation.1 | async-start | bytes 8912896 | tf_op jit(solution)/shard_map/all_gather | solution.py:65
  17.5 15.8 %collective-permute-start = (bf16[256,256]{1,0:T(8,128)(2,1)}, bf16[256,256]{1,0:T(8,128)(2,1)S(1)}, u32[]{:S(2)}, u32[]{:S(2)}) collective-permute-start(bf16[256,256]{1,0:T(8,128)(2,1)} %param.16), channel_id=1, source_target_pairs={{0,0},{1,16},{2,32},{3,48},{4,64},{5,80},{6,96},{7,112},{8,128},{9... | collective-permute-start | bytes 393224 | tf_op jit(solution)/shard_map/ppermute | solution.py:55
  34.2 188.8 %all-gather.13.cloned.1.call-start = ((), (), s32[]{:S(2)}) async-start(), calls=%async_computation.2 | async-start | bytes 3538944 | tf_op jit(solution)/shard_map/all_gather | solution.py:29
  128.1 4.6 %collective-permute-start.2 = (bf16[127,256]{1,0:T(8,128)(2,1)S(1)}, bf16[127,256]{1,0:T(8,128)(2,1)S(1)}, u32[]{:S(2)}, u32[]{:S(2)}) collective-permute-start(bf16[127,256]{1,0:T(8,128)(2,1)S(1)} %get-tuple-element.311), channel_id=1, source_target_pairs={{16,0},{32,16},{48,32},{64,48},{80,64},{96,80},{112,96},{128,112},... | collective-permute-start | bytes 195080 | tf_op jit(solution)/shard_map/ppermute | solution.py:19
  130.7 5.6 %collective-permute-start.1 = (bf16[127,256]{1,0:T(8,128)(2,1)S(1)}, bf16[127,256]{1,0:T(8,128)(2,1)S(1)}, u32[]{:S(2)}, u32[]{:S(2)}) collective-permute-start(bf16[127,256]{1,0:T(8,128)(2,1)S(1)} %get-tuple-element.310), channel_id=1, source_target_pairs={{0,16},{16,32},{32,48},{48,64},{64,80},{80,96},{96,112},{112,128},... | collective-permute-start | bytes 195080 | tf_op jit(solution)/shard_map/ppermute | solution.py:18
  166.6 70.5 %copy-start.1 = (bf16[256,3,256]{2,0,1:T(8,128)(2,1)S(1)}, bf16[256,3,256]{2,0,1:T(8,128)(2,1)}, u32[]{:S(2)}) copy-start(bf16[256,3,256]{2,0,1:T(8,128)(2,1)} %param.19) | copy-start | bytes 1179652
  174.8 63.3 %copy-start.4 = (bf16[256,256]{1,0:T(8,128)(2,1)S(1)}, bf16[256,256]{1,0:T(8,128)(2,1)}, u32[]{:S(2)}) copy-start(bf16[256,256]{1,0:T(8,128)(2,1)} %param.20) | copy-start | bytes 393220
  174.8 82.3 %copy-start.3 = (f32[16,256]{1,0:T(8,128)S(1)}, f32[16,256]{1,0:T(8,128)}, u32[]{:S(2)}) copy-start(f32[16,256]{1,0:T(8,128)} %param.21) | copy-start | bytes 49156
  174.9 109.0 %all-gather.15.cloned.1.call-start = ((), (), s32[]{:S(2)}) async-start(), calls=%async_computation.3 | async-start | bytes 3538944 | tf_op jit(solution)/shard_map/all_gather | solution.py:29
  178.0 160.3 %copy-start.6 = (f32[4096]{0:T(1024)S(1)}, f32[4096]{0:T(1024)}, u32[]{:S(2)}) copy-start(f32[4096]{0:T(1024)} %param.18) | copy-start | bytes 49156
  237.1 101.3 %all-gather.17.cloned.1.call-start = ((), (), s32[]{:S(2)}) async-start(), calls=%async_computation.4 | async-start | bytes 6684672 | tf_op jit(solution)/shard_map/all_gather | solution.py:33
  238.1 145.1 %all-gather.21.cloned.1.call-start = ((), (), s32[]{:S(2)}) async-start(), calls=%async_computation.6 | async-start | bytes 2228224 | tf_op jit(solution)/shard_map/all_gather | solution.py:59
  238.2 16.6 %collective-permute-start.3 = (bf16[256,256]{1,0:T(8,128)(2,1)S(1)}, bf16[256,256]{1,0:T(8,128)(2,1)S(1)}, u32[]{:S(2)}, u32[]{:S(2)}) collective-permute-start(bf16[256,256]{1,0:T(8,128)(2,1)S(1)} %copy-done.4), channel_id=1, source_target_pairs={{0,0},{1,16},{2,32},{3,48},{4,64},{5,80},{6,96},{7,112},{8,128},{9... | collective-permute-start | bytes 393224 | tf_op jit(solution)/shard_map/ppermute | solution.py:55
  254.8 0.7 copy-start.2
  255.4 174.5 %all-gather.19.cloned.1.call-start = ((), (), s32[]{:S(2)}) async-start(), calls=%async_computation.5 | async-start | bytes 3538944 | tf_op jit(solution)/shard_map/all_gather | solution.py:29
Sparse Core Ops, SparseCore 0:
  17.5 47.3 all-gather.8
  66.8 54.8 all-gather.10
  175.0 47.9 all-gather.12
  237.2 46.6 all-gather.14
  285.5 52.8 all-gather.16
  340.1 37.1 all-gather.20
  383.3 46.5 all-gather.18

commit v9 on v8

--- a/solution.py
+++ b/solution.py
@@ -82,13 +82,19 @@
 
 
 def project_groups(whole, columns, stream):
-    vmem = pl.BlockSpec(memory_space=pltpu.VMEM)
     rows, depth = whole.shape
+    width = stream.shape[1]
+    tile = 128 if rows % 128 == 0 else rows
     return pl.pallas_call(
         outproj_kernel,
         out_shape=jax.ShapeDtypeStruct(stream.shape, jnp.bfloat16),
-        in_specs=[vmem, vmem, vmem],
-        out_specs=vmem,
+        grid=(rows // tile,),
+        in_specs=[
+            pl.BlockSpec((tile, depth), lambda r: (r, 0)),
+            pl.BlockSpec((depth, width), lambda r: (0, 0)),
+            pl.BlockSpec((tile, width), lambda r: (r, 0)),
+        ],
+        out_specs=pl.BlockSpec((tile, width), lambda r: (r, 0)),
         cost_estimate=pl.CostEstimate(
             flops=2 * rows * depth * columns.shape[1],
             transcendentals=0,

time: 442 us -> 444 us (level)
  no operation moved by 1% of the time
where the time goes in v9:
time: 444 us; the launch traced here: 443 us
  waiting for transfers between devices  273 us (61%)
  blocking collectives  56.2 us (13%)
  other arithmetic  30.4 us (7%)
  local copies, waits for them, and re-layouts  22.8 us (5%)
  Pallas kernels  17.7 us (4%)
  starting transfers between devices  13.7 us (3%)
  between operations  13.7 us (3%)
  matrix products  12.8 us (3%)
    all_gather x4, waiting for transfers between devices, gather_channels(): return lax.all_gather(pair, 'z', axis=1, tiled=True)  143 us
    all_gather x1, waiting for transfers between devices, gather_layer_weights(): whole = lax.all_gather(joined, 'ctx', axis=0, tiled=True)  54.1 us
    all_gather x1, waiting for transfers between devices, gather_weights(): return lax.all_gather(inproj, 'ctx', axis=0, tiled=True)  51.9 us
    all_gather x4, blocking collectives, gather_channels(): pair = lax.all_gather(value, 'yh', axis=1, tiled=True)  38.4 us
    ppermute x2, waiting for transfers between devices, swap_blocks(): return lax.ppermute(outproj, ('ctx',) + CH, pairs)  20.8 us
    all_gather x1, blocking collectives, long_mix(): gathered = lax.all_gather(ends, 'ctx', axis=0, tiled=False)  17.9 us
    add x8, other arithmetic, tap_group(): running + jnp.where((source_docs == target_docs)[:, :, None], source, 0.0...  17.8 us
    dot_general x2, matrix products, features_in(): jnp.dot(normed, flat, preferred_element_type=jnp.float32)  12.8 us
  transfers between devices with their start and end apart: 11, of which 9 were waited for; matrix products, arithmetic and copies ran while one was open for 7% of the time, Pallas kernels for 2%

profile of v9, /device:TPU:4, one launch (start us, length us, event | category | flops | bytes accessed | tf_op | source)
XLA Modules:
  0.0 442.6 jit_solution(11435878075341472054)
XLA Ops:
  6.5 10.8 %all_gather.39 = bf16[384,512]{1,0:T(8,128)(2,1)} all-gather(bf16[384,256]{1,0:T(8,128)(2,1)} %stream_ref.1), channel_id=1, replica_groups=mesh['ctx'=16,'z'=8,'yh'=2] {'yh'}, dimensions={1}, use_global_device_ids=true | all-gather | bytes 589824 | tf_op jit(solution)/shard_map/all_gather | solution.py:28
  17.5 5.1 %collective-permute-start = (bf16[256,256]{1,0:T(8,128)(2,1)}, bf16[256,256]{1,0:T(8,128)(2,1)S(1)}, u32[]{:S(2)}, u32[]{:S(2)}) collective-permute-start(bf16[256,256]{1,0:T(8,128)(2,1)} %param.16), channel_id=1, source_target_pairs={{0,0},{1,16},{2,32},{3,48},{4,64},{5,80},{6,96},{7,112},{8,128},{9... | collective-permute-start | bytes 393224 | tf_op jit(solution)/shard_map/ppermute | solution.py:55
  22.6 1.2 copy.22
  23.9 9.4 %collective-permute-done = bf16[256,256]{1,0:T(8,128)(2,1)S(1)} collective-permute-done((bf16[256,256]{1,0:T(8,128)(2,1)}, bf16[256,256]{1,0:T(8,128)(2,1)S(1)}, u32[]{:S(2)}, u32[]{:S(2)}) %collective-permute-start) | collective-permute-done | bytes 131104 | tf_op jit(solution)/shard_map/ppermute | solution.py:55
  34.3 1.4 gather_fusion.2
  36.0 3.9 gather_fusion
  40.1 24.9 %all-gather.9.cloned.1.call-done = bf16[384,4096]{1,0:T(8,128)(2,1)} async-done(((bf16[384,512]{1,0:T(8,128)(2,1)}), bf16[384,4096]{1,0:T(8,128)(2,1)}) %all-gather.9.cloned.1.call-update) | async-done | bytes 3145744 | tf_op jit(solution)/shard_map/all_gather | solution.py:29
  64.9 2.6 fusion.31
  67.5 54.1 %all-gather.11.cloned.1.call-done = bf16[4096,1024]{1,0:T(8,128)(2,1)} async-done(((bf16[256,1024]{1,0:T(8,128)(2,1)}), bf16[4096,1024]{1,0:T(8,128)(2,1)}) %all-gather.11.cloned.1.call-update) | async-done | bytes 8388624 | tf_op jit(solution)/shard_map/all_gather | solution.py:65
  121.6 6.4 %fusion.49 = bf16[384,768]{1,0:T(8,128)(2,1)S(1)} fusion(bf16[4096,1024]{1,0:T(8,128)(2,1)} %all-gather.11.cloned.1.call-done, bf16[384,4096]{1,0:T(8,128)(2,1)} %all-gather.9.cloned.1.call-done, f32[4096]{0:T(1024)S(1)} %copy-done.5, f32[384]{0:T(512)S(1)} %add_rsqrt_fusion.1), kind=kOutput, calls=%fused_computation.85 | convolution fusion | flops 2422505472 | bytes 10044928 | tf_op jit(solution)/shard_map/dot_general | solution.py:43
  128.1 2.6 collective-permute-start.2
  130.7 1.9 collective-permute-start.1
  132.8 3.6 collective-permute-done.1
  136.4 30.2 %while.17 = (s32[]{:T(128)}, f32[2,192,256]{2,1,0:T(8,128)S(1)}, s32[2,319]{1,0:T(2,128)S(1)}, s32[2,192]{1,0:T(2,128)S(1)}, f32[2,319,256]{2,1,0:T(8,128)S(1)},...) while((s32[]{:T(128)}, f32[2,192,256]{2,1,0:T(8,128)S(1)}, ...), condition=%wide.region_2.3_spmd.clone, body=%wide.region_1.2_spmd.clone.sunk | while | flops 4823171 | bytes 7167463 | solution.py:156
  136.9 1.1 constant_dynamic-slice_fusion.33
  138.0 2.2 fusion.68
  140.6 1.1 constant_dynamic-slice_fusion.33
  141.7 2.2 fusion.68
  144.4 1.1 constant_dynamic-slice_fusion.33
  145.5 2.2 fusion.68
  148.2 1.1 constant_dynamic-slice_fusion.33
  149.3 2.2 fusion.68
  152.0 1.1 constant_dynamic-slice_fusion.33
  153.0 2.2 fusion.68
  155.7 1.1 constant_dynamic-slice_fusion.33
  156.8 2.2 fusion.68
  159.5 1.1 constant_dynamic-slice_fusion.33
  160.6 2.2 fusion.68
  163.3 1.1 constant_dynamic-slice_fusion.33
  164.4 2.2 fusion.68
  166.7 8.2 %all_gather.42 = bf16[384,512]{1,0:T(8,128)(2,1)} all-gather(bf16[384,256]{1,0:T(8,128)(2,1)S(1)} %fusion.55), channel_id=1, replica_groups=mesh['ctx'=16,'z'=8,'yh'=2] {'yh'}, dimensions={1}, use_global_device_ids=true | all-gather | bytes 589824 | tf_op jit(solution)/shard_map/all_gather | solution.py:28
  174.9 3.1 slice.82.columns_ref
  178.0 44.9 %all-gather.13.cloned.1.call-done.whole_ref = bf16[384,4096]{1,0:T(8,128)(2,1)} async-done(((bf16[384,512]{1,0:T(8,128)(2,1)}), bf16[384,4096]{1,0:T(8,128)(2,1)}) %all-gather.13.cloned.1.call-update) | async-done | bytes 3145744 | tf_op jit(solution)/shard_map/all_gather | solution.py:29
  223.0 5.0 %shard_map.109.stream_ref = bf16[384,256]{1,0:T(8,128)(2,1)} custom-call(bf16[384,4096]{1,0:T(8,128)(2,1)} %all-gather.13.cloned.1.call-done.whole_ref, bf16[4096,256]{1,0:T(8,128)(2,1)} %slice.82.columns_ref, bf16[384,256]{1,0:T(8,128)(2,1)} %stream_ref.1), custom_call_target="tpu_custom_call" | custom-call | flops 805306368 | bytes 5636096 | tf_op jit(solution)/shard_map/pallas_call | solution.py:88
  228.0 9.9 %all_gather.44 = bf16[384,512]{1,0:T(8,128)(2,1)} all-gather(bf16[384,256]{1,0:T(8,128)(2,1)} %shard_map.109.stream_ref), channel_id=1, replica_groups=mesh['ctx'=16,'z'=8,'yh'=2] {'yh'}, dimensions={1}, use_global_device_ids=true | all-gather | bytes 589824 | tf_op jit(solution)/shard_map/all_gather | solution.py:28
  239.0 3.8 collective-permute-start.3
  244.2 11.5 %collective-permute-done.3 = bf16[256,256]{1,0:T(8,128)(2,1)S(1)} collective-permute-done((bf16[256,256]{1,0:T(8,128)(2,1)S(1)}, bf16[256,256]{1,0:T(8,128)(2,1)S(1)}, u32[]{:S(2)}, u32[]{:S(2)}) %collective-permute-start.3) | collective-permute-done | bytes 131104 | tf_op jit(solution)/shard_map/ppermute | solution.py:55
  258.6 26.1 %all-gather.15.cloned.1.call-done = bf16[384,4096]{1,0:T(8,128)(2,1)} async-done(((bf16[384,512]{1,0:T(8,128)(2,1)}), bf16[384,4096]{1,0:T(8,128)(2,1)}) %all-gather.15.cloned.1.call-update) | async-done | bytes 3145744 | tf_op jit(solution)/shard_map/all_gather | solution.py:29
  284.7 2.6 fusion.34
  287.3 51.9 %all-gather.17.cloned.1.call-done = bf16[4096,3,256]{0,2,1:T(8,128)(2,1)} async-done(((bf16[256,3,256]{0,2,1:T(8,128)(2,1)}), bf16[4096,3,256]{0,2,1:T(8,128)(2,1)}) %all-gather.17.cloned.1.call-update) | async-done | bytes 6291472 | tf_op jit(solution)/shard_map/all_gather | solution.py:33
  339.2 6.4 %fusion.46 = bf16[384,768]{1,0:T(8,128)(2,1)S(1)} fusion(bf16[4096,768]{0,1:T(8,128)(2,1)} %bitcast.118, bf16[384,4096]{1,0:T(8,128)(2,1)} %all-gather.15.cloned.1.call-done, f32[4096]{0:T(1024)S(1)} %copy-done.6, f32[384]{0:T(512)S(1)} %add_rsqrt_fusion), kind=kOutput, calls=%fused_computation.84 | convolution fusion | flops 2422505472 | bytes 10044928 | tf_op jit(solution)/shard_map/dot_general | solution.py:43
  347.1 3.8 shard_map.110
  350.9 17.9 %all-gather = f32[32,16,256]{2,1,0:T(8,128)S(1)} all-gather(f32[2,16,256]{2,1,0:T(8,128)} %get-tuple-element.239), channel_id=2, replica_groups=mesh['ctx'=16,'z'=8,'yh'=2] {'ctx'}, dimensions={0}, use_global_device_ids=true | all-gather | bytes 557056 | tf_op jit(solution)/shard_map/all_gather | solution.py:226
  369.7 3.8 shard_map.111
  373.5 1.1 fusion.54
  374.6 9.4 %all_gather.49 = bf16[384,512]{1,0:T(8,128)(2,1)} all-gather(bf16[384,256]{1,0:T(8,128)(2,1)S(1)} %fusion.54), channel_id=1, replica_groups=mesh['ctx'=16,'z'=8,'yh'=2] {'yh'}, dimensions={1}, use_global_device_ids=true | all-gather | bytes 589824 | tf_op jit(solution)/shard_map/all_gather | solution.py:28
  384.1 46.6 %all-gather.19.cloned.1.call-done.whole_ref = bf16[384,4096]{1,0:T(8,128)(2,1)} async-done(((bf16[384,512]{1,0:T(8,128)(2,1)}), bf16[384,4096]{1,0:T(8,128)(2,1)}) %all-gather.19.cloned.1.call-update) | async-done | bytes 3145744 | tf_op jit(solution)/shard_map/all_gather | solution.py:29
  430.7 5.1 %shard_map.112 = bf16[384,256]{1,0:T(8,128)(2,1)} custom-call(bf16[384,4096]{1,0:T(8,128)(2,1)} %all-gather.19.cloned.1.call-done.whole_ref, bf16[4096,256]{1,0:T(8,128)(2,1)} %all-gather.21.cloned.1.call-done.columns_ref, bf16[384,256]{1,0:T(8,128)(2,1)} %shard_map.109.stream_ref), custom_call_target="tpu_custom_call" | custom-call | flops 805306368 | bytes 5636096 | tf_op jit(solution)/shard_map/pallas_call | solution.py:88
  (80 shorter events, 11.4 us)
Async XLA Ops:
  6.5 29.4 %copy-start = (s32[6144]{0:T(1024)S(1)}, s32[6144]{0:T(1024)}, u32[]{:S(2)}) copy-start(s32[6144]{0:T(1024)} %param.23) | copy-start | bytes 73732
  6.5 115.1 %copy-start.5 = (f32[4096]{0:T(1024)S(1)}, f32[4096]{0:T(1024)}, u32[]{:S(2)}) copy-start(f32[4096]{0:T(1024)} %param.14) | copy-start | bytes 49156
  6.5 58.4 %all-gather.9.cloned.1.call-start = ((), (), s32[]{:S(2)}) async-start(), calls=%async_computation | async-start | bytes 3538944 | tf_op jit(solution)/shard_map/all_gather | solution.py:29
  17.4 104.2 %all-gather.11.cloned.1.call-start = ((), (), s32[]{:S(2)}) async-start(), calls=%async_computation.1 | async-start | bytes 8912896 | tf_op jit(solution)/shard_map/all_gather | solution.py:65
  17.5 15.8 %collective-permute-start = (bf16[256,256]{1,0:T(8,128)(2,1)}, bf16[256,256]{1,0:T(8,128)(2,1)S(1)}, u32[]{:S(2)}, u32[]{:S(2)}) collective-permute-start(bf16[256,256]{1,0:T(8,128)(2,1)} %param.16), channel_id=1, source_target_pairs={{0,0},{1,16},{2,32},{3,48},{4,64},{5,80},{6,96},{7,112},{8,128},{9... | collective-permute-start | bytes 393224 | tf_op jit(solution)/shard_map/ppermute | solution.py:55
  34.2 188.8 %all-gather.13.cloned.1.call-start = ((), (), s32[]{:S(2)}) async-start(), calls=%async_computation.2 | async-start | bytes 3538944 | tf_op jit(solution)/shard_map/all_gather | solution.py:29
  128.1 4.6 %collective-permute-start.2 = (bf16[127,256]{1,0:T(8,128)(2,1)S(1)}, bf16[127,256]{1,0:T(8,128)(2,1)S(1)}, u32[]{:S(2)}, u32[]{:S(2)}) collective-permute-start(bf16[127,256]{1,0:T(8,128)(2,1)S(1)} %get-tuple-element.311), channel_id=1, source_target_pairs={{16,0},{32,16},{48,32},{64,48},{80,64},{96,80},{112,96},{128,112},... | collective-permute-start | bytes 195080 | tf_op jit(solution)/shard_map/ppermute | solution.py:19
  130.7 5.6 %collective-permute-start.1 = (bf16[127,256]{1,0:T(8,128)(2,1)S(1)}, bf16[127,256]{1,0:T(8,128)(2,1)S(1)}, u32[]{:S(2)}, u32[]{:S(2)}) collective-permute-start(bf16[127,256]{1,0:T(8,128)(2,1)S(1)} %get-tuple-element.310), channel_id=1, source_target_pairs={{0,16},{16,32},{32,48},{48,64},{64,80},{80,96},{96,112},{112,128},... | collective-permute-start | bytes 195080 | tf_op jit(solution)/shard_map/ppermute | solution.py:18
  166.6 71.4 %copy-start.1 = (bf16[256,3,256]{2,0,1:T(8,128)(2,1)S(1)}, bf16[256,3,256]{2,0,1:T(8,128)(2,1)}, u32[]{:S(2)}) copy-start(bf16[256,3,256]{2,0,1:T(8,128)(2,1)} %param.19) | copy-start | bytes 1179652
  174.8 64.2 %copy-start.4 = (bf16[256,256]{1,0:T(8,128)(2,1)S(1)}, bf16[256,256]{1,0:T(8,128)(2,1)}, u32[]{:S(2)}) copy-start(bf16[256,256]{1,0:T(8,128)(2,1)} %param.20) | copy-start | bytes 393220
  174.8 83.1 %copy-start.3 = (f32[16,256]{1,0:T(8,128)S(1)}, f32[16,256]{1,0:T(8,128)}, u32[]{:S(2)}) copy-start(f32[16,256]{1,0:T(8,128)} %param.21) | copy-start | bytes 49156
  174.9 109.9 %all-gather.15.cloned.1.call-start = ((), (), s32[]{:S(2)}) async-start(), calls=%async_computation.3 | async-start | bytes 3538944 | tf_op jit(solution)/shard_map/all_gather | solution.py:29
  178.0 161.2 %copy-start.6 = (f32[4096]{0:T(1024)S(1)}, f32[4096]{0:T(1024)}, u32[]{:S(2)}) copy-start(f32[4096]{0:T(1024)} %param.18) | copy-start | bytes 49156
  238.0 101.3 %all-gather.17.cloned.1.call-start = ((), (), s32[]{:S(2)}) async-start(), calls=%async_computation.4 | async-start | bytes 6684672 | tf_op jit(solution)/shard_map/all_gather | solution.py:33
  239.0 145.1 %all-gather.21.cloned.1.call-start = ((), (), s32[]{:S(2)}) async-start(), calls=%async_computation.6 | async-start | bytes 2228224 | tf_op jit(solution)/shard_map/all_gather | solution.py:59
  239.0 16.6 %collective-permute-start.3 = (bf16[256,256]{1,0:T(8,128)(2,1)S(1)}, bf16[256,256]{1,0:T(8,128)(2,1)S(1)}, u32[]{:S(2)}, u32[]{:S(2)}) collective-permute-start(bf16[256,256]{1,0:T(8,128)(2,1)S(1)} %copy-done.4), channel_id=1, source_target_pairs={{0,0},{1,16},{2,32},{3,48},{4,64},{5,80},{6,96},{7,112},{8,128},{9... | collective-permute-start | bytes 393224 | tf_op jit(solution)/shard_map/ppermute | solution.py:55
  255.6 0.7 copy-start.2
  256.3 174.4 %all-gather.19.cloned.1.call-start = ((), (), s32[]{:S(2)}) async-start(), calls=%async_computation.5 | async-start | bytes 3538944 | tf_op jit(solution)/shard_map/all_gather | solution.py:29
Sparse Core Ops, SparseCore 0:
  17.5 47.3 all-gather.8
  66.8 54.8 all-gather.10
  175.0 47.9 all-gather.12
  238.1 46.6 all-gather.14
  286.3 52.8 all-gather.16
  340.9 37.1 all-gather.20
  384.2 46.4 all-gather.18

commit v10 on v8

--- a/solution.py
+++ b/solution.py
@@ -97,8 +97,9 @@
     )(whole, columns, stream)
 
 
-def features_out(stream, query, mixed, columns):
-    gated = (query.astype(jnp.float32) * mixed).astype(jnp.bfloat16)
+def features_out(stream, query, mixed, columns, gated=None):
+    if gated is None:
+        gated = (query.astype(jnp.float32) * mixed).astype(jnp.bfloat16)
     whole = gather_channels(gated)
     return project_groups(whole, columns, stream)
 
@@ -153,16 +154,23 @@
     return mixed.reshape(shard_rows, channels)
 
 
-def scan_kernel(flags_ref, x_ref, factor_ref, init_ref, residue_ref, mixed_ref, end_ref):
+def scan_kernel(flags_ref, x_ref, factor_ref, init_ref, residue_ref, *refs):
+    if len(refs) == 4:
+        query_ref, gated_ref, end_ref, rows_ref = refs
+    else:
+        query_ref = gated_ref = None
+        end_ref, rows_ref = refs
     halves, span_rows, _ = x_ref.shape
     factor = factor_ref[...]
     residue = residue_ref[...]
+    rows_ref[0] = x_ref[...].astype(jnp.float32)
+    mixed_ref = rows_ref.at[1]
 
     def step(t, states):
         updated = []
         for half in range(halves):
             kept = factor * flags_ref[half * span_rows + t]
-            state = kept * states[half] + x_ref[half, pl.ds(t, 1), :]
+            state = kept * states[half] + rows_ref[0, half, pl.ds(t, 1), :]
             mixed_ref[half, pl.ds(t, 1), :] = jnp.sum(residue * state, axis=0, keepdims=True)
             updated.append(state)
         return tuple(updated)
@@ -170,25 +178,31 @@
     ends = lax.fori_loop(0, span_rows, step, tuple(init_ref[half] for half in range(halves)), unroll=8)
     for half in range(halves):
         end_ref[half] = ends[half]
-
-
-def run_scan(flags, values, factor, init, residue):
+    if gated_ref is not None:
+        gated_ref[...] = (query_ref[...].astype(jnp.float32) * mixed_ref[...]).astype(jnp.bfloat16)
+
+
+def run_scan(flags, values, factor, init, residue, query=None):
     halves, span_rows, channels = values.shape
     modes = factor.shape[0]
     vmem = pl.BlockSpec(memory_space=pltpu.VMEM)
     steps = halves * span_rows * modes * channels
+    ends = jax.ShapeDtypeStruct((halves, modes, channels), jnp.float32)
+    operands = [flags, values, factor, init, residue]
+    out_shape = (ends,)
+    if query is not None:
+        operands.append(query)
+        out_shape = (jax.ShapeDtypeStruct(query.shape, jnp.bfloat16), ends)
     return pl.pallas_call(
         scan_kernel,
-        out_shape=(
-            jax.ShapeDtypeStruct((halves, span_rows, channels), jnp.float32),
-            jax.ShapeDtypeStruct((halves, modes, channels), jnp.float32),
-        ),
-        in_specs=[pl.BlockSpec(memory_space=pltpu.SMEM), vmem, vmem, vmem, vmem],
-        out_specs=(vmem, vmem),
+        out_shape=out_shape,
+        in_specs=[pl.BlockSpec(memory_space=pltpu.SMEM)] + [vmem] * (len(operands) - 1),
+        out_specs=tuple(vmem for _ in out_shape),
+        scratch_shapes=[pltpu.VMEM((2, halves, span_rows, channels), jnp.float32)],
         cost_estimate=pl.CostEstimate(
             flops=5 * steps, transcendentals=0, bytes_accessed=8 * halves * span_rows * channels
         ),
-    )(flags, values, factor, init, residue)
+    )(*operands)
 
 
 def li_tables(doc_ids, li_decay, shard_rows):
@@ -208,20 +222,20 @@
     return flags, weights
 
 
-def long_mix(product, li_decay, li_residue, tables):
+def long_mix(product, query, li_decay, li_residue, tables):
     flags, weights = tables
     shard_rows, channels = product.shape
     span_rows = shard_rows // 2
     modes = li_decay.shape[0]
     factor = jnp.exp(-li_decay)
-    values = product.reshape(2, span_rows, channels).astype(jnp.float32)
+    values = product.reshape(2, span_rows, channels)
     zeros = jnp.zeros((2, modes, channels), jnp.float32)
-    _, ends = run_scan(flags, values, factor, zeros, li_residue)
+    (ends,) = run_scan(flags, values, factor, zeros, li_residue)
     gathered = lax.all_gather(ends, "ctx", axis=0, tiled=False)
     block_ends = jnp.concatenate([gathered[:, 0], gathered[::-1, 1]], 0)
     entry = jnp.sum(weights * block_ends[None], axis=1)
-    mixed, _ = run_scan(flags, values, factor, entry, li_residue)
-    return mixed.reshape(shard_rows, channels)
+    gated, _ = run_scan(flags, values, factor, entry, li_residue, query.reshape(2, span_rows, channels))
+    return gated.reshape(shard_rows, channels)
 
 
 def body(
@@ -245,7 +259,7 @@
     mixed = short_mix(product, mr_filter, doc_ids)
     stream = features_out(tokens, query, mixed, mr_columns)
     query, product = features_in(stream, li_gain, li_piece)
-    return features_out(stream, query, long_mix(product, li_decay, li_residue, tables), li_columns)
+    return features_out(stream, None, None, li_columns, long_mix(product, query, li_decay, li_residue, tables))
 
 
 def solution(mesh):

time: 442 us -> 444 us (level)
  no operation moved by 1% of the time
where the time goes in v10:
time: 444 us; the launch traced here: 443 us
  waiting for transfers between devices  272 us (61%)
  blocking collectives  57.9 us (13%)
  other arithmetic  29.2 us (7%)
  local copies, waits for them, and re-layouts  23.4 us (5%)
  Pallas kernels  17.7 us (4%)
  starting transfers between devices  13.7 us (3%)
  between operations  13.7 us (3%)
  matrix products  12.8 us (3%)
    all_gather x4, waiting for transfers between devices, gather_channels(): return lax.all_gather(pair, 'z', axis=1, tiled=True)  141 us
    all_gather x1, waiting for transfers between devices, gather_layer_weights(): whole = lax.all_gather(joined, 'ctx', axis=0, tiled=True)  54.1 us
    all_gather x1, waiting for transfers between devices, gather_weights(): return lax.all_gather(inproj, 'ctx', axis=0, tiled=True)  51.9 us
    all_gather x4, blocking collectives, gather_channels(): pair = lax.all_gather(value, 'yh', axis=1, tiled=True)  39.8 us
    ppermute x2, waiting for transfers between devices, swap_blocks(): return lax.ppermute(outproj, ('ctx',) + CH, pairs)  21.6 us
    all_gather x1, blocking collectives, long_mix(): gathered = lax.all_gather(ends, 'ctx', axis=0, tiled=False)  18.1 us
    add x8, other arithmetic, tap_group(): running + jnp.where((source_docs == target_docs)[:, :, None], source, 0.0...  17.8 us
    dot_general x2, matrix products, features_in(): jnp.dot(normed, flat, preferred_element_type=jnp.float32)  12.8 us
  transfers between devices with their start and end apart: 11, of which 9 were waited for; matrix products, arithmetic and copies ran while one was open for 7% of the time, Pallas kernels for 2%

profile of v10, /device:TPU:4, one launch (start us, length us, event | category | flops | bytes accessed | tf_op | source)
XLA Modules:
  0.0 443.1 jit_solution(1982822257667246146)
XLA Ops:
  6.5 10.8 %all_gather.39 = bf16[384,512]{1,0:T(8,128)(2,1)} all-gather(bf16[384,256]{1,0:T(8,128)(2,1)} %stream_ref.1), channel_id=1, replica_groups=mesh['ctx'=16,'z'=8,'yh'=2] {'yh'}, dimensions={1}, use_global_device_ids=true | all-gather | bytes 589824 | tf_op jit(solution)/shard_map/all_gather | solution.py:28
  17.4 5.1 %collective-permute-start = (bf16[256,256]{1,0:T(8,128)(2,1)}, bf16[256,256]{1,0:T(8,128)(2,1)S(1)}, u32[]{:S(2)}, u32[]{:S(2)}) collective-permute-start(bf16[256,256]{1,0:T(8,128)(2,1)} %param.16), channel_id=1, source_target_pairs={{0,0},{1,16},{2,32},{3,48},{4,64},{5,80},{6,96},{7,112},{8,128},{9... | collective-permute-start | bytes 393224 | tf_op jit(solution)/shard_map/ppermute | solution.py:55
  22.6 1.2 copy.22
  23.9 9.3 %collective-permute-done = bf16[256,256]{1,0:T(8,128)(2,1)S(1)} collective-permute-done((bf16[256,256]{1,0:T(8,128)(2,1)}, bf16[256,256]{1,0:T(8,128)(2,1)S(1)}, u32[]{:S(2)}, u32[]{:S(2)}) %collective-permute-start) | collective-permute-done | bytes 131104 | tf_op jit(solution)/shard_map/ppermute | solution.py:55
  34.3 1.4 gather_fusion.2
  35.9 3.9 gather_fusion
  40.0 24.9 %all-gather.9.cloned.1.call-done = bf16[384,4096]{1,0:T(8,128)(2,1)} async-done(((bf16[384,512]{1,0:T(8,128)(2,1)}), bf16[384,4096]{1,0:T(8,128)(2,1)}) %all-gather.9.cloned.1.call-update) | async-done | bytes 3145744 | tf_op jit(solution)/shard_map/all_gather | solution.py:29
  64.9 2.6 fusion.31
  67.5 54.1 %all-gather.11.cloned.1.call-done = bf16[4096,1024]{1,0:T(8,128)(2,1)} async-done(((bf16[256,1024]{1,0:T(8,128)(2,1)}), bf16[4096,1024]{1,0:T(8,128)(2,1)}) %all-gather.11.cloned.1.call-update) | async-done | bytes 8388624 | tf_op jit(solution)/shard_map/all_gather | solution.py:65
  121.6 6.4 %fusion.49 = bf16[384,768]{1,0:T(8,128)(2,1)S(1)} fusion(bf16[4096,1024]{1,0:T(8,128)(2,1)} %all-gather.11.cloned.1.call-done, bf16[384,4096]{1,0:T(8,128)(2,1)} %all-gather.9.cloned.1.call-done, f32[4096]{0:T(1024)S(1)} %copy-done.5, f32[384]{0:T(512)S(1)} %add_rsqrt_fusion.1), kind=kOutput, calls=%fused_computation.85 | convolution fusion | flops 2422505472 | bytes 10044928 | tf_op jit(solution)/shard_map/dot_general | solution.py:43
  128.1 2.6 collective-permute-start.2
  130.7 1.9 collective-permute-start.1
  132.8 3.6 collective-permute-done.1
  136.4 30.2 %while.17 = (s32[]{:T(128)}, f32[2,192,256]{2,1,0:T(8,128)S(1)}, s32[2,319]{1,0:T(2,128)S(1)}, s32[2,192]{1,0:T(2,128)S(1)}, f32[2,319,256]{2,1,0:T(8,128)S(1)},...) while((s32[]{:T(128)}, f32[2,192,256]{2,1,0:T(8,128)S(1)}, ...), condition=%wide.region_2.3_spmd.clone, body=%wide.region_1.2_spmd.clone.sunk | while | flops 4823171 | bytes 7167463 | solution.py:151
  136.9 1.1 constant_dynamic-slice_fusion.33
  138.0 2.2 fusion.67
  140.6 1.1 constant_dynamic-slice_fusion.33
  141.7 2.2 fusion.67
  144.4 1.1 constant_dynamic-slice_fusion.33
  145.5 2.2 fusion.67
  148.2 1.1 constant_dynamic-slice_fusion.33
  149.3 2.2 fusion.67
  152.0 1.1 constant_dynamic-slice_fusion.33
  153.0 2.2 fusion.67
  155.7 1.1 constant_dynamic-slice_fusion.33
  156.8 2.2 fusion.67
  159.5 1.1 constant_dynamic-slice_fusion.33
  160.6 2.2 fusion.67
  163.3 1.1 constant_dynamic-slice_fusion.33
  164.4 2.2 fusion.67
  166.7 8.2 %all_gather.42 = bf16[384,512]{1,0:T(8,128)(2,1)} all-gather(bf16[384,256]{1,0:T(8,128)(2,1)S(1)} %fusion.54), channel_id=1, replica_groups=mesh['ctx'=16,'z'=8,'yh'=2] {'yh'}, dimensions={1}, use_global_device_ids=true | all-gather | bytes 589824 | tf_op jit(solution)/shard_map/all_gather | solution.py:28
  174.9 3.1 slice.82.columns_ref
  178.0 44.9 %all-gather.13.cloned.1.call-done.whole_ref = bf16[384,4096]{1,0:T(8,128)(2,1)} async-done(((bf16[384,512]{1,0:T(8,128)(2,1)}), bf16[384,4096]{1,0:T(8,128)(2,1)}) %all-gather.13.cloned.1.call-update) | async-done | bytes 3145744 | tf_op jit(solution)/shard_map/all_gather | solution.py:29
  223.0 4.2 shard_map.109.stream_ref
  227.2 9.9 %all_gather.44 = bf16[384,512]{1,0:T(8,128)(2,1)} all-gather(bf16[384,256]{1,0:T(8,128)(2,1)} %shard_map.109.stream_ref), channel_id=1, replica_groups=mesh['ctx'=16,'z'=8,'yh'=2] {'yh'}, dimensions={1}, use_global_device_ids=true | all-gather | bytes 589824 | tf_op jit(solution)/shard_map/all_gather | solution.py:28
  237.2 0.9 copy.24
  238.2 3.8 collective-permute-start.3
  242.5 12.3 %collective-permute-done.3 = bf16[256,256]{1,0:T(8,128)(2,1)S(1)} collective-permute-done((bf16[256,256]{1,0:T(8,128)(2,1)S(1)}, bf16[256,256]{1,0:T(8,128)(2,1)S(1)}, u32[]{:S(2)}, u32[]{:S(2)}) %collective-permute-start.3) | collective-permute-done | bytes 131104 | tf_op jit(solution)/shard_map/ppermute | solution.py:55
  258.5 25.4 %all-gather.15.cloned.1.call-done = bf16[384,4096]{1,0:T(8,128)(2,1)} async-done(((bf16[384,512]{1,0:T(8,128)(2,1)}), bf16[384,4096]{1,0:T(8,128)(2,1)}) %all-gather.15.cloned.1.call-update) | async-done | bytes 3145744 | tf_op jit(solution)/shard_map/all_gather | solution.py:29
  283.9 2.6 fusion.34
  286.5 51.9 %all-gather.17.cloned.1.call-done = bf16[4096,3,256]{0,2,1:T(8,128)(2,1)} async-done(((bf16[256,3,256]{0,2,1:T(8,128)(2,1)}), bf16[4096,3,256]{0,2,1:T(8,128)(2,1)}) %all-gather.17.cloned.1.call-update) | async-done | bytes 6291472 | tf_op jit(solution)/shard_map/all_gather | solution.py:33
  338.4 6.4 %fusion.46 = bf16[384,768]{1,0:T(8,128)(2,1)S(1)} fusion(bf16[4096,768]{0,1:T(8,128)(2,1)} %bitcast.118, bf16[384,4096]{1,0:T(8,128)(2,1)} %all-gather.15.cloned.1.call-done, f32[4096]{0:T(1024)S(1)} %copy-done.6, f32[384]{0:T(512)S(1)} %add_rsqrt_fusion), kind=kOutput, calls=%fused_computation.84 | convolution fusion | flops 2422505472 | bytes 10044928 | tf_op jit(solution)/shard_map/dot_general | solution.py:43
  346.8 4.5 %shard_map.110 = f32[2,16,256]{2,1,0:T(8,128)} custom-call(f32[384]{0:T(512)} %reshape.436.flags_ref, bf16[2,192,256]{2,1,0:T(8,128)(2,1)} %bitcast.91, f32[16,256]{1,0:T(8,128)} %get-tuple-element.317.factor_ref, f32[2,16,256]{2,1,0:T(8,128)} %broadcast_in_dim.449.init_ref, f32[16,256]{1,0:T(8,128)} %residue_ref.3), custom_call_target="tpu_custom_call" | custom-call | flops 7864320 | bytes 786432 | tf_op jit(solution)/shard_map/pallas_call | solution.py:196
  351.3 18.1 %all-gather = f32[32,16,256]{2,1,0:T(8,128)S(1)} all-gather(f32[2,16,256]{2,1,0:T(8,128)} %shard_map.110), channel_id=2, replica_groups=mesh['ctx'=16,'z'=8,'yh'=2] {'ctx'}, dimensions={0}, use_global_device_ids=true | all-gather | bytes 557056 | tf_op jit(solution)/shard_map/all_gather | solution.py:234
  370.4 4.9 %shard_map.111 = (bf16[2,192,256]{2,1,0:T(8,128)(2,1)}, f32[2,16,256]{2,1,0:T(8,128)}) custom-call(f32[384]{0:T(512)} %reshape.436.flags_ref, bf16[2,192,256]{2,1,0:T(8,128)(2,1)} %bitcast.92, f32[16,256]{1,0:T(8,128)} %get-tuple-element.317.factor_ref, f32[2,16,256]{2,1,0:T(8,128)} %multiply_reduce_fusion.init_ref, f32[16,256]{1,0:T(8,128)} %residue_ref.3, ...), custom_call_target="tpu_custom_call" | custom-call | flops 7864320 | bytes 786432 | tf_op jit(solution)/shard_map/pallas_call | solution.py:196
  375.3 10.9 %all_gather.49 = bf16[384,512]{1,0:T(8,128)(2,1)} all-gather(bf16[384,256]{1,0:T(8,128)(2,1)} %bitcast.97), channel_id=1, replica_groups=mesh['ctx'=16,'z'=8,'yh'=2] {'yh'}, dimensions={1}, use_global_device_ids=true | all-gather | bytes 589824 | tf_op jit(solution)/shard_map/all_gather | solution.py:28
  386.2 45.8 %all-gather.19.cloned.1.call-done.whole_ref = bf16[384,4096]{1,0:T(8,128)(2,1)} async-done(((bf16[384,512]{1,0:T(8,128)(2,1)}), bf16[384,4096]{1,0:T(8,128)(2,1)}) %all-gather.19.cloned.1.call-update) | async-done | bytes 3145744 | tf_op jit(solution)/shard_map/all_gather | solution.py:29
  432.1 4.2 shard_map.112
  (79 shorter events, 11.0 us)
Async XLA Ops:
  6.5 29.4 %copy-start = (s32[6144]{0:T(1024)S(1)}, s32[6144]{0:T(1024)}, u32[]{:S(2)}) copy-start(s32[6144]{0:T(1024)} %param.23) | copy-start | bytes 73732
  6.5 115.1 %copy-start.5 = (f32[4096]{0:T(1024)S(1)}, f32[4096]{0:T(1024)}, u32[]{:S(2)}) copy-start(f32[4096]{0:T(1024)} %param.14) | copy-start | bytes 49156
  6.5 58.4 %all-gather.9.cloned.1.call-start = ((), (), s32[]{:S(2)}) async-start(), calls=%async_computation | async-start | bytes 3538944 | tf_op jit(solution)/shard_map/all_gather | solution.py:29
  17.4 104.2 %all-gather.11.cloned.1.call-start = ((), (), s32[]{:S(2)}) async-start(), calls=%async_computation.1 | async-start | bytes 8912896 | tf_op jit(solution)/shard_map/all_gather | solution.py:65
  17.4 15.8 %collective-permute-start = (bf16[256,256]{1,0:T(8,128)(2,1)}, bf16[256,256]{1,0:T(8,128)(2,1)S(1)}, u32[]{:S(2)}, u32[]{:S(2)}) collective-permute-start(bf16[256,256]{1,0:T(8,128)(2,1)} %param.16), channel_id=1, source_target_pairs={{0,0},{1,16},{2,32},{3,48},{4,64},{5,80},{6,96},{7,112},{8,128},{9... | collective-permute-start | bytes 393224 | tf_op jit(solution)/shard_map/ppermute | solution.py:55
  34.1 188.8 %all-gather.13.cloned.1.call-start = ((), (), s32[]{:S(2)}) async-start(), calls=%async_computation.2 | async-start | bytes 3538944 | tf_op jit(solution)/shard_map/all_gather | solution.py:29
  128.1 4.6 %collective-permute-start.2 = (bf16[127,256]{1,0:T(8,128)(2,1)S(1)}, bf16[127,256]{1,0:T(8,128)(2,1)S(1)}, u32[]{:S(2)}, u32[]{:S(2)}) collective-permute-start(bf16[127,256]{1,0:T(8,128)(2,1)S(1)} %get-tuple-element.309), channel_id=1, source_target_pairs={{16,0},{32,16},{48,32},{64,48},{80,64},{96,80},{112,96},{128,112},... | collective-permute-start | bytes 195080 | tf_op jit(solution)/shard_map/ppermute | solution.py:19
  130.7 5.6 %collective-permute-start.1 = (bf16[127,256]{1,0:T(8,128)(2,1)S(1)}, bf16[127,256]{1,0:T(8,128)(2,1)S(1)}, u32[]{:S(2)}, u32[]{:S(2)}) collective-permute-start(bf16[127,256]{1,0:T(8,128)(2,1)S(1)} %get-tuple-element.308), channel_id=1, source_target_pairs={{0,16},{16,32},{32,48},{48,64},{64,80},{80,96},{96,112},{112,128},... | collective-permute-start | bytes 195080 | tf_op jit(solution)/shard_map/ppermute | solution.py:18
  166.6 70.6 %copy-start.1 = (bf16[256,3,256]{2,0,1:T(8,128)(2,1)S(1)}, bf16[256,3,256]{2,0,1:T(8,128)(2,1)}, u32[]{:S(2)}) copy-start(bf16[256,3,256]{2,0,1:T(8,128)(2,1)} %param.19) | copy-start | bytes 1179652
  174.8 63.4 %copy-start.4 = (bf16[256,256]{1,0:T(8,128)(2,1)S(1)}, bf16[256,256]{1,0:T(8,128)(2,1)}, u32[]{:S(2)}) copy-start(bf16[256,256]{1,0:T(8,128)(2,1)} %param.20) | copy-start | bytes 393220
  174.8 83.0 %copy-start.3 = (f32[16,256]{1,0:T(8,128)S(1)}, f32[16,256]{1,0:T(8,128)}, u32[]{:S(2)}) copy-start(f32[16,256]{1,0:T(8,128)} %param.21) | copy-start | bytes 49156
  174.9 109.0 %all-gather.15.cloned.1.call-start = ((), (), s32[]{:S(2)}) async-start(), calls=%async_computation.3 | async-start | bytes 3538944 | tf_op jit(solution)/shard_map/all_gather | solution.py:29
  178.0 160.4 %copy-start.6 = (f32[4096]{0:T(1024)S(1)}, f32[4096]{0:T(1024)}, u32[]{:S(2)}) copy-start(f32[4096]{0:T(1024)} %param.18) | copy-start | bytes 49156
  237.1 101.3 %all-gather.17.cloned.1.call-start = ((), (), s32[]{:S(2)}) async-start(), calls=%async_computation.4 | async-start | bytes 6684672 | tf_op jit(solution)/shard_map/all_gather | solution.py:33
  238.1 148.1 %all-gather.21.cloned.1.call-start = ((), (), s32[]{:S(2)}) async-start(), calls=%async_computation.6 | async-start | bytes 2228224 | tf_op jit(solution)/shard_map/all_gather | solution.py:59
  238.2 16.6 %collective-permute-start.3 = (bf16[256,256]{1,0:T(8,128)(2,1)S(1)}, bf16[256,256]{1,0:T(8,128)(2,1)S(1)}, u32[]{:S(2)}, u32[]{:S(2)}) collective-permute-start(bf16[256,256]{1,0:T(8,128)(2,1)S(1)} %copy-done.4), channel_id=1, source_target_pairs={{0,0},{1,16},{2,32},{3,48},{4,64},{5,80},{6,96},{7,112},{8,128},{9... | collective-permute-start | bytes 393224 | tf_op jit(solution)/shard_map/ppermute | solution.py:55
  254.8 0.6 copy-start.2
  255.5 176.6 %all-gather.19.cloned.1.call-start = ((), (), s32[]{:S(2)}) async-start(), calls=%async_computation.5 | async-start | bytes 3538944 | tf_op jit(solution)/shard_map/all_gather | solution.py:29
Sparse Core Ops, SparseCore 0:
  17.5 47.3 all-gather.8
  66.7 54.8 all-gather.10
  175.0 47.9 all-gather.12
  237.2 46.5 all-gather.14
  285.5 52.8 all-gather.16
  340.1 37.8 all-gather.20
  386.3 45.6 all-gather.18
